TPU v7x, 1024 devices: a whole 4x8x16 slice. The times are simulated.
1024 devices in a mesh: gx: 16 (over y, core), gy: 64 (over z, x).
Axes of the slice: x: 4, y: 8, z: 16, core: 2. Of those that a mesh axis runs over, the one named last changes fastest.
Arguments:
- pressure_init: float32 [256, 2048, 128], P('gx', 'gy'), may hold values from -6 to 6
- source: float32 [256, 2048, 128], P('gx', 'gy'), may hold values from -6 to 6
- permeability: float32 [256, 2048, 128], P('gx', 'gy'), may hold values from 0.1 to 10
Outputs:
- pressure: float32 [256, 2048, 128], P('gx', 'gy')
- correction_mid: float32 [128, 1024, 128], P('gx', 'gy')
- correction_coarse: float32 [64, 512, 128], P('gx', 'gy')
All inputs are finite; a program needn't handle non-finite values.
Results may differ from a plain program's by a relative error of at most 0.0003.
Values sent between devices are 32-bit elements; how exact they have to be, the bound alone decides.
No kernel may reach another device: no remote copies, remote signals or barrier semaphores. Data moves between devices by JAX's collectives and lax.ppermute only.
A program may use at most 32 MiB of HBM per device.

v0:
```python
import jax
import jax.numpy as jnp
from jax import lax
from jax.sharding import PartitionSpec as P

SWEEPS = 2
COARSE = 4


STORE = 0.1
OMEGA = 0.8


def with_halo(x, sides, width):
    for axis, dim in sides:
        count, length = (lax.axis_size(axis), x.shape[dim])
        up = [(i, (i + 1) % count) for i in range(count - 1)]
        down = [(j, i) for i, j in up]
        last = lax.slice_in_dim(x, length - width, length, axis=dim)
        leading = lax.slice_in_dim(x, 0, width, axis=dim)
        before = lax.ppermute(last, axis, up)
        after = lax.ppermute(leading, axis, down)
        x = jnp.concatenate([before, x, after], axis=dim)
    return x


def harmonic(first, second):
    total = first + second
    return 2.0 * first * second / jnp.where(total > 0, total, 1.0)


def widths(axis, low):
    pads = [(0, 0), (0, 0), (0, 0)]
    pads[axis] = (1, 0) if low else (0, 1)
    return pads


def face_sum(coupling, axis):
    return jnp.pad(coupling, widths(axis, True)) + jnp.pad(coupling, widths(axis, False))


def net_flow(flow, axis):
    return jnp.pad(flow, widths(axis, False)) - jnp.pad(flow, widths(axis, True))


def coefficients(perm, scale):
    couple_x = scale * harmonic(perm[1:], perm[:-1])
    couple_y = scale * harmonic(perm[:, 1:], perm[:, :-1])
    couple_z = harmonic(perm[:, :, 1:], perm[:, :, :-1])
    diagonal = STORE + face_sum(couple_x, 0) + face_sum(couple_y, 1) + face_sum(couple_z, 2)
    return (couple_x, couple_y, couple_z, diagonal)


def apply_operator(value, parts):
    couple_x, couple_y, couple_z, diagonal = parts
    flow_x = couple_x * (value[:-1] - value[1:])
    flow_y = couple_y * (value[:, :-1] - value[:, 1:])
    flow_z = couple_z * (value[:, :, :-1] - value[:, :, 1:])
    return STORE * value + net_flow(flow_x, 0) + net_flow(flow_y, 1) + net_flow(flow_z, 2)


def restrict(field):
    sx, sy, sz = field.shape
    return 0.25 * jnp.sum(field.reshape(sx // 2, 2, sy // 2, 2, sz), axis=(1, 3))


def trim(field):
    return field[1:-1, 1:-1]


def grid_pad(stacked):
    return with_halo(stacked, (("gx", 1), ("gy", 2)), 1)


def pad_single(field, pad_fn):
    return pad_fn(field[None])[0]


def smooth_zero(rhs, perm_padded, scale, sweeps, pad_fn):
    parts = coefficients(perm_padded, scale)
    diagonal = trim(parts[3])
    value = OMEGA * rhs / diagonal
    for step in range(sweeps - 1):
        padded = pad_single(value, pad_fn)
        value = value + OMEGA * (rhs - trim(apply_operator(padded, parts))) / diagonal
    return (value, parts)


def body(pressure_init, source, permeability):
    region = grid_pad(jnp.stack([permeability, pressure_init]))
    parts0 = coefficients(region[0], 1.0)
    diagonal0 = trim(parts0[3])
    padded = region[1]
    pressure = pressure_init
    for step in range(SWEEPS):
        if step > 0:
            padded = pad_single(pressure, grid_pad)
        pressure = pressure + OMEGA * (source - trim(apply_operator(padded, parts0))) / diagonal0
    resid0 = source - trim(apply_operator(pad_single(pressure, grid_pad), parts0))
    rhs_mid = restrict(resid0)
    perm_mid = restrict(permeability)
    correction_mid, parts1 = smooth_zero(
        rhs_mid, pad_single(perm_mid, grid_pad), 0.25, SWEEPS, grid_pad
    )
    resid1 = rhs_mid - trim(apply_operator(pad_single(correction_mid, grid_pad), parts1))
    rhs_coarse = restrict(resid1)
    perm_coarse = restrict(perm_mid)
    correction_coarse, unused = smooth_zero(
        rhs_coarse, pad_single(perm_coarse, grid_pad), 0.0625, COARSE, grid_pad
    )
    return (pressure, correction_mid, correction_coarse)


def solution(mesh):
    placed = (P("gx", "gy", None), P("gx", "gy", None), P("gx", "gy", None))
    return jax.shard_map(
        body,
        mesh=mesh,
        in_specs=placed,
        out_specs=(P("gx", "gy", None), P("gx", "gy", None), P("gx", "gy", None)),
        check_vma=False,
    )
```

profile of v0, /device:TPU:223, one launch (start us, length us, event | category | flops | bytes accessed | tf_op | source)
XLA Modules:
  0.0 193.6 jit_solution(1409043302056227850)
XLA Ops:
  1.5 5.0 %collective-permute-start = (f32[2,1,32,128]{3,2,1,0:T(8,128)S(1)}, f32[2,1,32,128]{3,2,1,0:T(8,128)S(1)}, u32[]{:S(2)}, u32[]{:S(2)}) collective-permute-start(f32[2,1,32,128]{3,2,1,0:T(8,128)S(1)} %get-tuple-element.19), channel_id=1, source_target_pairs={{0,64},{64,128},{128,192},{192,256},{256,320},{320,384},{384,448},... | collective-permute-start | bytes 98312 | tf_op jit(solution)/shard_map/ppermute | solution.py:21
  6.4 1.9 collective-permute-start.1
  8.7 4.9 %collective-permute-start.24 = (f32[1,1,8,128]{3,2,1,0:T(8,128)S(1)}, f32[1,1,8,128]{3,2,1,0:T(8,128)S(1)}, u32[]{:S(2)}, u32[]{:S(2)}) collective-permute-start(f32[1,1,8,128]{3,2,1,0:T(8,128)S(1)} %get-tuple-element.75), channel_id=1, source_target_pairs={{0,64},{64,128},{128,192},{192,256},{256,320},{320,384},{384,448},... | collective-permute-start | bytes 12296 | tf_op jit(solution)/shard_map/ppermute | solution.py:21
  13.5 1.9 collective-permute-start.25
  15.5 4.9 %collective-permute-start.12 = (f32[1,1,16,128]{3,2,1,0:T(8,128)S(1)}, f32[1,1,16,128]{3,2,1,0:T(8,128)S(1)}, u32[]{:S(2)}, u32[]{:S(2)}) collective-permute-start(f32[1,1,16,128]{3,2,1,0:T(8,128)S(1)} %get-tuple-element.51), channel_id=1, source_target_pairs={{0,64},{64,128},{128,192},{192,256},{256,320},{320,384},{384,448},... | collective-permute-start | bytes 24584 | tf_op jit(solution)/shard_map/ppermute | solution.py:21
  20.3 1.9 collective-permute-start.13
  22.3 5.1 %collective-permute-start.26 = (f32[1,6,1,128]{3,2,1,0:T(1,128)S(1)}, f32[1,6,1,128]{3,2,1,0:T(1,128)S(1)}, u32[]{:S(2)}, u32[]{:S(2)}) collective-permute-start(f32[1,6,1,128]{3,2,1,0:T(1,128)S(1)} %get-tuple-element.67), channel_id=1, source_target_pairs={{0,1},{1,2},{2,3},{3,4},{4,5},{5,6},{6,7},{7,8},{8,9},{9,10},{10,1... | collective-permute-start | bytes 9224 | tf_op jit(solution)/shard_map/ppermute | solution.py:21
  27.4 1.9 collective-permute-start.27
  29.4 6.7 %collective-permute-start.2 = (f32[2,18,1,128]{3,2,1,0:T(1,128)S(1)}, f32[2,18,1,128]{3,2,1,0:T(1,128)S(1)}, u32[]{:S(2)}, u32[]{:S(2)}) collective-permute-start(f32[2,18,1,128]{3,2,1,0:T(1,128)S(1)} %get-tuple-element.17), channel_id=1, source_target_pairs={{0,1},{1,2},{2,3},{3,4},{4,5},{5,6},{6,7},{7,8},{8,9},{9,10},{10,1... | collective-permute-start | bytes 55304 | tf_op jit(solution)/shard_map/ppermute | solution.py:21
  36.1 1.9 collective-permute-start.3
  38.1 6.7 %collective-permute-start.14 = (f32[1,10,1,128]{3,2,1,0:T(1,128)S(1)}, f32[1,10,1,128]{3,2,1,0:T(1,128)S(1)}, u32[]{:S(2)}, u32[]{:S(2)}) collective-permute-start(f32[1,10,1,128]{3,2,1,0:T(1,128)S(1)} %get-tuple-element.43), channel_id=1, source_target_pairs={{0,1},{1,2},{2,3},{3,4},{4,5},{5,6},{6,7},{7,8},{8,9},{9,10},{10,1... | collective-permute-start | bytes 15368 | tf_op jit(solution)/shard_map/ppermute | solution.py:21
  44.8 1.9 collective-permute-start.15
  48.8 6.3 %collective-permute-start.4 = (f32[1,1,32,128]{3,2,1,0:T(8,128)S(1)}, f32[1,1,32,128]{3,2,1,0:T(8,128)S(1)}, u32[]{:S(2)}, u32[]{:S(2)}) collective-permute-start(f32[1,1,32,128]{3,2,1,0:T(8,128)S(1)} %get-tuple-element.31), channel_id=1, source_target_pairs={{0,64},{64,128},{128,192},{192,256},{256,320},{320,384},{384,448},... | collective-permute-start | bytes 49160 | tf_op jit(solution)/shard_map/ppermute | solution.py:21
  55.1 1.9 collective-permute-start.5
  57.0 4.3 %collective-permute-done.5 = f32[1,1,32,128]{3,2,1,0:T(8,128)S(1)} collective-permute-done((f32[1,1,32,128]{3,2,1,0:T(8,128)S(1)}, f32[1,1,32,128]{3,2,1,0:T(8,128)S(1)}, u32[]{:S(2)}, u32[]{:S(2)}) %collective-permute-start.5) | collective-permute-done | bytes 16416 | tf_op jit(solution)/shard_map/ppermute | solution.py:22
  61.4 7.0 %collective-permute-start.6 = (f32[1,18,1,128]{3,2,1,0:T(1,128)S(1)}, f32[1,18,1,128]{3,2,1,0:T(1,128)S(1)}, u32[]{:S(2)}, u32[]{:S(2)}) collective-permute-start(f32[1,18,1,128]{3,2,1,0:T(1,128)S(1)} %get-tuple-element.27), channel_id=1, source_target_pairs={{0,1},{1,2},{2,3},{3,4},{4,5},{5,6},{6,7},{7,8},{8,9},{9,10},{10,1... | collective-permute-start | bytes 27656 | tf_op jit(solution)/shard_map/ppermute | solution.py:21
  68.3 1.9 collective-permute-start.7
  70.3 5.7 %collective-permute-done.7 = f32[1,18,1,128]{3,2,1,0:T(1,128)S(1)} collective-permute-done((f32[1,18,1,128]{3,2,1,0:T(1,128)S(1)}, f32[1,18,1,128]{3,2,1,0:T(1,128)S(1)}, u32[]{:S(2)}, u32[]{:S(2)}) %collective-permute-start.7) | collective-permute-done | bytes 9248 | tf_op jit(solution)/shard_map/ppermute | solution.py:22
  76.7 3.4 %collective-permute-start.8 = (f32[1,1,32,128]{3,2,1,0:T(8,128)S(1)}, f32[1,1,32,128]{3,2,1,0:T(8,128)S(1)}, u32[]{:S(2)}, u32[]{:S(2)}) collective-permute-start(f32[1,1,32,128]{3,2,1,0:T(8,128)S(1)} %get-tuple-element.29), channel_id=1, source_target_pairs={{0,64},{64,128},{128,192},{192,256},{256,320},{320,384},{384,448},... | collective-permute-start | bytes 49160 | tf_op jit(solution)/shard_map/ppermute | solution.py:21
  80.1 1.9 collective-permute-start.9
  82.1 4.2 %collective-permute-done.9 = f32[1,1,32,128]{3,2,1,0:T(8,128)S(1)} collective-permute-done((f32[1,1,32,128]{3,2,1,0:T(8,128)S(1)}, f32[1,1,32,128]{3,2,1,0:T(8,128)S(1)}, u32[]{:S(2)}, u32[]{:S(2)}) %collective-permute-start.9) | collective-permute-done | bytes 16416 | tf_op jit(solution)/shard_map/ppermute | solution.py:22
  86.4 1.9 collective-permute-start.10
  88.3 3.4 %collective-permute-start.11 = (f32[1,18,1,128]{3,2,1,0:T(1,128)S(1)}, f32[1,18,1,128]{3,2,1,0:T(1,128)S(1)}, u32[]{:S(2)}, u32[]{:S(2)}) collective-permute-start(f32[1,18,1,128]{3,2,1,0:T(1,128)S(1)} %get-tuple-element.26), channel_id=1, source_target_pairs={{1,0},{2,1},{3,2},{4,3},{5,4},{6,5},{7,6},{8,7},{9,8},{10,9},{11,1... | collective-permute-start | bytes 27656 | tf_op jit(solution)/shard_map/ppermute | solution.py:22
  91.7 4.3 %collective-permute-done.11 = f32[1,18,1,128]{3,2,1,0:T(1,128)S(1)} collective-permute-done((f32[1,18,1,128]{3,2,1,0:T(1,128)S(1)}, f32[1,18,1,128]{3,2,1,0:T(1,128)S(1)}, u32[]{:S(2)}, u32[]{:S(2)}) %collective-permute-start.11) | collective-permute-done | bytes 9248 | tf_op jit(solution)/shard_map/ppermute | solution.py:22
  96.9 3.1 %collective-permute-start.16 = (f32[1,1,16,128]{3,2,1,0:T(8,128)S(1)}, f32[1,1,16,128]{3,2,1,0:T(8,128)S(1)}, u32[]{:S(2)}, u32[]{:S(2)}) collective-permute-start(f32[1,1,16,128]{3,2,1,0:T(8,128)S(1)} %get-tuple-element.49), channel_id=1, source_target_pairs={{0,64},{64,128},{128,192},{192,256},{256,320},{320,384},{384,448},... | collective-permute-start | bytes 24584 | tf_op jit(solution)/shard_map/ppermute | solution.py:21
  100.0 1.9 collective-permute-start.17
  102.0 4.2 %collective-permute-done.17 = f32[1,1,16,128]{3,2,1,0:T(8,128)S(1)} collective-permute-done((f32[1,1,16,128]{3,2,1,0:T(8,128)S(1)}, f32[1,1,16,128]{3,2,1,0:T(8,128)S(1)}, u32[]{:S(2)}, u32[]{:S(2)}) %collective-permute-start.17) | collective-permute-done | bytes 8224 | tf_op jit(solution)/shard_map/ppermute | solution.py:22
  106.2 1.9 collective-permute-start.18
  108.1 3.4 %collective-permute-start.19 = (f32[1,10,1,128]{3,2,1,0:T(1,128)S(1)}, f32[1,10,1,128]{3,2,1,0:T(1,128)S(1)}, u32[]{:S(2)}, u32[]{:S(2)}) collective-permute-start(f32[1,10,1,128]{3,2,1,0:T(1,128)S(1)} %get-tuple-element.42), channel_id=1, source_target_pairs={{1,0},{2,1},{3,2},{4,3},{5,4},{6,5},{7,6},{8,7},{9,8},{10,9},{11,1... | collective-permute-start | bytes 15368 | tf_op jit(solution)/shard_map/ppermute | solution.py:22
  111.5 4.3 %collective-permute-done.19 = f32[1,10,1,128]{3,2,1,0:T(1,128)S(1)} collective-permute-done((f32[1,10,1,128]{3,2,1,0:T(1,128)S(1)}, f32[1,10,1,128]{3,2,1,0:T(1,128)S(1)}, u32[]{:S(2)}, u32[]{:S(2)}) %collective-permute-start.19) | collective-permute-done | bytes 5152 | tf_op jit(solution)/shard_map/ppermute | solution.py:22
  116.2 3.1 %collective-permute-start.20 = (f32[1,1,16,128]{3,2,1,0:T(8,128)S(1)}, f32[1,1,16,128]{3,2,1,0:T(8,128)S(1)}, u32[]{:S(2)}, u32[]{:S(2)}) collective-permute-start(f32[1,1,16,128]{3,2,1,0:T(8,128)S(1)} %get-tuple-element.47), channel_id=1, source_target_pairs={{0,64},{64,128},{128,192},{192,256},{256,320},{320,384},{384,448},... | collective-permute-start | bytes 24584 | tf_op jit(solution)/shard_map/ppermute | solution.py:21
  121.4 4.1 %collective-permute-done.21 = f32[1,1,16,128]{3,2,1,0:T(8,128)S(1)} collective-permute-done((f32[1,1,16,128]{3,2,1,0:T(8,128)S(1)}, f32[1,1,16,128]{3,2,1,0:T(8,128)S(1)}, u32[]{:S(2)}, u32[]{:S(2)}) %collective-permute-start.21) | collective-permute-done | bytes 8224 | tf_op jit(solution)/shard_map/ppermute | solution.py:22
  125.5 1.9 collective-permute-start.22
  127.4 3.4 %collective-permute-start.23 = (f32[1,10,1,128]{3,2,1,0:T(1,128)S(1)}, f32[1,10,1,128]{3,2,1,0:T(1,128)S(1)}, u32[]{:S(2)}, u32[]{:S(2)}) collective-permute-start(f32[1,10,1,128]{3,2,1,0:T(1,128)S(1)} %get-tuple-element.40), channel_id=1, source_target_pairs={{1,0},{2,1},{3,2},{4,3},{5,4},{6,5},{7,6},{8,7},{9,8},{10,9},{11,1... | collective-permute-start | bytes 15368 | tf_op jit(solution)/shard_map/ppermute | solution.py:22
  130.9 4.3 %collective-permute-done.23 = f32[1,10,1,128]{3,2,1,0:T(1,128)S(1)} collective-permute-done((f32[1,10,1,128]{3,2,1,0:T(1,128)S(1)}, f32[1,10,1,128]{3,2,1,0:T(1,128)S(1)}, u32[]{:S(2)}, u32[]{:S(2)}) %collective-permute-start.23) | collective-permute-done | bytes 5152 | tf_op jit(solution)/shard_map/ppermute | solution.py:22
  135.7 3.1 %collective-permute-start.28 = (f32[1,1,8,128]{3,2,1,0:T(8,128)S(1)}, f32[1,1,8,128]{3,2,1,0:T(8,128)S(1)}, u32[]{:S(2)}, u32[]{:S(2)}) collective-permute-start(f32[1,1,8,128]{3,2,1,0:T(8,128)S(1)} %get-tuple-element.73), channel_id=1, source_target_pairs={{0,64},{64,128},{128,192},{192,256},{256,320},{320,384},{384,448},... | collective-permute-start | bytes 12296 | tf_op jit(solution)/shard_map/ppermute | solution.py:21
  140.7 4.2 %collective-permute-done.29 = f32[1,1,8,128]{3,2,1,0:T(8,128)S(1)} collective-permute-done((f32[1,1,8,128]{3,2,1,0:T(8,128)S(1)}, f32[1,1,8,128]{3,2,1,0:T(8,128)S(1)}, u32[]{:S(2)}, u32[]{:S(2)}) %collective-permute-start.29) | collective-permute-done | bytes 4128 | tf_op jit(solution)/shard_map/ppermute | solution.py:22
  146.8 3.4 %collective-permute-start.31 = (f32[1,6,1,128]{3,2,1,0:T(1,128)S(1)}, f32[1,6,1,128]{3,2,1,0:T(1,128)S(1)}, u32[]{:S(2)}, u32[]{:S(2)}) collective-permute-start(f32[1,6,1,128]{3,2,1,0:T(1,128)S(1)} %get-tuple-element.66), channel_id=1, source_target_pairs={{1,0},{2,1},{3,2},{4,3},{5,4},{6,5},{7,6},{8,7},{9,8},{10,9},{11,1... | collective-permute-start | bytes 9224 | tf_op jit(solution)/shard_map/ppermute | solution.py:22
  150.2 4.3 %collective-permute-done.31 = f32[1,6,1,128]{3,2,1,0:T(1,128)S(1)} collective-permute-done((f32[1,6,1,128]{3,2,1,0:T(1,128)S(1)}, f32[1,6,1,128]{3,2,1,0:T(1,128)S(1)}, u32[]{:S(2)}, u32[]{:S(2)}) %collective-permute-start.31) | collective-permute-done | bytes 3104 | tf_op jit(solution)/shard_map/ppermute | solution.py:22
  154.8 3.1 %collective-permute-start.32 = (f32[1,1,8,128]{3,2,1,0:T(8,128)S(1)}, f32[1,1,8,128]{3,2,1,0:T(8,128)S(1)}, u32[]{:S(2)}, u32[]{:S(2)}) collective-permute-start(f32[1,1,8,128]{3,2,1,0:T(8,128)S(1)} %get-tuple-element.71), channel_id=1, source_target_pairs={{0,64},{64,128},{128,192},{192,256},{256,320},{320,384},{384,448},... | collective-permute-start | bytes 12296 | tf_op jit(solution)/shard_map/ppermute | solution.py:21
  159.8 4.2 %collective-permute-done.33 = f32[1,1,8,128]{3,2,1,0:T(8,128)S(1)} collective-permute-done((f32[1,1,8,128]{3,2,1,0:T(8,128)S(1)}, f32[1,1,8,128]{3,2,1,0:T(8,128)S(1)}, u32[]{:S(2)}, u32[]{:S(2)}) %collective-permute-start.33) | collective-permute-done | bytes 4128 | tf_op jit(solution)/shard_map/ppermute | solution.py:22
  165.9 3.4 %collective-permute-start.35 = (f32[1,6,1,128]{3,2,1,0:T(1,128)S(1)}, f32[1,6,1,128]{3,2,1,0:T(1,128)S(1)}, u32[]{:S(2)}, u32[]{:S(2)}) collective-permute-start(f32[1,6,1,128]{3,2,1,0:T(1,128)S(1)} %get-tuple-element.64), channel_id=1, source_target_pairs={{1,0},{2,1},{3,2},{4,3},{5,4},{6,5},{7,6},{8,7},{9,8},{10,9},{11,1... | collective-permute-start | bytes 9224 | tf_op jit(solution)/shard_map/ppermute | solution.py:22
  169.3 4.3 %collective-permute-done.35 = f32[1,6,1,128]{3,2,1,0:T(1,128)S(1)} collective-permute-done((f32[1,6,1,128]{3,2,1,0:T(1,128)S(1)}, f32[1,6,1,128]{3,2,1,0:T(1,128)S(1)}, u32[]{:S(2)}, u32[]{:S(2)}) %collective-permute-start.35) | collective-permute-done | bytes 3104 | tf_op jit(solution)/shard_map/ppermute | solution.py:22
  173.9 3.1 %collective-permute-start.36 = (f32[1,1,8,128]{3,2,1,0:T(8,128)S(1)}, f32[1,1,8,128]{3,2,1,0:T(8,128)S(1)}, u32[]{:S(2)}, u32[]{:S(2)}) collective-permute-start(f32[1,1,8,128]{3,2,1,0:T(8,128)S(1)} %get-tuple-element.69), channel_id=1, source_target_pairs={{0,64},{64,128},{128,192},{192,256},{256,320},{320,384},{384,448},... | collective-permute-start | bytes 12296 | tf_op jit(solution)/shard_map/ppermute | solution.py:21
  177.0 1.9 collective-permute-start.37
  178.9 4.2 %collective-permute-done.37 = f32[1,1,8,128]{3,2,1,0:T(8,128)S(1)} collective-permute-done((f32[1,1,8,128]{3,2,1,0:T(8,128)S(1)}, f32[1,1,8,128]{3,2,1,0:T(8,128)S(1)}, u32[]{:S(2)}, u32[]{:S(2)}) %collective-permute-start.37) | collective-permute-done | bytes 4128 | tf_op jit(solution)/shard_map/ppermute | solution.py:22
  185.0 3.4 %collective-permute-start.39 = (f32[1,6,1,128]{3,2,1,0:T(1,128)S(1)}, f32[1,6,1,128]{3,2,1,0:T(1,128)S(1)}, u32[]{:S(2)}, u32[]{:S(2)}) collective-permute-start(f32[1,6,1,128]{3,2,1,0:T(1,128)S(1)} %get-tuple-element.62), channel_id=1, source_target_pairs={{1,0},{2,1},{3,2},{4,3},{5,4},{6,5},{7,6},{8,7},{9,8},{10,9},{11,1... | collective-permute-start | bytes 9224 | tf_op jit(solution)/shard_map/ppermute | solution.py:22
  188.4 4.3 %collective-permute-done.39 = f32[1,6,1,128]{3,2,1,0:T(1,128)S(1)} collective-permute-done((f32[1,6,1,128]{3,2,1,0:T(1,128)S(1)}, f32[1,6,1,128]{3,2,1,0:T(1,128)S(1)}, u32[]{:S(2)}, u32[]{:S(2)}) %collective-permute-start.39) | collective-permute-done | bytes 3104 | tf_op jit(solution)/shard_map/ppermute | solution.py:22
  (119 shorter events, 18.8 us)
Async XLA Ops:
  0.6 7.7 %copy-start = (f32[16,32,128]{2,1,0:T(8,128)S(1)}, f32[16,32,128]{2,1,0:T(8,128)}, u32[]{:S(2)}) copy-start(f32[16,32,128]{2,1,0:T(8,128)} %param.5) | copy-start | bytes 786436
  1.5 26.0 %collective-permute-start = (f32[2,1,32,128]{3,2,1,0:T(8,128)S(1)}, f32[2,1,32,128]{3,2,1,0:T(8,128)S(1)}, u32[]{:S(2)}, u32[]{:S(2)}) collective-permute-start(f32[2,1,32,128]{3,2,1,0:T(8,128)S(1)} %get-tuple-element.19), channel_id=1, source_target_pairs={{0,64},{64,128},{128,192},{192,256},{256,320},{320,384},{384,448},... | collective-permute-start | bytes 98312 | tf_op jit(solution)/shard_map/ppermute | solution.py:21
  6.4 22.9 %collective-permute-start.1 = (f32[2,1,32,128]{3,2,1,0:T(8,128)S(1)}, f32[2,1,32,128]{3,2,1,0:T(8,128)S(1)}, u32[]{:S(2)}, u32[]{:S(2)}) collective-permute-start(f32[2,1,32,128]{3,2,1,0:T(8,128)S(1)} %get-tuple-element.20), channel_id=1, source_target_pairs={{64,0},{128,64},{192,128},{256,192},{320,256},{384,320},{448,384},... | collective-permute-start | bytes 98312 | tf_op jit(solution)/shard_map/ppermute | solution.py:22
  8.6 20.8 %copy-start.1 = (f32[16,32,128]{2,1,0:T(8,128)S(1)}, f32[16,32,128]{2,1,0:T(8,128)}, u32[]{:S(2)}) copy-start(f32[16,32,128]{2,1,0:T(8,128)} %param.3) | copy-start | bytes 786436
  8.7 11.7 %collective-permute-start.24 = (f32[1,1,8,128]{3,2,1,0:T(8,128)S(1)}, f32[1,1,8,128]{3,2,1,0:T(8,128)S(1)}, u32[]{:S(2)}, u32[]{:S(2)}) collective-permute-start(f32[1,1,8,128]{3,2,1,0:T(8,128)S(1)} %get-tuple-element.75), channel_id=1, source_target_pairs={{0,64},{64,128},{128,192},{192,256},{256,320},{320,384},{384,448},... | collective-permute-start | bytes 12296 | tf_op jit(solution)/shard_map/ppermute | solution.py:21
  13.5 8.7 %collective-permute-start.25 = (f32[1,1,8,128]{3,2,1,0:T(8,128)S(1)}, f32[1,1,8,128]{3,2,1,0:T(8,128)S(1)}, u32[]{:S(2)}, u32[]{:S(2)}) collective-permute-start(f32[1,1,8,128]{3,2,1,0:T(8,128)S(1)} %get-tuple-element.76), channel_id=1, source_target_pairs={{64,0},{128,64},{192,128},{256,192},{320,256},{384,320},{448,384},... | collective-permute-start | bytes 12296 | tf_op jit(solution)/shard_map/ppermute | solution.py:22
  15.5 20.6 %collective-permute-start.12 = (f32[1,1,16,128]{3,2,1,0:T(8,128)S(1)}, f32[1,1,16,128]{3,2,1,0:T(8,128)S(1)}, u32[]{:S(2)}, u32[]{:S(2)}) collective-permute-start(f32[1,1,16,128]{3,2,1,0:T(8,128)S(1)} %get-tuple-element.51), channel_id=1, source_target_pairs={{0,64},{64,128},{128,192},{192,256},{256,320},{320,384},{384,448},... | collective-permute-start | bytes 24584 | tf_op jit(solution)/shard_map/ppermute | solution.py:21
  20.3 17.7 %collective-permute-start.13 = (f32[1,1,16,128]{3,2,1,0:T(8,128)S(1)}, f32[1,1,16,128]{3,2,1,0:T(8,128)S(1)}, u32[]{:S(2)}, u32[]{:S(2)}) collective-permute-start(f32[1,1,16,128]{3,2,1,0:T(8,128)S(1)} %get-tuple-element.52), channel_id=1, source_target_pairs={{64,0},{128,64},{192,128},{256,192},{320,256},{384,320},{448,384},... | collective-permute-start | bytes 24584 | tf_op jit(solution)/shard_map/ppermute | solution.py:22
  22.3 79.6 %collective-permute-start.26 = (f32[1,6,1,128]{3,2,1,0:T(1,128)S(1)}, f32[1,6,1,128]{3,2,1,0:T(1,128)S(1)}, u32[]{:S(2)}, u32[]{:S(2)}) collective-permute-start(f32[1,6,1,128]{3,2,1,0:T(1,128)S(1)} %get-tuple-element.67), channel_id=1, source_target_pairs={{0,1},{1,2},{2,3},{3,4},{4,5},{5,6},{6,7},{7,8},{8,9},{9,10},{10,1... | collective-permute-start | bytes 9224 | tf_op jit(solution)/shard_map/ppermute | solution.py:21
  27.4 74.5 %collective-permute-start.27 = (f32[1,6,1,128]{3,2,1,0:T(1,128)S(1)}, f32[1,6,1,128]{3,2,1,0:T(1,128)S(1)}, u32[]{:S(2)}, u32[]{:S(2)}) collective-permute-start(f32[1,6,1,128]{3,2,1,0:T(1,128)S(1)} %get-tuple-element.68), channel_id=1, source_target_pairs={{1,0},{2,1},{3,2},{4,3},{5,4},{6,5},{7,6},{8,7},{9,8},{10,9},{11,1... | collective-permute-start | bytes 9224 | tf_op jit(solution)/shard_map/ppermute | solution.py:22
  29.4 15.4 %collective-permute-start.2 = (f32[2,18,1,128]{3,2,1,0:T(1,128)S(1)}, f32[2,18,1,128]{3,2,1,0:T(1,128)S(1)}, u32[]{:S(2)}, u32[]{:S(2)}) collective-permute-start(f32[2,18,1,128]{3,2,1,0:T(1,128)S(1)} %get-tuple-element.17), channel_id=1, source_target_pairs={{0,1},{1,2},{2,3},{3,4},{4,5},{5,6},{6,7},{7,8},{8,9},{9,10},{10,1... | collective-permute-start | bytes 55304 | tf_op jit(solution)/shard_map/ppermute | solution.py:21
  36.1 10.6 %collective-permute-start.3 = (f32[2,18,1,128]{3,2,1,0:T(1,128)S(1)}, f32[2,18,1,128]{3,2,1,0:T(1,128)S(1)}, u32[]{:S(2)}, u32[]{:S(2)}) collective-permute-start(f32[2,18,1,128]{3,2,1,0:T(1,128)S(1)} %get-tuple-element.18), channel_id=1, source_target_pairs={{1,0},{2,1},{3,2},{4,3},{5,4},{6,5},{7,6},{8,7},{9,8},{10,9},{11,1... | collective-permute-start | bytes 55304 | tf_op jit(solution)/shard_map/ppermute | solution.py:22
  38.1 17.0 %collective-permute-start.14 = (f32[1,10,1,128]{3,2,1,0:T(1,128)S(1)}, f32[1,10,1,128]{3,2,1,0:T(1,128)S(1)}, u32[]{:S(2)}, u32[]{:S(2)}) collective-permute-start(f32[1,10,1,128]{3,2,1,0:T(1,128)S(1)} %get-tuple-element.43), channel_id=1, source_target_pairs={{0,1},{1,2},{2,3},{3,4},{4,5},{5,6},{6,7},{7,8},{8,9},{9,10},{10,1... | collective-permute-start | bytes 15368 | tf_op jit(solution)/shard_map/ppermute | solution.py:21
  44.8 12.2 %collective-permute-start.15 = (f32[1,10,1,128]{3,2,1,0:T(1,128)S(1)}, f32[1,10,1,128]{3,2,1,0:T(1,128)S(1)}, u32[]{:S(2)}, u32[]{:S(2)}) collective-permute-start(f32[1,10,1,128]{3,2,1,0:T(1,128)S(1)} %get-tuple-element.44), channel_id=1, source_target_pairs={{1,0},{2,1},{3,2},{4,3},{5,4},{6,5},{7,6},{8,7},{9,8},{10,9},{11,1... | collective-permute-start | bytes 15368 | tf_op jit(solution)/shard_map/ppermute | solution.py:22
  47.3 1.0 copy-start.3
  48.8 8.2 %collective-permute-start.4 = (f32[1,1,32,128]{3,2,1,0:T(8,128)S(1)}, f32[1,1,32,128]{3,2,1,0:T(8,128)S(1)}, u32[]{:S(2)}, u32[]{:S(2)}) collective-permute-start(f32[1,1,32,128]{3,2,1,0:T(8,128)S(1)} %get-tuple-element.31), channel_id=1, source_target_pairs={{0,64},{64,128},{128,192},{192,256},{256,320},{320,384},{384,448},... | collective-permute-start | bytes 49160 | tf_op jit(solution)/shard_map/ppermute | solution.py:21
  55.1 6.3 %collective-permute-start.5 = (f32[1,1,32,128]{3,2,1,0:T(8,128)S(1)}, f32[1,1,32,128]{3,2,1,0:T(8,128)S(1)}, u32[]{:S(2)}, u32[]{:S(2)}) collective-permute-start(f32[1,1,32,128]{3,2,1,0:T(8,128)S(1)} %get-tuple-element.32), channel_id=1, source_target_pairs={{64,0},{128,64},{192,128},{256,192},{320,256},{384,320},{448,384},... | collective-permute-start | bytes 49160 | tf_op jit(solution)/shard_map/ppermute | solution.py:22
  61.4 9.0 %collective-permute-start.6 = (f32[1,18,1,128]{3,2,1,0:T(1,128)S(1)}, f32[1,18,1,128]{3,2,1,0:T(1,128)S(1)}, u32[]{:S(2)}, u32[]{:S(2)}) collective-permute-start(f32[1,18,1,128]{3,2,1,0:T(1,128)S(1)} %get-tuple-element.27), channel_id=1, source_target_pairs={{0,1},{1,2},{2,3},{3,4},{4,5},{5,6},{6,7},{7,8},{8,9},{9,10},{10,1... | collective-permute-start | bytes 27656 | tf_op jit(solution)/shard_map/ppermute | solution.py:21
  68.3 7.7 %collective-permute-start.7 = (f32[1,18,1,128]{3,2,1,0:T(1,128)S(1)}, f32[1,18,1,128]{3,2,1,0:T(1,128)S(1)}, u32[]{:S(2)}, u32[]{:S(2)}) collective-permute-start(f32[1,18,1,128]{3,2,1,0:T(1,128)S(1)} %get-tuple-element.28), channel_id=1, source_target_pairs={{1,0},{2,1},{3,2},{4,3},{5,4},{6,5},{7,6},{8,7},{9,8},{10,9},{11,1... | collective-permute-start | bytes 27656 | tf_op jit(solution)/shard_map/ppermute | solution.py:22
  76.7 19.3 %copy-start.2 = (f32[16,32,128]{2,1,0:T(8,128)}, f32[16,32,128]{2,1,0:T(8,128)S(1)}, u32[]{:S(2)}) copy-start(f32[16,32,128]{2,1,0:T(8,128)S(1)} %fusion.23) | copy-start | bytes 786436
  76.7 5.4 %collective-permute-start.8 = (f32[1,1,32,128]{3,2,1,0:T(8,128)S(1)}, f32[1,1,32,128]{3,2,1,0:T(8,128)S(1)}, u32[]{:S(2)}, u32[]{:S(2)}) collective-permute-start(f32[1,1,32,128]{3,2,1,0:T(8,128)S(1)} %get-tuple-element.29), channel_id=1, source_target_pairs={{0,64},{64,128},{128,192},{192,256},{256,320},{320,384},{384,448},... | collective-permute-start | bytes 49160 | tf_op jit(solution)/shard_map/ppermute | solution.py:21
  80.1 6.3 %collective-permute-start.9 = (f32[1,1,32,128]{3,2,1,0:T(8,128)S(1)}, f32[1,1,32,128]{3,2,1,0:T(8,128)S(1)}, u32[]{:S(2)}, u32[]{:S(2)}) collective-permute-start(f32[1,1,32,128]{3,2,1,0:T(8,128)S(1)} %get-tuple-element.30), channel_id=1, source_target_pairs={{64,0},{128,64},{192,128},{256,192},{320,256},{384,320},{448,384},... | collective-permute-start | bytes 49160 | tf_op jit(solution)/shard_map/ppermute | solution.py:22
  86.4 5.3 %collective-permute-start.10 = (f32[1,18,1,128]{3,2,1,0:T(1,128)S(1)}, f32[1,18,1,128]{3,2,1,0:T(1,128)S(1)}, u32[]{:S(2)}, u32[]{:S(2)}) collective-permute-start(f32[1,18,1,128]{3,2,1,0:T(1,128)S(1)} %get-tuple-element.25), channel_id=1, source_target_pairs={{0,1},{1,2},{2,3},{3,4},{4,5},{5,6},{6,7},{7,8},{8,9},{9,10},{10,1... | collective-permute-start | bytes 27656 | tf_op jit(solution)/shard_map/ppermute | solution.py:21
  88.3 7.7 %collective-permute-start.11 = (f32[1,18,1,128]{3,2,1,0:T(1,128)S(1)}, f32[1,18,1,128]{3,2,1,0:T(1,128)S(1)}, u32[]{:S(2)}, u32[]{:S(2)}) collective-permute-start(f32[1,18,1,128]{3,2,1,0:T(1,128)S(1)} %get-tuple-element.26), channel_id=1, source_target_pairs={{1,0},{2,1},{3,2},{4,3},{5,4},{6,5},{7,6},{8,7},{9,8},{10,9},{11,1... | collective-permute-start | bytes 27656 | tf_op jit(solution)/shard_map/ppermute | solution.py:22
  96.9 5.1 %collective-permute-start.16 = (f32[1,1,16,128]{3,2,1,0:T(8,128)S(1)}, f32[1,1,16,128]{3,2,1,0:T(8,128)S(1)}, u32[]{:S(2)}, u32[]{:S(2)}) collective-permute-start(f32[1,1,16,128]{3,2,1,0:T(8,128)S(1)} %get-tuple-element.49), channel_id=1, source_target_pairs={{0,64},{64,128},{128,192},{192,256},{256,320},{320,384},{384,448},... | collective-permute-start | bytes 24584 | tf_op jit(solution)/shard_map/ppermute | solution.py:21
  100.0 6.2 %collective-permute-start.17 = (f32[1,1,16,128]{3,2,1,0:T(8,128)S(1)}, f32[1,1,16,128]{3,2,1,0:T(8,128)S(1)}, u32[]{:S(2)}, u32[]{:S(2)}) collective-permute-start(f32[1,1,16,128]{3,2,1,0:T(8,128)S(1)} %get-tuple-element.50), channel_id=1, source_target_pairs={{64,0},{128,64},{192,128},{256,192},{320,256},{384,320},{448,384},... | collective-permute-start | bytes 24584 | tf_op jit(solution)/shard_map/ppermute | solution.py:22
  106.2 5.3 %collective-permute-start.18 = (f32[1,10,1,128]{3,2,1,0:T(1,128)S(1)}, f32[1,10,1,128]{3,2,1,0:T(1,128)S(1)}, u32[]{:S(2)}, u32[]{:S(2)}) collective-permute-start(f32[1,10,1,128]{3,2,1,0:T(1,128)S(1)} %get-tuple-element.41), channel_id=1, source_target_pairs={{0,1},{1,2},{2,3},{3,4},{4,5},{5,6},{6,7},{7,8},{8,9},{9,10},{10,1... | collective-permute-start | bytes 15368 | tf_op jit(solution)/shard_map/ppermute | solution.py:21
  108.1 7.7 %collective-permute-start.19 = (f32[1,10,1,128]{3,2,1,0:T(1,128)S(1)}, f32[1,10,1,128]{3,2,1,0:T(1,128)S(1)}, u32[]{:S(2)}, u32[]{:S(2)}) collective-permute-start(f32[1,10,1,128]{3,2,1,0:T(1,128)S(1)} %get-tuple-element.42), channel_id=1, source_target_pairs={{1,0},{2,1},{3,2},{4,3},{5,4},{6,5},{7,6},{8,7},{9,8},{10,9},{11,1... | collective-permute-start | bytes 15368 | tf_op jit(solution)/shard_map/ppermute | solution.py:22
  116.2 18.9 %copy-start.4 = (f32[8,16,128]{2,1,0:T(8,128)}, f32[8,16,128]{2,1,0:T(8,128)S(1)}, u32[]{:S(2)}) copy-start(f32[8,16,128]{2,1,0:T(8,128)S(1)} %fusion.57) | copy-start | bytes 196612
  116.2 5.1 %collective-permute-start.20 = (f32[1,1,16,128]{3,2,1,0:T(8,128)S(1)}, f32[1,1,16,128]{3,2,1,0:T(8,128)S(1)}, u32[]{:S(2)}, u32[]{:S(2)}) collective-permute-start(f32[1,1,16,128]{3,2,1,0:T(8,128)S(1)} %get-tuple-element.47), channel_id=1, source_target_pairs={{0,64},{64,128},{128,192},{192,256},{256,320},{320,384},{384,448},... | collective-permute-start | bytes 24584 | tf_op jit(solution)/shard_map/ppermute | solution.py:21
  119.3 6.2 %collective-permute-start.21 = (f32[1,1,16,128]{3,2,1,0:T(8,128)S(1)}, f32[1,1,16,128]{3,2,1,0:T(8,128)S(1)}, u32[]{:S(2)}, u32[]{:S(2)}) collective-permute-start(f32[1,1,16,128]{3,2,1,0:T(8,128)S(1)} %get-tuple-element.48), channel_id=1, source_target_pairs={{64,0},{128,64},{192,128},{256,192},{320,256},{384,320},{448,384},... | collective-permute-start | bytes 24584 | tf_op jit(solution)/shard_map/ppermute | solution.py:22
  125.5 5.3 %collective-permute-start.22 = (f32[1,10,1,128]{3,2,1,0:T(1,128)S(1)}, f32[1,10,1,128]{3,2,1,0:T(1,128)S(1)}, u32[]{:S(2)}, u32[]{:S(2)}) collective-permute-start(f32[1,10,1,128]{3,2,1,0:T(1,128)S(1)} %get-tuple-element.39), channel_id=1, source_target_pairs={{0,1},{1,2},{2,3},{3,4},{4,5},{5,6},{6,7},{7,8},{8,9},{9,10},{10,1... | collective-permute-start | bytes 15368 | tf_op jit(solution)/shard_map/ppermute | solution.py:21
  127.4 7.7 %collective-permute-start.23 = (f32[1,10,1,128]{3,2,1,0:T(1,128)S(1)}, f32[1,10,1,128]{3,2,1,0:T(1,128)S(1)}, u32[]{:S(2)}, u32[]{:S(2)}) collective-permute-start(f32[1,10,1,128]{3,2,1,0:T(1,128)S(1)} %get-tuple-element.40), channel_id=1, source_target_pairs={{1,0},{2,1},{3,2},{4,3},{5,4},{6,5},{7,6},{8,7},{9,8},{10,9},{11,1... | collective-permute-start | bytes 15368 | tf_op jit(solution)/shard_map/ppermute | solution.py:22
  135.7 5.0 %collective-permute-start.28 = (f32[1,1,8,128]{3,2,1,0:T(8,128)S(1)}, f32[1,1,8,128]{3,2,1,0:T(8,128)S(1)}, u32[]{:S(2)}, u32[]{:S(2)}) collective-permute-start(f32[1,1,8,128]{3,2,1,0:T(8,128)S(1)} %get-tuple-element.73), channel_id=1, source_target_pairs={{0,64},{64,128},{128,192},{192,256},{256,320},{320,384},{384,448},... | collective-permute-start | bytes 12296 | tf_op jit(solution)/shard_map/ppermute | solution.py:21
  138.8 6.1 %collective-permute-start.29 = (f32[1,1,8,128]{3,2,1,0:T(8,128)S(1)}, f32[1,1,8,128]{3,2,1,0:T(8,128)S(1)}, u32[]{:S(2)}, u32[]{:S(2)}) collective-permute-start(f32[1,1,8,128]{3,2,1,0:T(8,128)S(1)} %get-tuple-element.74), channel_id=1, source_target_pairs={{64,0},{128,64},{192,128},{256,192},{320,256},{384,320},{448,384},... | collective-permute-start | bytes 12296 | tf_op jit(solution)/shard_map/ppermute | solution.py:22
  144.9 5.3 %collective-permute-start.30 = (f32[1,6,1,128]{3,2,1,0:T(1,128)S(1)}, f32[1,6,1,128]{3,2,1,0:T(1,128)S(1)}, u32[]{:S(2)}, u32[]{:S(2)}) collective-permute-start(f32[1,6,1,128]{3,2,1,0:T(1,128)S(1)} %get-tuple-element.65), channel_id=1, source_target_pairs={{0,1},{1,2},{2,3},{3,4},{4,5},{5,6},{6,7},{7,8},{8,9},{9,10},{10,1... | collective-permute-start | bytes 9224 | tf_op jit(solution)/shard_map/ppermute | solution.py:21
  146.8 7.7 %collective-permute-start.31 = (f32[1,6,1,128]{3,2,1,0:T(1,128)S(1)}, f32[1,6,1,128]{3,2,1,0:T(1,128)S(1)}, u32[]{:S(2)}, u32[]{:S(2)}) collective-permute-start(f32[1,6,1,128]{3,2,1,0:T(1,128)S(1)} %get-tuple-element.66), channel_id=1, source_target_pairs={{1,0},{2,1},{3,2},{4,3},{5,4},{6,5},{7,6},{8,7},{9,8},{10,9},{11,1... | collective-permute-start | bytes 9224 | tf_op jit(solution)/shard_map/ppermute | solution.py:22
  154.8 5.0 %collective-permute-start.32 = (f32[1,1,8,128]{3,2,1,0:T(8,128)S(1)}, f32[1,1,8,128]{3,2,1,0:T(8,128)S(1)}, u32[]{:S(2)}, u32[]{:S(2)}) collective-permute-start(f32[1,1,8,128]{3,2,1,0:T(8,128)S(1)} %get-tuple-element.71), channel_id=1, source_target_pairs={{0,64},{64,128},{128,192},{192,256},{256,320},{320,384},{384,448},... | collective-permute-start | bytes 12296 | tf_op jit(solution)/shard_map/ppermute | solution.py:21
  157.9 6.1 %collective-permute-start.33 = (f32[1,1,8,128]{3,2,1,0:T(8,128)S(1)}, f32[1,1,8,128]{3,2,1,0:T(8,128)S(1)}, u32[]{:S(2)}, u32[]{:S(2)}) collective-permute-start(f32[1,1,8,128]{3,2,1,0:T(8,128)S(1)} %get-tuple-element.72), channel_id=1, source_target_pairs={{64,0},{128,64},{192,128},{256,192},{320,256},{384,320},{448,384},... | collective-permute-start | bytes 12296 | tf_op jit(solution)/shard_map/ppermute | solution.py:22
  164.0 5.3 %collective-permute-start.34 = (f32[1,6,1,128]{3,2,1,0:T(1,128)S(1)}, f32[1,6,1,128]{3,2,1,0:T(1,128)S(1)}, u32[]{:S(2)}, u32[]{:S(2)}) collective-permute-start(f32[1,6,1,128]{3,2,1,0:T(1,128)S(1)} %get-tuple-element.63), channel_id=1, source_target_pairs={{0,1},{1,2},{2,3},{3,4},{4,5},{5,6},{6,7},{7,8},{8,9},{9,10},{10,1... | collective-permute-start | bytes 9224 | tf_op jit(solution)/shard_map/ppermute | solution.py:21
  165.9 7.7 %collective-permute-start.35 = (f32[1,6,1,128]{3,2,1,0:T(1,128)S(1)}, f32[1,6,1,128]{3,2,1,0:T(1,128)S(1)}, u32[]{:S(2)}, u32[]{:S(2)}) collective-permute-start(f32[1,6,1,128]{3,2,1,0:T(1,128)S(1)} %get-tuple-element.64), channel_id=1, source_target_pairs={{1,0},{2,1},{3,2},{4,3},{5,4},{6,5},{7,6},{8,7},{9,8},{10,9},{11,1... | collective-permute-start | bytes 9224 | tf_op jit(solution)/shard_map/ppermute | solution.py:22
  173.9 5.0 %collective-permute-start.36 = (f32[1,1,8,128]{3,2,1,0:T(8,128)S(1)}, f32[1,1,8,128]{3,2,1,0:T(8,128)S(1)}, u32[]{:S(2)}, u32[]{:S(2)}) collective-permute-start(f32[1,1,8,128]{3,2,1,0:T(8,128)S(1)} %get-tuple-element.69), channel_id=1, source_target_pairs={{0,64},{64,128},{128,192},{192,256},{256,320},{320,384},{384,448},... | collective-permute-start | bytes 12296 | tf_op jit(solution)/shard_map/ppermute | solution.py:21
  177.0 6.1 %collective-permute-start.37 = (f32[1,1,8,128]{3,2,1,0:T(8,128)S(1)}, f32[1,1,8,128]{3,2,1,0:T(8,128)S(1)}, u32[]{:S(2)}, u32[]{:S(2)}) collective-permute-start(f32[1,1,8,128]{3,2,1,0:T(8,128)S(1)} %get-tuple-element.70), channel_id=1, source_target_pairs={{64,0},{128,64},{192,128},{256,192},{320,256},{384,320},{448,384},... | collective-permute-start | bytes 12296 | tf_op jit(solution)/shard_map/ppermute | solution.py:22
  183.1 5.3 %collective-permute-start.38 = (f32[1,6,1,128]{3,2,1,0:T(1,128)S(1)}, f32[1,6,1,128]{3,2,1,0:T(1,128)S(1)}, u32[]{:S(2)}, u32[]{:S(2)}) collective-permute-start(f32[1,6,1,128]{3,2,1,0:T(1,128)S(1)} %get-tuple-element.61), channel_id=1, source_target_pairs={{0,1},{1,2},{2,3},{3,4},{4,5},{5,6},{6,7},{7,8},{8,9},{9,10},{10,1... | collective-permute-start | bytes 9224 | tf_op jit(solution)/shard_map/ppermute | solution.py:21
  185.0 7.7 %collective-permute-start.39 = (f32[1,6,1,128]{3,2,1,0:T(1,128)S(1)}, f32[1,6,1,128]{3,2,1,0:T(1,128)S(1)}, u32[]{:S(2)}, u32[]{:S(2)}) collective-permute-start(f32[1,6,1,128]{3,2,1,0:T(1,128)S(1)} %get-tuple-element.62), channel_id=1, source_target_pairs={{1,0},{2,1},{3,2},{4,3},{5,4},{6,5},{7,6},{8,7},{9,8},{10,9},{11,1... | collective-permute-start | bytes 9224 | tf_op jit(solution)/shard_map/ppermute | solution.py:22
where the time goes:
time: 195 us; the launch traced here: 194 us
  starting transfers between devices  124 us (64%)
  waiting for transfers between devices  60.9 us (31%)
  other arithmetic  6.34 us (3%)
    ppermute x20, starting transfers between devices, with_halo(): before = lax.ppermute(last, axis, up)  76.7 us
    ppermute x20, waiting for transfers between devices, with_halo(): after = lax.ppermute(leading, axis, down)  60.9 us
    ppermute x20, starting transfers between devices, with_halo(): after = lax.ppermute(leading, axis, down)  47.1 us
  transfers between devices with their start and end apart: 40, of which 14 were waited for; matrix products, arithmetic and copies ran while one was open for 2% of the time, Pallas kernels for 0%

commit v1 on v0

v1 whole, which is shorter than its diff:
```python
import jax
import jax.numpy as jnp
from jax import lax
from jax.sharding import PartitionSpec as P

SWEEPS = 2
COARSE = 4

STORE = 0.1
OMEGA = 0.8

FINE_HALO = 8
COARSE_HALO = 4


def harmonic(first, second):
    total = first + second
    return 2.0 * first * second / jnp.where(total > 0, total, 1.0)


def shift(a, axis, step):
    length = a.shape[axis]
    zeros_shape = list(a.shape)
    zeros_shape[axis] = abs(step)
    zeros = jnp.zeros(zeros_shape, a.dtype)
    if step > 0:
        return jnp.concatenate([lax.slice_in_dim(a, step, length, axis=axis), zeros], axis=axis)
    return jnp.concatenate([zeros, lax.slice_in_dim(a, 0, length + step, axis=axis)], axis=axis)


def coefficients(perm, scale):
    couple = []
    for axis in range(3):
        c = harmonic(shift(perm, axis, 1), perm)
        if axis < 2:
            c = scale * c
        couple.append(c)
    diagonal = STORE
    for axis in range(3):
        diagonal = diagonal + (shift(couple[axis], axis, -1) + couple[axis])
    return couple, diagonal


def apply_operator(value, parts):
    couple, diagonal = parts
    out = STORE * value
    for axis in range(3):
        flow = couple[axis] * (value - shift(value, axis, 1))
        out = out + (flow - shift(flow, axis, -1))
    return out


def restrict(field):
    sx, sy, sz = field.shape
    return 0.25 * jnp.sum(field.reshape(sx // 2, 2, sy // 2, 2, sz), axis=(1, 3))


def exchange(x, h):
    nxg = lax.axis_size("gx")
    nyg = lax.axis_size("gy")
    nx, ny = x.shape[-3], x.shape[-2]

    def sl(a, lo, hi, axis):
        return lax.slice_in_dim(a, lo, hi, axis=a.ndim + axis)

    def send(block, dx, dy):
        if dx == 0:
            pairs = [(j, j + dy) for j in range(nyg) if 0 <= j + dy < nyg]
            return lax.ppermute(block, "gy", pairs)
        if dy == 0:
            pairs = [(i, i + dx) for i in range(nxg) if 0 <= i + dx < nxg]
            return lax.ppermute(block, "gx", pairs)
        pairs = [
            (i * nyg + j, (i + dx) * nyg + j + dy)
            for i in range(nxg)
            for j in range(nyg)
            if 0 <= i + dx < nxg and 0 <= j + dy < nyg
        ]
        return lax.ppermute(block, ("gx", "gy"), pairs)

    x_lo = sl(x, 0, h, -3)
    x_hi = sl(x, nx - h, nx, -3)
    y_lo = sl(x, 0, h, -2)
    y_hi = sl(x, ny - h, ny, -2)
    from_xm = send(x_hi, 1, 0)
    from_xp = send(x_lo, -1, 0)
    from_ym = send(y_hi, 0, 1)
    from_yp = send(y_lo, 0, -1)
    from_mm = send(sl(x_hi, ny - h, ny, -2), 1, 1)
    from_mp = send(sl(x_hi, 0, h, -2), 1, -1)
    from_pm = send(sl(x_lo, ny - h, ny, -2), -1, 1)
    from_pp = send(sl(x_lo, 0, h, -2), -1, -1)
    low = jnp.concatenate([from_mm, from_xm, from_mp], axis=-2)
    mid = jnp.concatenate([from_ym, x, from_yp], axis=-2)
    high = jnp.concatenate([from_pm, from_xp, from_pp], axis=-2)
    return jnp.concatenate([low, mid, high], axis=-3)


def inner(a, h):
    return a[h:a.shape[0] - h, h:a.shape[1] - h]


def body(pressure_init, source, permeability):
    h0 = FINE_HALO
    region = exchange(jnp.stack([permeability, pressure_init, source]), h0)
    perm0, pressure, src = region[0], region[1], region[2]
    parts0 = coefficients(perm0, 1.0)
    for step in range(SWEEPS):
        pressure = pressure + OMEGA * (src - apply_operator(pressure, parts0)) / parts0[1]
    resid0 = src - apply_operator(pressure, parts0)
    pressure_out = inner(pressure, h0)

    h1 = h0 // 2
    rhs_mid = restrict(resid0)
    perm_mid = restrict(perm0)
    parts1 = coefficients(perm_mid, 0.25)
    value = OMEGA * rhs_mid / parts1[1]
    for step in range(SWEEPS - 1):
        value = value + OMEGA * (rhs_mid - apply_operator(value, parts1)) / parts1[1]
    resid1 = rhs_mid - apply_operator(value, parts1)
    correction_mid = inner(value, h1)

    h2 = COARSE_HALO
    rhs_coarse = restrict(inner(resid1, h1))
    perm_coarse = restrict(inner(perm_mid, h1))
    region2 = exchange(jnp.stack([perm_coarse, rhs_coarse]), h2)
    perm2, rhs2 = region2[0], region2[1]
    parts2 = coefficients(perm2, 0.0625)
    value = OMEGA * rhs2 / parts2[1]
    for step in range(COARSE - 1):
        value = value + OMEGA * (rhs2 - apply_operator(value, parts2)) / parts2[1]
    correction_coarse = inner(value, h2)
    return (pressure_out, correction_mid, correction_coarse)


def solution(mesh):
    placed = (P("gx", "gy", None), P("gx", "gy", None), P("gx", "gy", None))
    return jax.shard_map(
        body,
        mesh=mesh,
        in_specs=placed,
        out_specs=(P("gx", "gy", None), P("gx", "gy", None), P("gx", "gy", None)),
        check_vma=False,
    )
```

time: 195 us -> 96.5 us (0.49)
  the two profiles are of different devices: /device:TPU:223 before, /device:TPU:800 now
where the time goes in v1:
time: 96.5 us; the launch traced here: 95.8 us
  starting transfers between devices  51.4 us (53%)
  waiting for transfers between devices  17.9 us (19%)
  other arithmetic  16 us (17%)
  local copies, waits for them, and re-layouts  9.12 us (9%)
  between operations  1.44 us (1%)
    ppermute x8, starting transfers between devices, send(): return lax.ppermute(block, ('gx', 'gy'), pairs)  30.1 us
    ppermute x8, waiting for transfers between devices, send(): return lax.ppermute(block, ('gx', 'gy'), pairs)  17.9 us
    ppermute x4, starting transfers between devices, send(): return lax.ppermute(block, 'gy', pairs)  11.2 us
    ppermute x4, starting transfers between devices, send(): return lax.ppermute(block, 'gx', pairs)  10 us
    slice x33, local copies, waits for them, and re-layouts, shift(): lax.slice_in_dim(a, step, length, axis=axis)  6.37 us
    mul x8, other arithmetic, apply_operator(): flow = couple[axis] * (value - shift(value, axis, 1))  4.08 us
    reduce_sum x4, other arithmetic, restrict(): jnp.sum(field.reshape(sx // 2, 2, sy // 2, 2, sz), axis=(1, 3))  3.48 us
  transfers between devices with their start and end apart: 16, of which 2 were waited for; matrix products, arithmetic and copies ran while one was open for 1% of the time, Pallas kernels for 0%

profile of v1, /device:TPU:800, one launch (start us, length us, event | category | flops | bytes accessed | tf_op | source)
XLA Modules:
  0.0 95.8 jit_solution(16055457773510341034)
XLA Ops:
  0.7 1.2 %pad_maximum_fusion = f32[3,16,32,128]{3,2,1,0:T(8,128)S(1)} fusion(f32[1,16,32,128]{3,2,1,0:T(8,128)} %bitcast.99, f32[1,16,32,128]{3,2,1,0:T(8,128)} %bitcast.101, f32[1,16,32,128]{3,2,1,0:T(8,128)} %bitcast.103), kind=kLoop, calls=%fused_computation.9 | loop fusion | flops 393216 | bytes 1572864 | tf_op jit(solution)/shard_map/stack | solution.py:105
  1.9 5.2 %collective-permute-start.7 = (f32[3,8,8,128]{3,2,1,0:T(8,128)S(1)}, f32[3,8,8,128]{3,2,1,0:T(8,128)S(1)}, u32[]{:S(2)}, u32[]{:S(2)}) collective-permute-start(f32[3,8,8,128]{3,2,1,0:T(8,128)S(1)} %get-tuple-element.34), channel_id=1, source_target_pairs={{65,0},{66,1},{67,2},{68,3},{69,4},{70,5},{71,6},{72,7},{73,8},{74... | collective-permute-start | bytes 294920 | tf_op jit(solution)/shard_map/ppermute | solution.py:79
  7.2 2.8 %collective-permute-start.6 = (f32[3,8,32,128]{3,2,1,0:T(8,128)S(1)}, f32[3,8,32,128]{3,2,1,0:T(8,128)S(1)}, u32[]{:S(2)}, u32[]{:S(2)}) collective-permute-start(f32[3,8,32,128]{3,2,1,0:T(8,128)S(1)} %get-tuple-element.37), channel_id=1, source_target_pairs={{64,0},{128,64},{192,128},{256,192},{320,256},{384,320},{448,384},... | collective-permute-start | bytes 1179656 | tf_op jit(solution)/shard_map/ppermute | solution.py:72
  10.0 1.9 %collective-permute-start.5 = (f32[3,8,8,128]{3,2,1,0:T(8,128)S(1)}, f32[3,8,8,128]{3,2,1,0:T(8,128)S(1)}, u32[]{:S(2)}, u32[]{:S(2)}) collective-permute-start(f32[3,8,8,128]{3,2,1,0:T(8,128)S(1)} %get-tuple-element.33), channel_id=1, source_target_pairs={{64,1},{65,2},{66,3},{67,4},{68,5},{69,6},{70,7},{71,8},{72,9},{73... | collective-permute-start | bytes 294920 | tf_op jit(solution)/shard_map/ppermute | solution.py:79
  11.9 7.0 %collective-permute-start.2 = (f32[3,8,8,128]{3,2,1,0:T(8,128)S(1)}, f32[3,8,8,128]{3,2,1,0:T(8,128)S(1)}, u32[]{:S(2)}, u32[]{:S(2)}) collective-permute-start(f32[3,8,8,128]{3,2,1,0:T(8,128)S(1)} %get-tuple-element.35), channel_id=1, source_target_pairs={{1,64},{2,65},{3,66},{4,67},{5,68},{6,69},{7,70},{8,71},{9,72},{10... | collective-permute-start | bytes 294920 | tf_op jit(solution)/shard_map/ppermute | solution.py:79
  18.9 2.8 %collective-permute-start.1 = (f32[3,8,32,128]{3,2,1,0:T(8,128)S(1)}, f32[3,8,32,128]{3,2,1,0:T(8,128)S(1)}, u32[]{:S(2)}, u32[]{:S(2)}) collective-permute-start(f32[3,8,32,128]{3,2,1,0:T(8,128)S(1)} %get-tuple-element.36), channel_id=1, source_target_pairs={{0,64},{64,128},{128,192},{192,256},{256,320},{320,384},{384,448},... | collective-permute-start | bytes 1179656 | tf_op jit(solution)/shard_map/ppermute | solution.py:72
  21.7 1.9 %collective-permute-start.4 = (f32[3,16,8,128]{3,2,1,0:T(8,128)S(1)}, f32[3,16,8,128]{3,2,1,0:T(8,128)S(1)}, u32[]{:S(2)}, u32[]{:S(2)}) collective-permute-start(f32[3,16,8,128]{3,2,1,0:T(8,128)S(1)} %get-tuple-element.39), channel_id=1, source_target_pairs={{1,0},{2,1},{3,2},{4,3},{5,4},{6,5},{7,6},{8,7},{9,8},{10,9},{11,1... | collective-permute-start | bytes 589832 | tf_op jit(solution)/shard_map/ppermute | solution.py:69
  23.6 3.9 %collective-permute-start.3 = (f32[3,16,8,128]{3,2,1,0:T(8,128)S(1)}, f32[3,16,8,128]{3,2,1,0:T(8,128)S(1)}, u32[]{:S(2)}, u32[]{:S(2)}) collective-permute-start(f32[3,16,8,128]{3,2,1,0:T(8,128)S(1)} %get-tuple-element.38), channel_id=1, source_target_pairs={{0,1},{1,2},{2,3},{3,4},{4,5},{5,6},{6,7},{7,8},{8,9},{9,10},{10,1... | collective-permute-start | bytes 589832 | tf_op jit(solution)/shard_map/ppermute | solution.py:69
  27.6 2.1 %collective-permute-start = (f32[3,8,8,128]{3,2,1,0:T(8,128)S(1)}, f32[3,8,8,128]{3,2,1,0:T(8,128)S(1)}, u32[]{:S(2)}, u32[]{:S(2)}) collective-permute-start(f32[3,8,8,128]{3,2,1,0:T(8,128)S(1)} %get-tuple-element.32), channel_id=1, source_target_pairs={{0,65},{1,66},{2,67},{3,68},{4,69},{5,70},{6,71},{7,72},{8,73},{9,... | collective-permute-start | bytes 294920 | tf_op jit(solution)/shard_map/ppermute | solution.py:79
  29.7 10.0 %collective-permute-done = f32[3,8,8,128]{3,2,1,0:T(8,128)S(1)} collective-permute-done((f32[3,8,8,128]{3,2,1,0:T(8,128)S(1)}, f32[3,8,8,128]{3,2,1,0:T(8,128)S(1)}, u32[]{:S(2)}, u32[]{:S(2)}) %collective-permute-start) | collective-permute-done | bytes 98336 | tf_op jit(solution)/shard_map/ppermute | solution.py:79
  39.7 1.1 %maximum_maximum_fusion = f32[3,32,48,128]{3,2,1,0:T(8,128)S(1)} fusion(f32[3,8,8,128]{3,2,1,0:T(8,128)S(1)} %collective-permute-done.7, f32[3,8,32,128]{3,2,1,0:T(8,128)S(1)} %collective-permute-done.6, f32[3,8,8,128]{3,2,1,0:T(8,128)S(1)} %collective-permute-done.5, f32[3,16,8,128]{3,2,1,0:T(8,128)S(1)} %collective-permute-done.4, ...), kind=kLoop, calls=%fused_computation | loop fusion | flops 5898240 | bytes 4718592 | tf_op jit(solution)/shard_map/concatenate | solution.py:96
  41.0 1.0 %fusion.23 = (f32[1,32,48,128]{3,2,1,0:T(8,128)}, f32[32,48,128]{2,1,0:T(8,128)S(1)}, f32[32,48,128]{2,1,0:T(8,128)S(1)}) fusion(f32[3,32,48,128]{3,2,1,0:T(8,128)S(1)} %maximum_maximum_fusion), kind=kLoop, calls=%fused_computation.95 | loop fusion | bytes 3932160 | tf_op jit(solution)/shard_map/slice | solution.py:106
  42.1 0.3 slice.385
  42.4 0.3 slice.384
  42.7 0.8 subtract_multiply_fusion.8
  43.7 0.9 divide_add_fusion.1
  44.6 0.3 slice.394
  45.0 0.3 subtract_multiply_fusion.5
  45.4 0.5 divide_add_fusion
  45.9 1.0 %slice.397 = f32[31,48,128]{2,1,0:T(8,128)} slice(f32[32,48,128]{2,1,0:T(8,128)S(1)} %divide_add_fusion), slice={[1:32], [0:48], [0:128]} | slice | bytes 1523712 | tf_op jit(solution)/shard_map/slice | solution.py:27
  46.9 1.2 %slice.401 = f32[32,48,127]{2,1,0:T(8,128)} slice(f32[32,48,128]{2,1,0:T(8,128)S(1)} %divide_add_fusion), slice={[0:32], [0:48], [1:128]} | slice | bytes 1560576 | tf_op jit(solution)/shard_map/slice | solution.py:27
  48.0 0.9 slice.399
  49.0 1.7 %reduce_sum.37 = f32[16,24,128]{2,1,0:T(8,128)S(1)} reduce(f32[16,2,24,2,128]{4,3,2,1,0:T(2,128)} %bitcast.93, f32[]{:T(128)} %constant.9.clone.1), dimensions={1,3}, to_apply=%region_1.2 | reduce | flops 147456 | bytes 983044 | tf_op jit(solution)/shard_map/reduce_sum | solution.py:55
  50.7 0.8 slice.407
  51.5 0.7 slice.405
  52.2 2.7 %subtract_multiply_fusion.2 = (f32[32,48,128]{2,1,0:T(8,128)S(1)}, f32[32,48,128]{2,1,0:T(8,128)S(1)}, f32[32,48,128]{2,1,0:T(8,128)S(1)}) fusion(f32[32,48,128]{2,1,0:T(8,128)} %copy-done.2, f32[32,48,128]{2,1,0:T(8,128)S(1)} %divide_add_fusion, f32[31,48,128]{2,1,0:T(8,128)} %slice.397, f32[32,48,128]{2,1,0:T(8,128)} %copy-done.1, ...), kind=kLoop, calls=%fused_computation.13 | loop fusion | flops 1179648 | bytes 7817216 | tf_op jit(solution)/shard_map/mul | solution.py:48
  54.9 1.3 %add_subtract_fusion = f32[32,48,128]{2,1,0:T(8,128)} fusion(f32[32,48,128]{2,1,0:T(8,128)S(1)} %get-tuple-element.27, f32[32,48,127]{2,1,0:T(8,128)S(1)} %bitcast.87, f32[32,48,128]{2,1,0:T(8,128)S(1)} %get-tuple-element.28, f32[32,47,128]{2,1,0:T(8,128)S(1)} %bitcast.88, f32[32,48,128]{2,1,0:T(8,128)S(1)} %get-tuple-element.26, ...), kind=kLoop, calls=%fused_computation.10 | loop fusion | flops 1572864 | bytes 7030784 | tf_op jit(solution)/shard_map/sub | solution.py:110
  56.2 1.7 %reduce_sum.36 = f32[16,24,128]{2,1,0:T(8,128)S(1)} reduce(f32[16,2,24,2,128]{4,3,2,1,0:T(2,128)} %bitcast.94, f32[]{:T(128)} %constant.9.clone.1), dimensions={1,3}, to_apply=%region_0.1 | reduce | flops 147456 | bytes 983044 | tf_op jit(solution)/shard_map/reduce_sum | solution.py:55
  57.9 1.2 %fusion.4 = (f32[16,24,128]{2,1,0:T(8,128)S(1)}, f32[16,24,128]{2,1,0:T(8,128)S(1)}, f32[16,24,128]{2,1,0:T(8,128)S(1)}) fusion(f32[15,24,128]{2,1,0:T(8,128)S(1)} %slice-done, f32[16,24,128]{2,1,0:T(8,128)S(1)} %reduce_sum.37, f32[16,24,127]{2,1,0:T(8,128)} %slice.407, f32[16,23,128]{2,1,0:T(8,128)} %slice.405), kind=kLoop, calls=%fused_computation.32 | loop fusion | flops 1032192 | bytes 1354240 | tf_op jit(solution)/shard_map/mul | solution.py:36
  59.2 0.1 multiply_divide_fusion
  59.3 0.1 slice.413
  59.6 0.1 divide_add_fusion.2
  59.8 0.1 slice.421
  59.9 0.5 copy-done.4
  60.5 0.7 slice_subtract_fusion
  61.3 1.9 %collective-permute-start.15 = (f32[2,4,4,128]{3,2,1,0:T(4,128)S(1)}, f32[2,4,4,128]{3,2,1,0:T(4,128)S(1)}, u32[]{:S(2)}, u32[]{:S(2)}) collective-permute-start(f32[2,4,4,128]{3,2,1,0:T(4,128)S(1)} %get-tuple-element.66), channel_id=1, source_target_pairs={{65,0},{66,1},{67,2},{68,3},{69,4},{70,5},{71,6},{72,7},{73,8},{74... | collective-permute-start | bytes 49160 | tf_op jit(solution)/shard_map/ppermute | solution.py:79
  63.2 1.9 %collective-permute-start.12 = (f32[2,4,4,128]{3,2,1,0:T(4,128)S(1)}, f32[2,4,4,128]{3,2,1,0:T(4,128)S(1)}, u32[]{:S(2)}, u32[]{:S(2)}) collective-permute-start(f32[2,4,4,128]{3,2,1,0:T(4,128)S(1)} %get-tuple-element.66), channel_id=1, source_target_pairs={{1,0},{2,1},{3,2},{4,3},{5,4},{6,5},{7,6},{8,7},{9,8},{10,9},{11,1... | collective-permute-start | bytes 49160 | tf_op jit(solution)/shard_map/ppermute | solution.py:69
  65.2 3.4 %collective-permute-start.13 = (f32[2,4,4,128]{3,2,1,0:T(4,128)S(1)}, f32[2,4,4,128]{3,2,1,0:T(4,128)S(1)}, u32[]{:S(2)}, u32[]{:S(2)}) collective-permute-start(f32[2,4,4,128]{3,2,1,0:T(4,128)S(1)} %get-tuple-element.65), channel_id=1, source_target_pairs={{64,1},{65,2},{66,3},{67,4},{68,5},{69,6},{70,7},{71,8},{72,9},{73... | collective-permute-start | bytes 49160 | tf_op jit(solution)/shard_map/ppermute | solution.py:79
  68.6 2.5 %collective-permute-start.14 = (f32[2,4,8,128]{3,2,1,0:T(8,128)S(1)}, f32[2,4,8,128]{3,2,1,0:T(8,128)S(1)}, u32[]{:S(2)}, u32[]{:S(2)}) collective-permute-start(f32[2,4,8,128]{3,2,1,0:T(8,128)S(1)} %pad_maximum_fusion.1), channel_id=1, source_target_pairs={{64,0},{128,64},{192,128},{256,192},{320,256},{384,320},{448,384},... | collective-permute-start | bytes 98312 | tf_op jit(solution)/shard_map/ppermute | solution.py:72
  71.0 2.0 %collective-permute-start.9 = (f32[2,4,8,128]{3,2,1,0:T(8,128)S(1)}, f32[2,4,8,128]{3,2,1,0:T(8,128)S(1)}, u32[]{:S(2)}, u32[]{:S(2)}) collective-permute-start(f32[2,4,8,128]{3,2,1,0:T(8,128)S(1)} %pad_maximum_fusion.1), channel_id=1, source_target_pairs={{0,64},{64,128},{128,192},{192,256},{256,320},{320,384},{384,448},... | collective-permute-start | bytes 98312 | tf_op jit(solution)/shard_map/ppermute | solution.py:72
  73.1 3.5 %collective-permute-start.11 = (f32[2,4,4,128]{3,2,1,0:T(4,128)S(1)}, f32[2,4,4,128]{3,2,1,0:T(4,128)S(1)}, u32[]{:S(2)}, u32[]{:S(2)}) collective-permute-start(f32[2,4,4,128]{3,2,1,0:T(4,128)S(1)} %get-tuple-element.65), channel_id=1, source_target_pairs={{0,1},{1,2},{2,3},{3,4},{4,5},{5,6},{6,7},{7,8},{8,9},{9,10},{10,1... | collective-permute-start | bytes 49160 | tf_op jit(solution)/shard_map/ppermute | solution.py:69
  76.6 6.8 %collective-permute-start.10 = (f32[2,4,4,128]{3,2,1,0:T(4,128)S(1)}, f32[2,4,4,128]{3,2,1,0:T(4,128)S(1)}, u32[]{:S(2)}, u32[]{:S(2)}) collective-permute-start(f32[2,4,4,128]{3,2,1,0:T(4,128)S(1)} %get-tuple-element.66), channel_id=1, source_target_pairs={{1,64},{2,65},{3,66},{4,67},{5,68},{6,69},{7,70},{8,71},{9,72},{10... | collective-permute-start | bytes 49160 | tf_op jit(solution)/shard_map/ppermute | solution.py:79
  83.3 1.9 %collective-permute-start.8 = (f32[2,4,4,128]{3,2,1,0:T(4,128)S(1)}, f32[2,4,4,128]{3,2,1,0:T(4,128)S(1)}, u32[]{:S(2)}, u32[]{:S(2)}) collective-permute-start(f32[2,4,4,128]{3,2,1,0:T(4,128)S(1)} %get-tuple-element.65), channel_id=1, source_target_pairs={{0,65},{1,66},{2,67},{3,68},{4,69},{5,70},{6,71},{7,72},{8,73},{9,... | collective-permute-start | bytes 49160 | tf_op jit(solution)/shard_map/ppermute | solution.py:79
  85.3 0.7 slice.396
  86.0 7.8 %collective-permute-done.8 = f32[2,4,4,128]{3,2,1,0:T(4,128)S(1)} collective-permute-done((f32[2,4,4,128]{3,2,1,0:T(4,128)S(1)}, f32[2,4,4,128]{3,2,1,0:T(4,128)S(1)}, u32[]{:S(2)}, u32[]{:S(2)}) %collective-permute-start.8) | collective-permute-done | bytes 16416 | tf_op jit(solution)/shard_map/ppermute | solution.py:79
  94.1 0.1 multiply_divide_fusion.1
  94.5 0.1 divide_add_fusion.4
  95.1 0.7 slice_add_fusion
  (84 shorter events, 2.0 us)
Async XLA Ops:
  0.6 39.1 %copy-start.5 = (f32[16,32,128]{2,1,0:T(8,128)S(1)}, f32[16,32,128]{2,1,0:T(8,128)}, u32[]{:S(2)}) copy-start(f32[16,32,128]{2,1,0:T(8,128)} %param.4) | copy-start | bytes 786436
  0.6 39.1 %copy-start.6 = (f32[16,32,128]{2,1,0:T(8,128)S(1)}, f32[16,32,128]{2,1,0:T(8,128)}, u32[]{:S(2)}) copy-start(f32[16,32,128]{2,1,0:T(8,128)} %param.3) | copy-start | bytes 786436
  0.7 39.1 %copy-start.7 = (f32[16,32,128]{2,1,0:T(8,128)S(1)}, f32[16,32,128]{2,1,0:T(8,128)}, u32[]{:S(2)}) copy-start(f32[16,32,128]{2,1,0:T(8,128)} %param.5) | copy-start | bytes 786436
  1.9 19.8 %collective-permute-start.7 = (f32[3,8,8,128]{3,2,1,0:T(8,128)S(1)}, f32[3,8,8,128]{3,2,1,0:T(8,128)S(1)}, u32[]{:S(2)}, u32[]{:S(2)}) collective-permute-start(f32[3,8,8,128]{3,2,1,0:T(8,128)S(1)} %get-tuple-element.34), channel_id=1, source_target_pairs={{65,0},{66,1},{67,2},{68,3},{69,4},{70,5},{71,6},{72,7},{73,8},{74... | collective-permute-start | bytes 294920 | tf_op jit(solution)/shard_map/ppermute | solution.py:79
  7.2 32.5 %collective-permute-start.6 = (f32[3,8,32,128]{3,2,1,0:T(8,128)S(1)}, f32[3,8,32,128]{3,2,1,0:T(8,128)S(1)}, u32[]{:S(2)}, u32[]{:S(2)}) collective-permute-start(f32[3,8,32,128]{3,2,1,0:T(8,128)S(1)} %get-tuple-element.37), channel_id=1, source_target_pairs={{64,0},{128,64},{192,128},{256,192},{320,256},{384,320},{448,384},... | collective-permute-start | bytes 1179656 | tf_op jit(solution)/shard_map/ppermute | solution.py:72
  10.0 13.6 %collective-permute-start.5 = (f32[3,8,8,128]{3,2,1,0:T(8,128)S(1)}, f32[3,8,8,128]{3,2,1,0:T(8,128)S(1)}, u32[]{:S(2)}, u32[]{:S(2)}) collective-permute-start(f32[3,8,8,128]{3,2,1,0:T(8,128)S(1)} %get-tuple-element.33), channel_id=1, source_target_pairs={{64,1},{65,2},{66,3},{67,4},{68,5},{69,6},{70,7},{71,8},{72,9},{73... | collective-permute-start | bytes 294920 | tf_op jit(solution)/shard_map/ppermute | solution.py:79
  11.9 15.7 %collective-permute-start.2 = (f32[3,8,8,128]{3,2,1,0:T(8,128)S(1)}, f32[3,8,8,128]{3,2,1,0:T(8,128)S(1)}, u32[]{:S(2)}, u32[]{:S(2)}) collective-permute-start(f32[3,8,8,128]{3,2,1,0:T(8,128)S(1)} %get-tuple-element.35), channel_id=1, source_target_pairs={{1,64},{2,65},{3,66},{4,67},{5,68},{6,69},{7,70},{8,71},{9,72},{10... | collective-permute-start | bytes 294920 | tf_op jit(solution)/shard_map/ppermute | solution.py:79
  18.9 20.8 %collective-permute-start.1 = (f32[3,8,32,128]{3,2,1,0:T(8,128)S(1)}, f32[3,8,32,128]{3,2,1,0:T(8,128)S(1)}, u32[]{:S(2)}, u32[]{:S(2)}) collective-permute-start(f32[3,8,32,128]{3,2,1,0:T(8,128)S(1)} %get-tuple-element.36), channel_id=1, source_target_pairs={{0,64},{64,128},{128,192},{192,256},{256,320},{320,384},{384,448},... | collective-permute-start | bytes 1179656 | tf_op jit(solution)/shard_map/ppermute | solution.py:72
  21.7 18.0 %collective-permute-start.4 = (f32[3,16,8,128]{3,2,1,0:T(8,128)S(1)}, f32[3,16,8,128]{3,2,1,0:T(8,128)S(1)}, u32[]{:S(2)}, u32[]{:S(2)}) collective-permute-start(f32[3,16,8,128]{3,2,1,0:T(8,128)S(1)} %get-tuple-element.39), channel_id=1, source_target_pairs={{1,0},{2,1},{3,2},{4,3},{5,4},{6,5},{7,6},{8,7},{9,8},{10,9},{11,1... | collective-permute-start | bytes 589832 | tf_op jit(solution)/shard_map/ppermute | solution.py:69
  23.6 16.1 %collective-permute-start.3 = (f32[3,16,8,128]{3,2,1,0:T(8,128)S(1)}, f32[3,16,8,128]{3,2,1,0:T(8,128)S(1)}, u32[]{:S(2)}, u32[]{:S(2)}) collective-permute-start(f32[3,16,8,128]{3,2,1,0:T(8,128)S(1)} %get-tuple-element.38), channel_id=1, source_target_pairs={{0,1},{1,2},{2,3},{3,4},{4,5},{5,6},{6,7},{7,8},{8,9},{9,10},{10,1... | collective-permute-start | bytes 589832 | tf_op jit(solution)/shard_map/ppermute | solution.py:69
  27.6 12.1 %collective-permute-start = (f32[3,8,8,128]{3,2,1,0:T(8,128)S(1)}, f32[3,8,8,128]{3,2,1,0:T(8,128)S(1)}, u32[]{:S(2)}, u32[]{:S(2)}) collective-permute-start(f32[3,8,8,128]{3,2,1,0:T(8,128)S(1)} %get-tuple-element.32), channel_id=1, source_target_pairs={{0,65},{1,66},{2,67},{3,68},{4,69},{5,70},{6,71},{7,72},{8,73},{9,... | collective-permute-start | bytes 294920 | tf_op jit(solution)/shard_map/ppermute | solution.py:79
  43.5 1.4 %copy-start = (f32[32,48,128]{2,1,0:T(8,128)}, f32[32,48,128]{2,1,0:T(8,128)S(1)}, u32[]{:S(2)}) copy-start(f32[32,48,128]{2,1,0:T(8,128)S(1)} %get-tuple-element.21) | copy-start | bytes 2359300
  43.5 1.4 %copy-start.1 = (f32[32,48,128]{2,1,0:T(8,128)}, f32[32,48,128]{2,1,0:T(8,128)S(1)}, u32[]{:S(2)}) copy-start(f32[32,48,128]{2,1,0:T(8,128)S(1)} %get-tuple-element.23) | copy-start | bytes 2359300
  43.5 1.4 %copy-start.2 = (f32[32,48,128]{2,1,0:T(8,128)}, f32[32,48,128]{2,1,0:T(8,128)S(1)}, u32[]{:S(2)}) copy-start(f32[32,48,128]{2,1,0:T(8,128)S(1)} %get-tuple-element.12) | copy-start | bytes 2359300
  50.7 4.2 %copy-start.3 = (f32[16,24,128]{2,1,0:T(8,128)}, f32[16,24,128]{2,1,0:T(8,128)S(1)}, u32[]{:S(2)}) copy-start(f32[16,24,128]{2,1,0:T(8,128)S(1)} %broadcast_multiply_fusion.1) | copy-start | bytes 589828
  54.9 3.0 %slice-start = ((f32[16,24,128]{2,1,0:T(8,128)}), f32[15,24,128]{2,1,0:T(8,128)S(1)}, s32[]{:S(2)}) async-start(f32[16,24,128]{2,1,0:T(8,128)} %copy-done.3), calls=%async_computation | async-start | bytes 368640 | tf_op jit(solution)/shard_map/slice | solution.py:27
  59.5 0.9 copy-start.4
  61.3 11.8 %collective-permute-start.15 = (f32[2,4,4,128]{3,2,1,0:T(4,128)S(1)}, f32[2,4,4,128]{3,2,1,0:T(4,128)S(1)}, u32[]{:S(2)}, u32[]{:S(2)}) collective-permute-start(f32[2,4,4,128]{3,2,1,0:T(4,128)S(1)} %get-tuple-element.66), channel_id=1, source_target_pairs={{65,0},{66,1},{67,2},{68,3},{69,4},{70,5},{71,6},{72,7},{73,8},{74... | collective-permute-start | bytes 49160 | tf_op jit(solution)/shard_map/ppermute | solution.py:79
  63.2 20.1 %collective-permute-start.12 = (f32[2,4,4,128]{3,2,1,0:T(4,128)S(1)}, f32[2,4,4,128]{3,2,1,0:T(4,128)S(1)}, u32[]{:S(2)}, u32[]{:S(2)}) collective-permute-start(f32[2,4,4,128]{3,2,1,0:T(4,128)S(1)} %get-tuple-element.66), channel_id=1, source_target_pairs={{1,0},{2,1},{3,2},{4,3},{5,4},{6,5},{7,6},{8,7},{9,8},{10,9},{11,1... | collective-permute-start | bytes 49160 | tf_op jit(solution)/shard_map/ppermute | solution.py:69
  65.2 11.4 %collective-permute-start.13 = (f32[2,4,4,128]{3,2,1,0:T(4,128)S(1)}, f32[2,4,4,128]{3,2,1,0:T(4,128)S(1)}, u32[]{:S(2)}, u32[]{:S(2)}) collective-permute-start(f32[2,4,4,128]{3,2,1,0:T(4,128)S(1)} %get-tuple-element.65), channel_id=1, source_target_pairs={{64,1},{65,2},{66,3},{67,4},{68,5},{69,6},{70,7},{71,8},{72,9},{73... | collective-permute-start | bytes 49160 | tf_op jit(solution)/shard_map/ppermute | solution.py:79
  68.6 25.3 %collective-permute-start.14 = (f32[2,4,8,128]{3,2,1,0:T(8,128)S(1)}, f32[2,4,8,128]{3,2,1,0:T(8,128)S(1)}, u32[]{:S(2)}, u32[]{:S(2)}) collective-permute-start(f32[2,4,8,128]{3,2,1,0:T(8,128)S(1)} %pad_maximum_fusion.1), channel_id=1, source_target_pairs={{64,0},{128,64},{192,128},{256,192},{320,256},{384,320},{448,384},... | collective-permute-start | bytes 98312 | tf_op jit(solution)/shard_map/ppermute | solution.py:72
  71.0 22.8 %collective-permute-start.9 = (f32[2,4,8,128]{3,2,1,0:T(8,128)S(1)}, f32[2,4,8,128]{3,2,1,0:T(8,128)S(1)}, u32[]{:S(2)}, u32[]{:S(2)}) collective-permute-start(f32[2,4,8,128]{3,2,1,0:T(8,128)S(1)} %pad_maximum_fusion.1), channel_id=1, source_target_pairs={{0,64},{64,128},{128,192},{192,256},{256,320},{320,384},{384,448},... | collective-permute-start | bytes 98312 | tf_op jit(solution)/shard_map/ppermute | solution.py:72
  73.1 12.9 %collective-permute-start.11 = (f32[2,4,4,128]{3,2,1,0:T(4,128)S(1)}, f32[2,4,4,128]{3,2,1,0:T(4,128)S(1)}, u32[]{:S(2)}, u32[]{:S(2)}) collective-permute-start(f32[2,4,4,128]{3,2,1,0:T(4,128)S(1)} %get-tuple-element.65), channel_id=1, source_target_pairs={{0,1},{1,2},{2,3},{3,4},{4,5},{5,6},{6,7},{7,8},{8,9},{9,10},{10,1... | collective-permute-start | bytes 49160 | tf_op jit(solution)/shard_map/ppermute | solution.py:69
  76.6 9.4 %collective-permute-start.10 = (f32[2,4,4,128]{3,2,1,0:T(4,128)S(1)}, f32[2,4,4,128]{3,2,1,0:T(4,128)S(1)}, u32[]{:S(2)}, u32[]{:S(2)}) collective-permute-start(f32[2,4,4,128]{3,2,1,0:T(4,128)S(1)} %get-tuple-element.66), channel_id=1, source_target_pairs={{1,64},{2,65},{3,66},{4,67},{5,68},{6,69},{7,70},{8,71},{9,72},{10... | collective-permute-start | bytes 49160 | tf_op jit(solution)/shard_map/ppermute | solution.py:79
  83.3 10.5 %collective-permute-start.8 = (f32[2,4,4,128]{3,2,1,0:T(4,128)S(1)}, f32[2,4,4,128]{3,2,1,0:T(4,128)S(1)}, u32[]{:S(2)}, u32[]{:S(2)}) collective-permute-start(f32[2,4,4,128]{3,2,1,0:T(4,128)S(1)} %get-tuple-element.65), channel_id=1, source_target_pairs={{0,65},{1,66},{2,67},{3,68},{4,69},{5,70},{6,71},{7,72},{8,73},{9,... | collective-permute-start | bytes 49160 | tf_op jit(solution)/shard_map/ppermute | solution.py:79

commit v2 on v1

--- a/solution.py
+++ b/solution.py
@@ -56,44 +56,14 @@
 
 
 def exchange(x, h):
-    nxg = lax.axis_size("gx")
-    nyg = lax.axis_size("gy")
-    nx, ny = x.shape[-3], x.shape[-2]
-
-    def sl(a, lo, hi, axis):
-        return lax.slice_in_dim(a, lo, hi, axis=a.ndim + axis)
-
-    def send(block, dx, dy):
-        if dx == 0:
-            pairs = [(j, j + dy) for j in range(nyg) if 0 <= j + dy < nyg]
-            return lax.ppermute(block, "gy", pairs)
-        if dy == 0:
-            pairs = [(i, i + dx) for i in range(nxg) if 0 <= i + dx < nxg]
-            return lax.ppermute(block, "gx", pairs)
-        pairs = [
-            (i * nyg + j, (i + dx) * nyg + j + dy)
-            for i in range(nxg)
-            for j in range(nyg)
-            if 0 <= i + dx < nxg and 0 <= j + dy < nyg
-        ]
-        return lax.ppermute(block, ("gx", "gy"), pairs)
-
-    x_lo = sl(x, 0, h, -3)
-    x_hi = sl(x, nx - h, nx, -3)
-    y_lo = sl(x, 0, h, -2)
-    y_hi = sl(x, ny - h, ny, -2)
-    from_xm = send(x_hi, 1, 0)
-    from_xp = send(x_lo, -1, 0)
-    from_ym = send(y_hi, 0, 1)
-    from_yp = send(y_lo, 0, -1)
-    from_mm = send(sl(x_hi, ny - h, ny, -2), 1, 1)
-    from_mp = send(sl(x_hi, 0, h, -2), 1, -1)
-    from_pm = send(sl(x_lo, ny - h, ny, -2), -1, 1)
-    from_pp = send(sl(x_lo, 0, h, -2), -1, -1)
-    low = jnp.concatenate([from_mm, from_xm, from_mp], axis=-2)
-    mid = jnp.concatenate([from_ym, x, from_yp], axis=-2)
-    high = jnp.concatenate([from_pm, from_xp, from_pp], axis=-2)
-    return jnp.concatenate([low, mid, high], axis=-3)
+    for axis, dim in (("gx", x.ndim - 3), ("gy", x.ndim - 2)):
+        count, length = lax.axis_size(axis), x.shape[dim]
+        up = [(i, i + 1) for i in range(count - 1)]
+        down = [(i + 1, i) for i in range(count - 1)]
+        before = lax.ppermute(lax.slice_in_dim(x, length - h, length, axis=dim), axis, up)
+        after = lax.ppermute(lax.slice_in_dim(x, 0, h, axis=dim), axis, down)
+        x = jnp.concatenate([before, x, after], axis=dim)
+    return x
 
 
 def inner(a, h):

time: 96.5 us -> 77.4 us (0.80)
  starting transfers between devices: 51.4 us -> 22.4 us
  waiting for transfers between devices: 17.9 us -> 28.9 us
    ppermute x16 -> x8, starting transfers between devices: 51.4 us -> 22.4 us  [the longest x4 12.3 us: exchange(): after = lax.ppermute(lax.slice_in_dim(x, 0, h, axis=dim), axis, down)]
    ppermute x16 -> x8, waiting for transfers between devices: 17.9 us -> 28.9 us  [the longest x4 21.6 us: exchange(): lax.ppermute(lax.slice_in_dim(x, length - h, length, axis=dim), axis, up)]
  transfers between devices with their start and end apart: 16 -> 8, of which waited for: 2 -> 6; matrix products, arithmetic and copies ran while one was open for 1% -> 1% of each run, Pallas kernels for 0% -> 0%
where the time goes in v2:
time: 77.4 us; the launch traced here: 77 us
  waiting for transfers between devices  28.9 us (37%)
  starting transfers between devices  22.4 us (29%)
  other arithmetic  15.2 us (20%)
  local copies, waits for them, and re-layouts  9.13 us (12%)
  between operations  1.29 us (2%)
    ppermute x4, waiting for transfers between devices, exchange(): lax.ppermute(lax.slice_in_dim(x, length - h, length, axis=dim), axis, up)  21.6 us
    ppermute x4, starting transfers between devices, exchange(): after = lax.ppermute(lax.slice_in_dim(x, 0, h, axis=dim), axis, down)  12.3 us
    ppermute x4, starting transfers between devices, exchange(): lax.ppermute(lax.slice_in_dim(x, length - h, length, axis=dim), axis, up)  10.2 us
    ppermute x4, waiting for transfers between devices, exchange(): after = lax.ppermute(lax.slice_in_dim(x, 0, h, axis=dim), axis, down)  7.32 us
    slice x33, local copies, waits for them, and re-layouts, shift(): lax.slice_in_dim(a, step, length, axis=axis)  6.42 us
    mul x8, other arithmetic, apply_operator(): flow = couple[axis] * (value - shift(value, axis, 1))  4.08 us
    reduce_sum x4, other arithmetic, restrict(): jnp.sum(field.reshape(sx // 2, 2, sy // 2, 2, sz), axis=(1, 3))  3.48 us
  transfers between devices with their start and end apart: 8, of which 6 were waited for; matrix products, arithmetic and copies ran while one was open for 1% of the time, Pallas kernels for 0%

profile of v2, /device:TPU:800, one launch (start us, length us, event | category | flops | bytes accessed | tf_op | source)
XLA Modules:
  0.0 77.0 jit_solution(9721368508242583535)
XLA Ops:
  0.7 1.2 %pad_maximum_fusion.1 = f32[3,16,32,128]{3,2,1,0:T(8,128)S(1)} fusion(f32[1,16,32,128]{3,2,1,0:T(8,128)} %bitcast.95, f32[1,16,32,128]{3,2,1,0:T(8,128)} %bitcast.98, f32[1,16,32,128]{3,2,1,0:T(8,128)} %bitcast.101), kind=kLoop, calls=%fused_computation.9 | loop fusion | flops 393216 | bytes 1572864 | tf_op jit(solution)/shard_map/stack | solution.py:75
  2.0 1.9 %collective-permute-start.1 = (f32[3,8,32,128]{3,2,1,0:T(8,128)S(1)}, f32[3,8,32,128]{3,2,1,0:T(8,128)S(1)}, u32[]{:S(2)}, u32[]{:S(2)}) collective-permute-start(f32[3,8,32,128]{3,2,1,0:T(8,128)S(1)} %get-tuple-element.35), channel_id=1, source_target_pairs={{64,0},{128,64},{192,128},{256,192},{320,256},{384,320},{448,384},... | collective-permute-start | bytes 1179656 | tf_op jit(solution)/shard_map/ppermute | solution.py:64
  3.9 2.4 %collective-permute-start = (f32[3,8,32,128]{3,2,1,0:T(8,128)S(1)}, f32[3,8,32,128]{3,2,1,0:T(8,128)S(1)}, u32[]{:S(2)}, u32[]{:S(2)}) collective-permute-start(f32[3,8,32,128]{3,2,1,0:T(8,128)S(1)} %get-tuple-element.34), channel_id=1, source_target_pairs={{0,64},{64,128},{128,192},{192,256},{256,320},{320,384},{384,448},... | collective-permute-start | bytes 1179656 | tf_op jit(solution)/shard_map/ppermute | solution.py:63
  6.3 2.9 %collective-permute-done.1 = f32[3,8,32,128]{3,2,1,0:T(8,128)S(1)} collective-permute-done((f32[3,8,32,128]{3,2,1,0:T(8,128)S(1)}, f32[3,8,32,128]{3,2,1,0:T(8,128)S(1)}, u32[]{:S(2)}, u32[]{:S(2)}) %collective-permute-start.1) | collective-permute-done | bytes 393248 | tf_op jit(solution)/shard_map/ppermute | solution.py:64
  9.2 5.0 %collective-permute-done = f32[3,8,32,128]{3,2,1,0:T(8,128)S(1)} collective-permute-done((f32[3,8,32,128]{3,2,1,0:T(8,128)S(1)}, f32[3,8,32,128]{3,2,1,0:T(8,128)S(1)}, u32[]{:S(2)}, u32[]{:S(2)}) %collective-permute-start) | collective-permute-done | bytes 393248 | tf_op jit(solution)/shard_map/ppermute | solution.py:63
  14.3 5.9 %collective-permute-start.3 = (f32[3,32,8,128]{3,2,1,0:T(8,128)S(1)}, f32[3,32,8,128]{3,2,1,0:T(8,128)S(1)}, u32[]{:S(2)}, u32[]{:S(2)}) collective-permute-start(f32[3,32,8,128]{3,2,1,0:T(8,128)S(1)} %get-tuple-element.27), channel_id=1, source_target_pairs={{1,0},{2,1},{3,2},{4,3},{5,4},{6,5},{7,6},{8,7},{9,8},{10,9},{11,1... | collective-permute-start | bytes 1179656 | tf_op jit(solution)/shard_map/ppermute | solution.py:64
  20.2 1.9 %collective-permute-start.2 = (f32[3,32,8,128]{3,2,1,0:T(8,128)S(1)}, f32[3,32,8,128]{3,2,1,0:T(8,128)S(1)}, u32[]{:S(2)}, u32[]{:S(2)}) collective-permute-start(f32[3,32,8,128]{3,2,1,0:T(8,128)S(1)} %get-tuple-element.26), channel_id=1, source_target_pairs={{0,1},{1,2},{2,3},{3,4},{4,5},{5,6},{6,7},{7,8},{8,9},{9,10},{10,1... | collective-permute-start | bytes 1179656 | tf_op jit(solution)/shard_map/ppermute | solution.py:63
  22.1 4.5 %collective-permute-done.3 = f32[3,32,8,128]{3,2,1,0:T(8,128)S(1)} collective-permute-done((f32[3,32,8,128]{3,2,1,0:T(8,128)S(1)}, f32[3,32,8,128]{3,2,1,0:T(8,128)S(1)}, u32[]{:S(2)}, u32[]{:S(2)}) %collective-permute-start.3) | collective-permute-done | bytes 393248 | tf_op jit(solution)/shard_map/ppermute | solution.py:64
  26.5 7.4 %collective-permute-done.2 = f32[3,32,8,128]{3,2,1,0:T(8,128)S(1)} collective-permute-done((f32[3,32,8,128]{3,2,1,0:T(8,128)S(1)}, f32[3,32,8,128]{3,2,1,0:T(8,128)S(1)}, u32[]{:S(2)}, u32[]{:S(2)}) %collective-permute-start.2) | collective-permute-done | bytes 393248 | tf_op jit(solution)/shard_map/ppermute | solution.py:63
  34.0 0.2 pad_maximum_fusion
  34.2 0.1 slice_bitcast_fusion.3
  34.3 1.0 %fusion.21 = (f32[1,32,48,128]{3,2,1,0:T(8,128)}, f32[32,48,128]{2,1,0:T(8,128)S(1)}, f32[32,48,128]{2,1,0:T(8,128)S(1)}) fusion(f32[3,32,48,128]{3,2,1,0:T(8,128)S(1)} %pad_maximum_fusion), kind=kLoop, calls=%fused_computation.95 | loop fusion | bytes 3932160 | tf_op jit(solution)/shard_map/slice | solution.py:76
  35.4 0.3 slice.355
  35.7 0.3 slice.354
  36.0 0.8 %subtract_multiply_fusion.8 = (f32[32,48,128]{2,1,0:T(8,128)S(1)}, f32[32,48,128]{2,1,0:T(8,128)S(1)}, f32[32,48,128]{2,1,0:T(8,128)S(1)}, f32[32,48,128]{2,1,0:...) fusion(f32[31,48,128]{2,1,0:T(8,128)S(1)} %get-tuple-element.25, ...), kind=kLoop, calls=%fused_computation.22 | loop fusion | flops 4718592 | bytes 10915840 | tf_op jit(solution)/shard_map/mul | solution.py:48
  37.0 0.9 %divide_add_fusion.1 = (f32[32,48,128]{2,1,0:T(8,128)S(1)}, f32[32,48,128]{2,1,0:T(8,128)S(1)}) fusion(f32[32,48,128]{2,1,0:T(8,128)S(1)} %get-tuple-element.22, f32[32,48,127]{2,1,0:T(8,128)S(1)} %bitcast.86, f32[32,48,128]{2,1,0:T(8,128)S(1)} %get-tuple-element.20, f32[32,47,128]{2,1,0:T(8,128)S(1)} %bitcast.85, f32[32,48,128]{2,1,0:T(8,128)S(1)} %get-tuple-element.11, ...), kind=kLoop, calls=%fused_computation.18 | loop fusion | flops 3342336 | bytes 12488704 | tf_op jit(solution)/shard_map/add | solution.py:79
  38.0 0.3 slice.364
  38.3 0.4 subtract_multiply_fusion.5
  38.7 0.5 divide_add_fusion
  39.3 1.0 %slice.367 = f32[31,48,128]{2,1,0:T(8,128)} slice(f32[32,48,128]{2,1,0:T(8,128)S(1)} %divide_add_fusion), slice={[1:32], [0:48], [0:128]} | slice | bytes 1523712 | tf_op jit(solution)/shard_map/slice | solution.py:27
  40.2 1.2 %slice.371 = f32[32,48,127]{2,1,0:T(8,128)} slice(f32[32,48,128]{2,1,0:T(8,128)S(1)} %divide_add_fusion), slice={[0:32], [0:48], [1:128]} | slice | bytes 1560576 | tf_op jit(solution)/shard_map/slice | solution.py:27
  41.4 0.9 %slice.369 = f32[32,47,128]{2,1,0:T(8,128)} slice(f32[32,48,128]{2,1,0:T(8,128)S(1)} %divide_add_fusion), slice={[0:32], [1:48], [0:128]} | slice | bytes 1540096 | tf_op jit(solution)/shard_map/slice | solution.py:27
  42.3 1.7 %reduce_sum.37 = f32[16,24,128]{2,1,0:T(8,128)S(1)} reduce(f32[16,2,24,2,128]{4,3,2,1,0:T(2,128)} %bitcast.93, f32[]{:T(128)} %constant.9.clone.1), dimensions={1,3}, to_apply=%region_1.2 | reduce | flops 147456 | bytes 983044 | tf_op jit(solution)/shard_map/reduce_sum | solution.py:55
  44.1 0.8 %slice.377 = f32[16,24,127]{2,1,0:T(8,128)} slice(f32[16,24,128]{2,1,0:T(8,128)S(1)} %broadcast_multiply_fusion.1), slice={[0:16], [0:24], [1:128]} | slice | bytes 390144 | tf_op jit(solution)/shard_map/slice | solution.py:27
  44.9 0.7 slice.375
  45.6 2.7 %subtract_multiply_fusion.2 = (f32[32,48,128]{2,1,0:T(8,128)S(1)}, f32[32,48,128]{2,1,0:T(8,128)S(1)}, f32[32,48,128]{2,1,0:T(8,128)S(1)}) fusion(f32[32,48,128]{2,1,0:T(8,128)} %copy-done.2, f32[32,48,128]{2,1,0:T(8,128)S(1)} %divide_add_fusion, f32[31,48,128]{2,1,0:T(8,128)} %slice.367, f32[32,48,128]{2,1,0:T(8,128)} %copy-done.1, ...), kind=kLoop, calls=%fused_computation.13 | loop fusion | flops 1179648 | bytes 7817216 | tf_op jit(solution)/shard_map/mul | solution.py:48
  48.3 1.3 %add_subtract_fusion = f32[32,48,128]{2,1,0:T(8,128)} fusion(f32[32,48,128]{2,1,0:T(8,128)S(1)} %get-tuple-element.29, f32[32,48,127]{2,1,0:T(8,128)S(1)} %bitcast.87, f32[32,48,128]{2,1,0:T(8,128)S(1)} %get-tuple-element.30, f32[32,47,128]{2,1,0:T(8,128)S(1)} %bitcast.88, f32[32,48,128]{2,1,0:T(8,128)S(1)} %get-tuple-element.28, ...), kind=kLoop, calls=%fused_computation.10 | loop fusion | flops 1572864 | bytes 7030784 | tf_op jit(solution)/shard_map/sub | solution.py:80
  49.7 1.7 %reduce_sum.36 = f32[16,24,128]{2,1,0:T(8,128)S(1)} reduce(f32[16,2,24,2,128]{4,3,2,1,0:T(2,128)} %bitcast.94, f32[]{:T(128)} %constant.9.clone.1), dimensions={1,3}, to_apply=%region_0.1 | reduce | flops 147456 | bytes 983044 | tf_op jit(solution)/shard_map/reduce_sum | solution.py:55
  51.4 1.2 %fusion.4 = (f32[16,24,128]{2,1,0:T(8,128)S(1)}, f32[16,24,128]{2,1,0:T(8,128)S(1)}, f32[16,24,128]{2,1,0:T(8,128)S(1)}) fusion(f32[15,24,128]{2,1,0:T(8,128)S(1)} %slice-done, f32[16,24,128]{2,1,0:T(8,128)S(1)} %reduce_sum.37, f32[16,24,127]{2,1,0:T(8,128)} %slice.377, f32[16,23,128]{2,1,0:T(8,128)} %slice.375), kind=kLoop, calls=%fused_computation.37 | loop fusion | flops 1032192 | bytes 1354240 | tf_op jit(solution)/shard_map/mul | solution.py:36
  52.6 0.1 multiply_divide_fusion
  52.8 0.1 slice.383
  53.0 0.1 divide_add_fusion.2
  53.2 0.1 slice.391
  53.3 0.5 copy-done.4
  53.9 0.7 slice_subtract_fusion
  54.7 2.6 %collective-permute-start.5 = (f32[2,4,8,128]{3,2,1,0:T(8,128)S(1)}, f32[2,4,8,128]{3,2,1,0:T(8,128)S(1)}, u32[]{:S(2)}, u32[]{:S(2)}) collective-permute-start(f32[2,4,8,128]{3,2,1,0:T(8,128)S(1)} %pad_maximum_fusion.9), channel_id=1, source_target_pairs={{64,0},{128,64},{192,128},{256,192},{320,256},{384,320},{448,384},... | collective-permute-start | bytes 98312 | tf_op jit(solution)/shard_map/ppermute | solution.py:64
  57.3 1.9 %collective-permute-start.4 = (f32[2,4,8,128]{3,2,1,0:T(8,128)S(1)}, f32[2,4,8,128]{3,2,1,0:T(8,128)S(1)}, u32[]{:S(2)}, u32[]{:S(2)}) collective-permute-start(f32[2,4,8,128]{3,2,1,0:T(8,128)S(1)} %pad_maximum_fusion.9), channel_id=1, source_target_pairs={{0,64},{64,128},{128,192},{192,256},{256,320},{320,384},{384,448},... | collective-permute-start | bytes 98312 | tf_op jit(solution)/shard_map/ppermute | solution.py:63
  59.3 4.5 %collective-permute-done.4 = f32[2,4,8,128]{3,2,1,0:T(8,128)S(1)} collective-permute-done((f32[2,4,8,128]{3,2,1,0:T(8,128)S(1)}, f32[2,4,8,128]{3,2,1,0:T(8,128)S(1)}, u32[]{:S(2)}, u32[]{:S(2)}) %collective-permute-start.4) | collective-permute-done | bytes 32800 | tf_op jit(solution)/shard_map/ppermute | solution.py:63
  63.8 1.9 %collective-permute-start.7 = (f32[2,12,4,128]{3,2,1,0:T(4,128)S(1)}, f32[2,12,4,128]{3,2,1,0:T(4,128)S(1)}, u32[]{:S(2)}, u32[]{:S(2)}) collective-permute-start(f32[2,12,4,128]{3,2,1,0:T(4,128)S(1)} %get-tuple-element.62), channel_id=1, source_target_pairs={{1,0},{2,1},{3,2},{4,3},{5,4},{6,5},{7,6},{8,7},{9,8},{10,9},{11,1... | collective-permute-start | bytes 147464 | tf_op jit(solution)/shard_map/ppermute | solution.py:64
  65.7 3.9 %collective-permute-start.6 = (f32[2,12,4,128]{3,2,1,0:T(4,128)S(1)}, f32[2,12,4,128]{3,2,1,0:T(4,128)S(1)}, u32[]{:S(2)}, u32[]{:S(2)}) collective-permute-start(f32[2,12,4,128]{3,2,1,0:T(4,128)S(1)} %get-tuple-element.61), channel_id=1, source_target_pairs={{0,1},{1,2},{2,3},{3,4},{4,5},{5,6},{6,7},{7,8},{8,9},{9,10},{10,1... | collective-permute-start | bytes 147464 | tf_op jit(solution)/shard_map/ppermute | solution.py:63
  69.7 0.7 slice.366
  70.4 4.6 %collective-permute-done.6 = f32[2,12,4,128]{3,2,1,0:T(4,128)S(1)} collective-permute-done((f32[2,12,4,128]{3,2,1,0:T(4,128)S(1)}, f32[2,12,4,128]{3,2,1,0:T(4,128)S(1)}, u32[]{:S(2)}, u32[]{:S(2)}) %collective-permute-start.6) | collective-permute-done | bytes 49184 | tf_op jit(solution)/shard_map/ppermute | solution.py:63
  75.1 0.1 slice.406
  75.2 0.1 fusion.9
  75.3 0.1 multiply_divide_fusion.1
  75.6 0.1 divide_add_fusion.4
  75.9 0.1 divide_add_fusion.3
  76.3 0.7 slice_add_fusion
  (68 shorter events, 1.6 us)
Async XLA Ops:
  0.6 13.6 %copy-start.5 = (f32[16,32,128]{2,1,0:T(8,128)S(1)}, f32[16,32,128]{2,1,0:T(8,128)}, u32[]{:S(2)}) copy-start(f32[16,32,128]{2,1,0:T(8,128)} %param.4) | copy-start | bytes 786436
  0.6 13.6 %copy-start.6 = (f32[16,32,128]{2,1,0:T(8,128)S(1)}, f32[16,32,128]{2,1,0:T(8,128)}, u32[]{:S(2)}) copy-start(f32[16,32,128]{2,1,0:T(8,128)} %param.3) | copy-start | bytes 786436
  0.7 13.6 %copy-start.7 = (f32[16,32,128]{2,1,0:T(8,128)S(1)}, f32[16,32,128]{2,1,0:T(8,128)}, u32[]{:S(2)}) copy-start(f32[16,32,128]{2,1,0:T(8,128)} %param.5) | copy-start | bytes 786436
  2.0 7.2 %collective-permute-start.1 = (f32[3,8,32,128]{3,2,1,0:T(8,128)S(1)}, f32[3,8,32,128]{3,2,1,0:T(8,128)S(1)}, u32[]{:S(2)}, u32[]{:S(2)}) collective-permute-start(f32[3,8,32,128]{3,2,1,0:T(8,128)S(1)} %get-tuple-element.35), channel_id=1, source_target_pairs={{64,0},{128,64},{192,128},{256,192},{320,256},{384,320},{448,384},... | collective-permute-start | bytes 1179656 | tf_op jit(solution)/shard_map/ppermute | solution.py:64
  3.9 10.3 %collective-permute-start = (f32[3,8,32,128]{3,2,1,0:T(8,128)S(1)}, f32[3,8,32,128]{3,2,1,0:T(8,128)S(1)}, u32[]{:S(2)}, u32[]{:S(2)}) collective-permute-start(f32[3,8,32,128]{3,2,1,0:T(8,128)S(1)} %get-tuple-element.34), channel_id=1, source_target_pairs={{0,64},{64,128},{128,192},{192,256},{256,320},{320,384},{384,448},... | collective-permute-start | bytes 1179656 | tf_op jit(solution)/shard_map/ppermute | solution.py:63
  14.3 12.3 %collective-permute-start.3 = (f32[3,32,8,128]{3,2,1,0:T(8,128)S(1)}, f32[3,32,8,128]{3,2,1,0:T(8,128)S(1)}, u32[]{:S(2)}, u32[]{:S(2)}) collective-permute-start(f32[3,32,8,128]{3,2,1,0:T(8,128)S(1)} %get-tuple-element.27), channel_id=1, source_target_pairs={{1,0},{2,1},{3,2},{4,3},{5,4},{6,5},{7,6},{8,7},{9,8},{10,9},{11,1... | collective-permute-start | bytes 1179656 | tf_op jit(solution)/shard_map/ppermute | solution.py:64
  20.2 13.8 %collective-permute-start.2 = (f32[3,32,8,128]{3,2,1,0:T(8,128)S(1)}, f32[3,32,8,128]{3,2,1,0:T(8,128)S(1)}, u32[]{:S(2)}, u32[]{:S(2)}) collective-permute-start(f32[3,32,8,128]{3,2,1,0:T(8,128)S(1)} %get-tuple-element.26), channel_id=1, source_target_pairs={{0,1},{1,2},{2,3},{3,4},{4,5},{5,6},{6,7},{7,8},{8,9},{9,10},{10,1... | collective-permute-start | bytes 1179656 | tf_op jit(solution)/shard_map/ppermute | solution.py:63
  36.8 1.5 %copy-start = (f32[32,48,128]{2,1,0:T(8,128)}, f32[32,48,128]{2,1,0:T(8,128)S(1)}, u32[]{:S(2)}) copy-start(f32[32,48,128]{2,1,0:T(8,128)S(1)} %get-tuple-element.21) | copy-start | bytes 2359300
  36.8 1.5 %copy-start.1 = (f32[32,48,128]{2,1,0:T(8,128)}, f32[32,48,128]{2,1,0:T(8,128)S(1)}, u32[]{:S(2)}) copy-start(f32[32,48,128]{2,1,0:T(8,128)S(1)} %get-tuple-element.23) | copy-start | bytes 2359300
  36.9 1.5 %copy-start.2 = (f32[32,48,128]{2,1,0:T(8,128)}, f32[32,48,128]{2,1,0:T(8,128)S(1)}, u32[]{:S(2)}) copy-start(f32[32,48,128]{2,1,0:T(8,128)S(1)} %get-tuple-element.12) | copy-start | bytes 2359300
  44.1 4.2 %copy-start.3 = (f32[16,24,128]{2,1,0:T(8,128)}, f32[16,24,128]{2,1,0:T(8,128)S(1)}, u32[]{:S(2)}) copy-start(f32[16,24,128]{2,1,0:T(8,128)S(1)} %broadcast_multiply_fusion.1) | copy-start | bytes 589828
  48.3 3.0 %slice-start = ((f32[16,24,128]{2,1,0:T(8,128)}), f32[15,24,128]{2,1,0:T(8,128)S(1)}, s32[]{:S(2)}) async-start(f32[16,24,128]{2,1,0:T(8,128)} %copy-done.3), calls=%async_computation | async-start | bytes 368640 | tf_op jit(solution)/shard_map/slice | solution.py:27
  52.9 0.9 %copy-start.4 = (f32[16,24,128]{2,1,0:T(8,128)S(1)}, f32[16,24,128]{2,1,0:T(8,128)}, u32[]{:S(2)}) copy-start(f32[16,24,128]{2,1,0:T(8,128)} %copy-done.3) | copy-start | bytes 589828
  54.7 4.5 %collective-permute-start.5 = (f32[2,4,8,128]{3,2,1,0:T(8,128)S(1)}, f32[2,4,8,128]{3,2,1,0:T(8,128)S(1)}, u32[]{:S(2)}, u32[]{:S(2)}) collective-permute-start(f32[2,4,8,128]{3,2,1,0:T(8,128)S(1)} %pad_maximum_fusion.9), channel_id=1, source_target_pairs={{64,0},{128,64},{192,128},{256,192},{320,256},{384,320},{448,384},... | collective-permute-start | bytes 98312 | tf_op jit(solution)/shard_map/ppermute | solution.py:64
  57.3 6.4 %collective-permute-start.4 = (f32[2,4,8,128]{3,2,1,0:T(8,128)S(1)}, f32[2,4,8,128]{3,2,1,0:T(8,128)S(1)}, u32[]{:S(2)}, u32[]{:S(2)}) collective-permute-start(f32[2,4,8,128]{3,2,1,0:T(8,128)S(1)} %pad_maximum_fusion.9), channel_id=1, source_target_pairs={{0,64},{64,128},{128,192},{192,256},{256,320},{320,384},{384,448},... | collective-permute-start | bytes 98312 | tf_op jit(solution)/shard_map/ppermute | solution.py:63
  63.8 6.6 %collective-permute-start.7 = (f32[2,12,4,128]{3,2,1,0:T(4,128)S(1)}, f32[2,12,4,128]{3,2,1,0:T(4,128)S(1)}, u32[]{:S(2)}, u32[]{:S(2)}) collective-permute-start(f32[2,12,4,128]{3,2,1,0:T(4,128)S(1)} %get-tuple-element.62), channel_id=1, source_target_pairs={{1,0},{2,1},{3,2},{4,3},{5,4},{6,5},{7,6},{8,7},{9,8},{10,9},{11,1... | collective-permute-start | bytes 147464 | tf_op jit(solution)/shard_map/ppermute | solution.py:64
  65.7 9.3 %collective-permute-start.6 = (f32[2,12,4,128]{3,2,1,0:T(4,128)S(1)}, f32[2,12,4,128]{3,2,1,0:T(4,128)S(1)}, u32[]{:S(2)}, u32[]{:S(2)}) collective-permute-start(f32[2,12,4,128]{3,2,1,0:T(4,128)S(1)} %get-tuple-element.61), channel_id=1, source_target_pairs={{0,1},{1,2},{2,3},{3,4},{4,5},{5,6},{6,7},{7,8},{8,9},{9,10},{10,1... | collective-permute-start | bytes 147464 | tf_op jit(solution)/shard_map/ppermute | solution.py:63

commit v3 on v2

--- a/solution.py
+++ b/solution.py
@@ -1,6 +1,8 @@
 import jax
 import jax.numpy as jnp
 from jax import lax
+from jax.experimental import pallas as pl
+from jax.experimental.pallas import tpu as pltpu
 from jax.sharding import PartitionSpec as P
 
 SWEEPS = 2
@@ -70,36 +72,115 @@
     return a[h:a.shape[0] - h, h:a.shape[1] - h]
 
 
-def body(pressure_init, source, permeability):
+def k_shift(a, axis, step):
+    n = a.shape[axis]
+    if axis == 0:
+        if step > 0:
+            return jnp.concatenate([a[step:], a[:step]], axis=0)
+        return jnp.concatenate([a[n + step:], a[:n + step]], axis=0)
+    return pltpu.roll(a, (-step) % n, axis)
+
+
+def k_coefficients(perm, scale):
+    couple = []
+    last_z = lax.broadcasted_iota(jnp.int32, perm.shape, 2) == perm.shape[2] - 1
+    for axis in range(3):
+        c = harmonic(k_shift(perm, axis, 1), perm)
+        if axis < 2:
+            c = scale * c
+        else:
+            c = jnp.where(last_z, 0.0, c)
+        couple.append(c)
+    diagonal = STORE
+    for axis in range(3):
+        diagonal = diagonal + (k_shift(couple[axis], axis, -1) + couple[axis])
+    return couple, diagonal
+
+
+def k_apply(value, parts):
+    couple, diagonal = parts
+    out = STORE * value
+    for axis in range(3):
+        flow = couple[axis] * (value - k_shift(value, axis, 1))
+        out = out + (flow - k_shift(flow, axis, -1))
+    return out
+
+
+def k_restrict(ref, lo, nx, ny):
+    def at(dx, dy):
+        return ref[pl.ds(lo + dx, nx, stride=2), pl.ds(lo + dy, ny, stride=2), :]
+    return 0.25 * ((at(0, 0) + at(1, 0)) + (at(0, 1) + at(1, 1)))
+
+
+def fine_kernel(region, p_out, mid_out, rhs2_out, perm2_out, k0_scr, r0_scr, k1_scr, r1_scr):
     h0 = FINE_HALO
-    region = exchange(jnp.stack([permeability, pressure_init, source]), h0)
-    perm0, pressure, src = region[0], region[1], region[2]
-    parts0 = coefficients(perm0, 1.0)
+    h1 = h0 // 2
+    perm0 = region[0]
+    pressure = region[1]
+    src = region[2]
+    parts0 = k_coefficients(perm0, 1.0)
     for step in range(SWEEPS):
-        pressure = pressure + OMEGA * (src - apply_operator(pressure, parts0)) / parts0[1]
-    resid0 = src - apply_operator(pressure, parts0)
-    pressure_out = inner(pressure, h0)
-
-    h1 = h0 // 2
-    rhs_mid = restrict(resid0)
-    perm_mid = restrict(perm0)
-    parts1 = coefficients(perm_mid, 0.25)
+        pressure = pressure + OMEGA * (src - k_apply(pressure, parts0)) / parts0[1]
+    resid0 = src - k_apply(pressure, parts0)
+    p_out[...] = inner(pressure, h0)
+    k0_scr[...] = perm0
+    r0_scr[...] = resid0
+    cx, cy = r0_scr.shape[0] // 2, r0_scr.shape[1] // 2
+    rhs_mid = k_restrict(r0_scr, 0, cx, cy)
+    perm_mid = k_restrict(k0_scr, 0, cx, cy)
+    parts1 = k_coefficients(perm_mid, 0.25)
     value = OMEGA * rhs_mid / parts1[1]
     for step in range(SWEEPS - 1):
-        value = value + OMEGA * (rhs_mid - apply_operator(value, parts1)) / parts1[1]
-    resid1 = rhs_mid - apply_operator(value, parts1)
-    correction_mid = inner(value, h1)
+        value = value + OMEGA * (rhs_mid - k_apply(value, parts1)) / parts1[1]
+    resid1 = rhs_mid - k_apply(value, parts1)
+    k1_scr[...] = perm_mid
+    mx, my = mid_out.shape[0], mid_out.shape[1]
+    r1_scr[...] = value
+    mid_out[...] = r1_scr[pl.ds(h1, mx), pl.ds(h1, my), :]
+    r1_scr[...] = resid1
+    rhs2_out[...] = k_restrict(r1_scr, h1, mx // 2, my // 2)
+    perm2_out[...] = k_restrict(k1_scr, h1, mx // 2, my // 2)
 
+
+def coarse_kernel(region, out, scr):
     h2 = COARSE_HALO
-    rhs_coarse = restrict(inner(resid1, h1))
-    perm_coarse = restrict(inner(perm_mid, h1))
-    region2 = exchange(jnp.stack([perm_coarse, rhs_coarse]), h2)
-    perm2, rhs2 = region2[0], region2[1]
-    parts2 = coefficients(perm2, 0.0625)
+    perm2 = region[0]
+    rhs2 = region[1]
+    parts2 = k_coefficients(perm2, 0.0625)
     value = OMEGA * rhs2 / parts2[1]
     for step in range(COARSE - 1):
-        value = value + OMEGA * (rhs2 - apply_operator(value, parts2)) / parts2[1]
-    correction_coarse = inner(value, h2)
+        value = value + OMEGA * (rhs2 - k_apply(value, parts2)) / parts2[1]
+    scr[...] = value
+    out[...] = scr[pl.ds(h2, out.shape[0]), pl.ds(h2, out.shape[1]), :]
+
+
+def vmem_call(kernel, outs, scratch, *args):
+    return pl.pallas_call(
+        kernel,
+        out_shape=[jax.ShapeDtypeStruct(s, jnp.float32) for s in outs],
+        in_specs=[pl.BlockSpec(memory_space=pltpu.VMEM) for a in args],
+        out_specs=[pl.BlockSpec(memory_space=pltpu.VMEM) for s in outs],
+        scratch_shapes=[pltpu.VMEM(s, jnp.float32) for s in scratch],
+        compiler_params=pltpu.CompilerParams(vmem_limit_bytes=48 * 1024 * 1024),
+    )(*args)
+
+
+def body(pressure_init, source, permeability):
+    h0, h2 = FINE_HALO, COARSE_HALO
+    nx, ny, nz = pressure_init.shape
+    region = exchange(jnp.stack([permeability, pressure_init, source]), h0)
+    px, py = nx + 2 * h0, ny + 2 * h0
+    mid = (nx // 2, ny // 2, nz)
+    coarse = (nx // 4, ny // 4, nz)
+    pressure_out, correction_mid, rhs_coarse, perm_coarse = vmem_call(
+        fine_kernel,
+        [(nx, ny, nz), mid, coarse, coarse],
+        [(px, py, nz), (px, py, nz), (px // 2, py // 2, nz), (px // 2, py // 2, nz)],
+        region,
+    )
+    region2 = exchange(jnp.stack([perm_coarse, rhs_coarse]), h2)
+    c2x, c2y = coarse[0] + 2 * h2, coarse[1] + 2 * h2
+    (correction_coarse,) = vmem_call(coarse_kernel, [coarse], [(c2x, c2y, nz)], region2)
     return (pressure_out, correction_mid, correction_coarse)
 
 

time: 77.4 us -> 60.7 us (0.78)
  the two profiles are of different devices: /device:TPU:800 before, /device:TPU:486 now
where the time goes in v3:
time: 60.7 us; the launch traced here: 60.4 us
  waiting for transfers between devices  28.6 us (47%)
  starting transfers between devices  24.3 us (40%)
  Pallas kernels  5.18 us (9%)
  other arithmetic  1.5 us (2%)
  between operations  0.77 us (1%)
    ppermute x4, waiting for transfers between devices, exchange(): after = lax.ppermute(lax.slice_in_dim(x, 0, h, axis=dim), axis, down)  14.4 us
    ppermute x4, waiting for transfers between devices, exchange(): lax.ppermute(lax.slice_in_dim(x, length - h, length, axis=dim), axis, up)  14.2 us
    ppermute x4, starting transfers between devices, exchange(): after = lax.ppermute(lax.slice_in_dim(x, 0, h, axis=dim), axis, down)  12.8 us
    ppermute x4, starting transfers between devices, exchange(): lax.ppermute(lax.slice_in_dim(x, length - h, length, axis=dim), axis, up)  11.5 us
    pallas_call x2, Pallas kernels, vmem_call(): pl.pallas_call(kernel, out_shape=[jax.ShapeDtypeStruct(s, jnp.float32) fo...  5.18 us
    another operation x1, other arithmetic, body(): region = exchange(jnp.stack([permeability, pressure_init, source]), h0)  1.23 us
  transfers between devices with their start and end apart: 8, of which 7 were waited for; matrix products, arithmetic and copies ran while one was open for 0% of the time, Pallas kernels for 0%

profile of v3, /device:TPU:486, one launch (start us, length us, event | category | flops | bytes accessed | tf_op | source)
XLA Modules:
  0.0 60.4 jit_solution(8363438238998615265)
XLA Ops:
  0.6 0.0 copy-start.2
  0.6 0.0 copy-start
  0.7 0.0 copy-start.1
  0.7 1.2 %pad_maximum_fusion.1 = f32[3,16,32,128]{3,2,1,0:T(8,128)S(1)} fusion(f32[1,16,32,128]{3,2,1,0:T(8,128)} %bitcast.11, f32[1,16,32,128]{3,2,1,0:T(8,128)} %bitcast.14, f32[1,16,32,128]{3,2,1,0:T(8,128)} %bitcast.17), kind=kLoop, calls=%fused_computation.1 | loop fusion | flops 393216 | bytes 1572864 | tf_op jit(solution)/shard_map/stack | solution.py:171
  1.9 0.1 fusion
  2.0 1.9 %collective-permute-start = (f32[3,8,32,128]{3,2,1,0:T(8,128)S(1)}, f32[3,8,32,128]{3,2,1,0:T(8,128)S(1)}, u32[]{:S(2)}, u32[]{:S(2)}) collective-permute-start(f32[3,8,32,128]{3,2,1,0:T(8,128)S(1)} %get-tuple-element.13), channel_id=1, source_target_pairs={{0,64},{64,128},{128,192},{192,256},{256,320},{320,384},{384,448},... | collective-permute-start | bytes 1179656 | tf_op jit(solution)/shard_map/ppermute | solution.py:65
  3.9 4.9 %collective-permute-start.1 = (f32[3,8,32,128]{3,2,1,0:T(8,128)S(1)}, f32[3,8,32,128]{3,2,1,0:T(8,128)S(1)}, u32[]{:S(2)}, u32[]{:S(2)}) collective-permute-start(f32[3,8,32,128]{3,2,1,0:T(8,128)S(1)} %get-tuple-element.14), channel_id=1, source_target_pairs={{64,0},{128,64},{192,128},{256,192},{320,256},{384,320},{448,384},... | collective-permute-start | bytes 1179656 | tf_op jit(solution)/shard_map/ppermute | solution.py:66
  8.8 3.5 %collective-permute-done = f32[3,8,32,128]{3,2,1,0:T(8,128)S(1)} collective-permute-done((f32[3,8,32,128]{3,2,1,0:T(8,128)S(1)}, f32[3,8,32,128]{3,2,1,0:T(8,128)S(1)}, u32[]{:S(2)}, u32[]{:S(2)}) %collective-permute-start) | collective-permute-done | bytes 393248 | tf_op jit(solution)/shard_map/ppermute | solution.py:65
  12.3 1.8 %collective-permute-done.1 = f32[3,8,32,128]{3,2,1,0:T(8,128)S(1)} collective-permute-done((f32[3,8,32,128]{3,2,1,0:T(8,128)S(1)}, f32[3,8,32,128]{3,2,1,0:T(8,128)S(1)}, u32[]{:S(2)}, u32[]{:S(2)}) %collective-permute-start.1) | collective-permute-done | bytes 393248 | tf_op jit(solution)/shard_map/ppermute | solution.py:66
  14.0 0.0 copy-done.2
  14.0 0.0 copy-done
  14.0 0.0 copy-done.1
  14.0 0.1 pad_maximum_fusion.6
  14.1 5.4 %collective-permute-start.2 = (f32[3,32,8,128]{3,2,1,0:T(8,128)S(1)}, f32[3,32,8,128]{3,2,1,0:T(8,128)S(1)}, u32[]{:S(2)}, u32[]{:S(2)}) collective-permute-start(f32[3,32,8,128]{3,2,1,0:T(8,128)S(1)} %get-tuple-element.11), channel_id=1, source_target_pairs={{0,1},{1,2},{2,3},{3,4},{4,5},{5,6},{6,7},{7,8},{8,9},{9,10},{10,1... | collective-permute-start | bytes 1179656 | tf_op jit(solution)/shard_map/ppermute | solution.py:65
  19.5 1.9 %collective-permute-start.3 = (f32[3,32,8,128]{3,2,1,0:T(8,128)S(1)}, f32[3,32,8,128]{3,2,1,0:T(8,128)S(1)}, u32[]{:S(2)}, u32[]{:S(2)}) collective-permute-start(f32[3,32,8,128]{3,2,1,0:T(8,128)S(1)} %get-tuple-element.12), channel_id=1, source_target_pairs={{1,0},{2,1},{3,2},{4,3},{5,4},{6,5},{7,6},{8,7},{9,8},{10,9},{11,1... | collective-permute-start | bytes 1179656 | tf_op jit(solution)/shard_map/ppermute | solution.py:66
  21.4 6.3 %collective-permute-done.2 = f32[3,32,8,128]{3,2,1,0:T(8,128)S(1)} collective-permute-done((f32[3,32,8,128]{3,2,1,0:T(8,128)S(1)}, f32[3,32,8,128]{3,2,1,0:T(8,128)S(1)}, u32[]{:S(2)}, u32[]{:S(2)}) %collective-permute-start.2) | collective-permute-done | bytes 393248 | tf_op jit(solution)/shard_map/ppermute | solution.py:65
  27.8 7.4 %collective-permute-done.3 = f32[3,32,8,128]{3,2,1,0:T(8,128)S(1)} collective-permute-done((f32[3,32,8,128]{3,2,1,0:T(8,128)S(1)}, f32[3,32,8,128]{3,2,1,0:T(8,128)S(1)}, u32[]{:S(2)}, u32[]{:S(2)}) %collective-permute-start.3) | collective-permute-done | bytes 393248 | tf_op jit(solution)/shard_map/ppermute | solution.py:66
  35.2 0.2 pad_maximum_fusion.region
  35.4 4.0 %shard_map.58 = (f32[16,32,128]{2,1,0:T(8,128)}, f32[8,16,128]{2,1,0:T(8,128)}, f32[4,8,128]{2,1,0:T(8,128)S(1)}, f32[4,8,128]{2,1,0:T(8,128)S(1)}) custom-call(f32[3,32,48,128]{3,2,1,0:T(8,128)S(1)} %pad_maximum_fusion.region), custom_call_target="tpu_custom_call" | custom-call | tf_op jit(solution)/shard_map/pallas_call | solution.py:158
  39.4 2.1 %collective-permute-start.5 = (f32[2,4,8,128]{3,2,1,0:T(8,128)S(1)}, f32[2,4,8,128]{3,2,1,0:T(8,128)S(1)}, u32[]{:S(2)}, u32[]{:S(2)}) collective-permute-start(f32[2,4,8,128]{3,2,1,0:T(8,128)S(1)} %pad_maximum_fusion.9), channel_id=1, source_target_pairs={{64,0},{128,64},{192,128},{256,192},{320,256},{384,320},{448,384},... | collective-permute-start | bytes 98312 | tf_op jit(solution)/shard_map/ppermute | solution.py:66
  41.4 2.3 %collective-permute-start.4 = (f32[2,4,8,128]{3,2,1,0:T(8,128)S(1)}, f32[2,4,8,128]{3,2,1,0:T(8,128)S(1)}, u32[]{:S(2)}, u32[]{:S(2)}) collective-permute-start(f32[2,4,8,128]{3,2,1,0:T(8,128)S(1)} %pad_maximum_fusion.9), channel_id=1, source_target_pairs={{0,64},{64,128},{128,192},{192,256},{256,320},{320,384},{384,448},... | collective-permute-start | bytes 98312 | tf_op jit(solution)/shard_map/ppermute | solution.py:65
  43.7 0.0 collective-permute-done.5
  43.7 4.2 %collective-permute-done.4 = f32[2,4,8,128]{3,2,1,0:T(8,128)S(1)} collective-permute-done((f32[2,4,8,128]{3,2,1,0:T(8,128)S(1)}, f32[2,4,8,128]{3,2,1,0:T(8,128)S(1)}, u32[]{:S(2)}, u32[]{:S(2)}) %collective-permute-start.4) | collective-permute-done | bytes 32800 | tf_op jit(solution)/shard_map/ppermute | solution.py:65
  47.9 1.9 %collective-permute-start.6 = (f32[2,12,4,128]{3,2,1,0:T(4,128)S(1)}, f32[2,12,4,128]{3,2,1,0:T(4,128)S(1)}, u32[]{:S(2)}, u32[]{:S(2)}) collective-permute-start(f32[2,12,4,128]{3,2,1,0:T(4,128)S(1)} %get-tuple-element.15), channel_id=1, source_target_pairs={{0,1},{1,2},{2,3},{3,4},{4,5},{5,6},{6,7},{7,8},{8,9},{9,10},{10,1... | collective-permute-start | bytes 147464 | tf_op jit(solution)/shard_map/ppermute | solution.py:65
  49.8 3.9 %collective-permute-start.7 = (f32[2,12,4,128]{3,2,1,0:T(4,128)S(1)}, f32[2,12,4,128]{3,2,1,0:T(4,128)S(1)}, u32[]{:S(2)}, u32[]{:S(2)}) collective-permute-start(f32[2,12,4,128]{3,2,1,0:T(4,128)S(1)} %get-tuple-element.16), channel_id=1, source_target_pairs={{1,0},{2,1},{3,2},{4,3},{5,4},{6,5},{7,6},{8,7},{9,8},{10,9},{11,1... | collective-permute-start | bytes 147464 | tf_op jit(solution)/shard_map/ppermute | solution.py:66
  53.8 0.1 collective-permute-done.6
  53.9 5.2 %collective-permute-done.7 = f32[2,12,4,128]{3,2,1,0:T(4,128)S(1)} collective-permute-done((f32[2,12,4,128]{3,2,1,0:T(4,128)S(1)}, f32[2,12,4,128]{3,2,1,0:T(4,128)S(1)}, u32[]{:S(2)}, u32[]{:S(2)}) %collective-permute-start.7) | collective-permute-done | bytes 49184 | tf_op jit(solution)/shard_map/ppermute | solution.py:66
  59.2 1.2 %shard_map.59 = f32[4,8,128]{2,1,0:T(8,128)} custom-call(f32[2,12,16,128]{3,2,1,0:T(8,128)S(1)} %pad_maximum_fusion.7.region), custom_call_target="tpu_custom_call" | custom-call | tf_op jit(solution)/shard_map/pallas_call | solution.py:158
  (4 shorter events, 0.1 us)
Async XLA Ops:
  0.6 13.4 %copy-start.2 = (f32[16,32,128]{2,1,0:T(8,128)S(1)}, f32[16,32,128]{2,1,0:T(8,128)}, u32[]{:S(2)}) copy-start(f32[16,32,128]{2,1,0:T(8,128)} %param.5) | copy-start | bytes 786436
  0.6 13.4 %copy-start = (f32[16,32,128]{2,1,0:T(8,128)S(1)}, f32[16,32,128]{2,1,0:T(8,128)}, u32[]{:S(2)}) copy-start(f32[16,32,128]{2,1,0:T(8,128)} %param.4) | copy-start | bytes 786436
  0.7 13.4 %copy-start.1 = (f32[16,32,128]{2,1,0:T(8,128)S(1)}, f32[16,32,128]{2,1,0:T(8,128)}, u32[]{:S(2)}) copy-start(f32[16,32,128]{2,1,0:T(8,128)} %param.3) | copy-start | bytes 786436
  2.0 10.3 %collective-permute-start = (f32[3,8,32,128]{3,2,1,0:T(8,128)S(1)}, f32[3,8,32,128]{3,2,1,0:T(8,128)S(1)}, u32[]{:S(2)}, u32[]{:S(2)}) collective-permute-start(f32[3,8,32,128]{3,2,1,0:T(8,128)S(1)} %get-tuple-element.13), channel_id=1, source_target_pairs={{0,64},{64,128},{128,192},{192,256},{256,320},{320,384},{384,448},... | collective-permute-start | bytes 1179656 | tf_op jit(solution)/shard_map/ppermute | solution.py:65
  3.9 10.1 %collective-permute-start.1 = (f32[3,8,32,128]{3,2,1,0:T(8,128)S(1)}, f32[3,8,32,128]{3,2,1,0:T(8,128)S(1)}, u32[]{:S(2)}, u32[]{:S(2)}) collective-permute-start(f32[3,8,32,128]{3,2,1,0:T(8,128)S(1)} %get-tuple-element.14), channel_id=1, source_target_pairs={{64,0},{128,64},{192,128},{256,192},{320,256},{384,320},{448,384},... | collective-permute-start | bytes 1179656 | tf_op jit(solution)/shard_map/ppermute | solution.py:66
  14.1 13.7 %collective-permute-start.2 = (f32[3,32,8,128]{3,2,1,0:T(8,128)S(1)}, f32[3,32,8,128]{3,2,1,0:T(8,128)S(1)}, u32[]{:S(2)}, u32[]{:S(2)}) collective-permute-start(f32[3,32,8,128]{3,2,1,0:T(8,128)S(1)} %get-tuple-element.11), channel_id=1, source_target_pairs={{0,1},{1,2},{2,3},{3,4},{4,5},{5,6},{6,7},{7,8},{8,9},{9,10},{10,1... | collective-permute-start | bytes 1179656 | tf_op jit(solution)/shard_map/ppermute | solution.py:65
  19.5 15.7 %collective-permute-start.3 = (f32[3,32,8,128]{3,2,1,0:T(8,128)S(1)}, f32[3,32,8,128]{3,2,1,0:T(8,128)S(1)}, u32[]{:S(2)}, u32[]{:S(2)}) collective-permute-start(f32[3,32,8,128]{3,2,1,0:T(8,128)S(1)} %get-tuple-element.12), channel_id=1, source_target_pairs={{1,0},{2,1},{3,2},{4,3},{5,4},{6,5},{7,6},{8,7},{9,8},{10,9},{11,1... | collective-permute-start | bytes 1179656 | tf_op jit(solution)/shard_map/ppermute | solution.py:66
  39.4 4.3 %collective-permute-start.5 = (f32[2,4,8,128]{3,2,1,0:T(8,128)S(1)}, f32[2,4,8,128]{3,2,1,0:T(8,128)S(1)}, u32[]{:S(2)}, u32[]{:S(2)}) collective-permute-start(f32[2,4,8,128]{3,2,1,0:T(8,128)S(1)} %pad_maximum_fusion.9), channel_id=1, source_target_pairs={{64,0},{128,64},{192,128},{256,192},{320,256},{384,320},{448,384},... | collective-permute-start | bytes 98312 | tf_op jit(solution)/shard_map/ppermute | solution.py:66
  41.4 6.4 %collective-permute-start.4 = (f32[2,4,8,128]{3,2,1,0:T(8,128)S(1)}, f32[2,4,8,128]{3,2,1,0:T(8,128)S(1)}, u32[]{:S(2)}, u32[]{:S(2)}) collective-permute-start(f32[2,4,8,128]{3,2,1,0:T(8,128)S(1)} %pad_maximum_fusion.9), channel_id=1, source_target_pairs={{0,64},{64,128},{128,192},{192,256},{256,320},{320,384},{384,448},... | collective-permute-start | bytes 98312 | tf_op jit(solution)/shard_map/ppermute | solution.py:65
  47.9 6.0 %collective-permute-start.6 = (f32[2,12,4,128]{3,2,1,0:T(4,128)S(1)}, f32[2,12,4,128]{3,2,1,0:T(4,128)S(1)}, u32[]{:S(2)}, u32[]{:S(2)}) collective-permute-start(f32[2,12,4,128]{3,2,1,0:T(4,128)S(1)} %get-tuple-element.15), channel_id=1, source_target_pairs={{0,1},{1,2},{2,3},{3,4},{4,5},{5,6},{6,7},{7,8},{8,9},{9,10},{10,1... | collective-permute-start | bytes 147464 | tf_op jit(solution)/shard_map/ppermute | solution.py:65
  49.8 9.3 %collective-permute-start.7 = (f32[2,12,4,128]{3,2,1,0:T(4,128)S(1)}, f32[2,12,4,128]{3,2,1,0:T(4,128)S(1)}, u32[]{:S(2)}, u32[]{:S(2)}) collective-permute-start(f32[2,12,4,128]{3,2,1,0:T(4,128)S(1)} %get-tuple-element.16), channel_id=1, source_target_pairs={{1,0},{2,1},{3,2},{4,3},{5,4},{6,5},{7,6},{8,7},{9,8},{10,9},{11,1... | collective-permute-start | bytes 147464 | tf_op jit(solution)/shard_map/ppermute | solution.py:66

commit v4 on v3

--- a/solution.py
+++ b/solution.py
@@ -58,7 +58,7 @@
 
 
 def exchange(x, h):
-    for axis, dim in (("gx", x.ndim - 3), ("gy", x.ndim - 2)):
+    for axis, dim in (("gy", x.ndim - 2), ("gx", x.ndim - 3)):
         count, length = lax.axis_size(axis), x.shape[dim]
         up = [(i, i + 1) for i in range(count - 1)]
         down = [(i + 1, i) for i in range(count - 1)]

time: 60.7 us -> 61.6 us (1.015)
  waiting for transfers between devices: 28.6 us -> 26.9 us
  starting transfers between devices: 24.3 us -> 25.9 us
  other arithmetic: 1.5 us -> 2.45 us
    ppermute x4, starting transfers between devices: 12.8 us -> 14.7 us  [exchange(): after = lax.ppermute(lax.slice_in_dim(x, 0, h, axis=dim), axis, down)]
    ppermute x4, waiting for transfers between devices: 14.2 us -> 12.5 us  [exchange(): lax.ppermute(lax.slice_in_dim(x, length - h, length, axis=dim), axis, up)]
    another operation x1 -> x0, other arithmetic: 1.23 us -> none  [body(): region = exchange(jnp.stack([permeability, pressure_init, source]), h0)]
    concatenate x3 -> x4, other arithmetic: 0.21 us -> 1.41 us  [exchange(): x = jnp.concatenate([before, x, after], axis=dim)]
    slice x1, other arithmetic: 0.05 us -> 1.03 us  [exchange(): lax.slice_in_dim(x, length - h, length, axis=dim)]
  transfers between devices with their start and end apart: 8 -> 8, of which waited for: 7 -> 6; matrix products, arithmetic and copies ran while one was open for 0% -> 0% of each run, Pallas kernels for 0% -> 0%
where the time goes in v4:
time: 61.6 us; the launch traced here: 61.3 us
  waiting for transfers between devices  26.9 us (44%)
  starting transfers between devices  25.9 us (42%)
  Pallas kernels  5.18 us (8%)
  other arithmetic  2.45 us (4%)
  between operations  0.77 us (1%)
    ppermute x4, starting transfers between devices, exchange(): after = lax.ppermute(lax.slice_in_dim(x, 0, h, axis=dim), axis, down)  14.7 us
    ppermute x4, waiting for transfers between devices, exchange(): after = lax.ppermute(lax.slice_in_dim(x, 0, h, axis=dim), axis, down)  14.4 us
    ppermute x4, waiting for transfers between devices, exchange(): lax.ppermute(lax.slice_in_dim(x, length - h, length, axis=dim), axis, up)  12.5 us
    ppermute x4, starting transfers between devices, exchange(): lax.ppermute(lax.slice_in_dim(x, length - h, length, axis=dim), axis, up)  11.2 us
    pallas_call x2, Pallas kernels, vmem_call(): pl.pallas_call(kernel, out_shape=[jax.ShapeDtypeStruct(s, jnp.float32) fo...  5.18 us
    concatenate x4, other arithmetic, exchange(): x = jnp.concatenate([before, x, after], axis=dim)  1.41 us
  transfers between devices with their start and end apart: 8, of which 6 were waited for; matrix products, arithmetic and copies ran while one was open for 0% of the time, Pallas kernels for 0%

profile of v4, /device:TPU:486, one launch (start us, length us, event | category | flops | bytes accessed | tf_op | source)
XLA Modules:
  0.0 61.3 jit_solution(14958894034982358210)
XLA Ops:
  0.6 1.0 %pad_maximum_fusion.4 = (f32[3,16,8,128]{3,2,1,0:T(8,128)S(1)}, f32[3,16,8,128]{3,2,1,0:T(8,128)S(1)}) fusion(f32[1,16,32,128]{3,2,1,0:T(8,128)} %bitcast.11, f32[1,16,32,128]{3,2,1,0:T(8,128)} %bitcast.14, f32[1,16,32,128]{3,2,1,0:T(8,128)} %bitcast.17), kind=kLoop, calls=%fused_computation.4 | loop fusion | flops 196608 | bytes 1179648 | tf_op jit(solution)/shard_map/slice | solution.py:65
  1.7 5.4 %collective-permute-start = (f32[3,16,8,128]{3,2,1,0:T(8,128)S(1)}, f32[3,16,8,128]{3,2,1,0:T(8,128)S(1)}, u32[]{:S(2)}, u32[]{:S(2)}) collective-permute-start(f32[3,16,8,128]{3,2,1,0:T(8,128)S(1)} %get-tuple-element.13), channel_id=1, source_target_pairs={{0,1},{1,2},{2,3},{3,4},{4,5},{5,6},{6,7},{7,8},{8,9},{9,10},{10,1... | collective-permute-start | bytes 589832 | tf_op jit(solution)/shard_map/ppermute | solution.py:65
  7.1 0.0 copy-start
  7.1 0.0 copy-start.1
  7.1 0.0 copy-start.2
  7.1 2.1 %collective-permute-start.1 = (f32[3,16,8,128]{3,2,1,0:T(8,128)S(1)}, f32[3,16,8,128]{3,2,1,0:T(8,128)S(1)}, u32[]{:S(2)}, u32[]{:S(2)}) collective-permute-start(f32[3,16,8,128]{3,2,1,0:T(8,128)S(1)} %get-tuple-element.14), channel_id=1, source_target_pairs={{1,0},{2,1},{3,2},{4,3},{5,4},{6,5},{7,6},{8,7},{9,8},{10,9},{11,1... | collective-permute-start | bytes 589832 | tf_op jit(solution)/shard_map/ppermute | solution.py:66
  9.2 2.0 %collective-permute-done = f32[3,16,8,128]{3,2,1,0:T(8,128)S(1)} collective-permute-done((f32[3,16,8,128]{3,2,1,0:T(8,128)S(1)}, f32[3,16,8,128]{3,2,1,0:T(8,128)S(1)}, u32[]{:S(2)}, u32[]{:S(2)}) %collective-permute-start) | collective-permute-done | bytes 196640 | tf_op jit(solution)/shard_map/ppermute | solution.py:65
  11.2 7.6 %collective-permute-done.1 = f32[3,16,8,128]{3,2,1,0:T(8,128)S(1)} collective-permute-done((f32[3,16,8,128]{3,2,1,0:T(8,128)S(1)}, f32[3,16,8,128]{3,2,1,0:T(8,128)S(1)}, u32[]{:S(2)}, u32[]{:S(2)}) %collective-permute-start.1) | collective-permute-done | bytes 196640 | tf_op jit(solution)/shard_map/ppermute | solution.py:66
  18.8 1.2 %pad_maximum_fusion.1 = f32[3,16,48,128]{3,2,1,0:T(8,128)S(1)} fusion(f32[3,16,8,128]{3,2,1,0:T(8,128)S(1)} %collective-permute-done.1, f32[1,16,32,128]{3,2,1,0:T(8,128)} %bitcast.12, f32[1,16,32,128]{3,2,1,0:T(8,128)} %bitcast.15, f32[1,16,32,128]{3,2,1,0:T(8,128)} %bitcast.18, f32[3,16,8,128]{3,2,1,0:T(8,128)S(1)} %collective-permute-done), kind=kLoop, calls=%fused_computation.1 | loop fusion | flops 1179648 | bytes 2359296 | tf_op jit(solution)/shard_map/concatenate | solution.py:67
  20.0 0.1 fusion.1
  20.1 1.9 %collective-permute-start.2 = (f32[3,8,48,128]{3,2,1,0:T(8,128)S(1)}, f32[3,8,48,128]{3,2,1,0:T(8,128)S(1)}, u32[]{:S(2)}, u32[]{:S(2)}) collective-permute-start(f32[3,8,48,128]{3,2,1,0:T(8,128)S(1)} %get-tuple-element.11), channel_id=1, source_target_pairs={{0,64},{64,128},{128,192},{192,256},{256,320},{320,384},{384,448},... | collective-permute-start | bytes 1769480 | tf_op jit(solution)/shard_map/ppermute | solution.py:65
  22.0 4.9 %collective-permute-start.3 = (f32[3,8,48,128]{3,2,1,0:T(8,128)S(1)}, f32[3,8,48,128]{3,2,1,0:T(8,128)S(1)}, u32[]{:S(2)}, u32[]{:S(2)}) collective-permute-start(f32[3,8,48,128]{3,2,1,0:T(8,128)S(1)} %get-tuple-element.12), channel_id=1, source_target_pairs={{64,0},{128,64},{192,128},{256,192},{320,256},{384,320},{448,384},... | collective-permute-start | bytes 1769480 | tf_op jit(solution)/shard_map/ppermute | solution.py:66
  26.9 5.6 %collective-permute-done.2 = f32[3,8,48,128]{3,2,1,0:T(8,128)S(1)} collective-permute-done((f32[3,8,48,128]{3,2,1,0:T(8,128)S(1)}, f32[3,8,48,128]{3,2,1,0:T(8,128)S(1)}, u32[]{:S(2)}, u32[]{:S(2)}) %collective-permute-start.2) | collective-permute-done | bytes 589856 | tf_op jit(solution)/shard_map/ppermute | solution.py:65
  32.5 1.8 %collective-permute-done.3 = f32[3,8,48,128]{3,2,1,0:T(8,128)S(1)} collective-permute-done((f32[3,8,48,128]{3,2,1,0:T(8,128)S(1)}, f32[3,8,48,128]{3,2,1,0:T(8,128)S(1)}, u32[]{:S(2)}, u32[]{:S(2)}) %collective-permute-start.3) | collective-permute-done | bytes 589856 | tf_op jit(solution)/shard_map/ppermute | solution.py:66
  34.3 0.0 copy-done
  34.3 0.0 copy-done.1
  34.3 0.0 copy-done.2
  34.3 0.2 pad_maximum_fusion.region
  34.5 4.0 %shard_map.58 = (f32[16,32,128]{2,1,0:T(8,128)}, f32[8,16,128]{2,1,0:T(8,128)}, f32[4,8,128]{2,1,0:T(8,128)S(1)}, f32[4,8,128]{2,1,0:T(8,128)S(1)}) custom-call(f32[3,32,48,128]{3,2,1,0:T(8,128)S(1)} %pad_maximum_fusion.region), custom_call_target="tpu_custom_call" | custom-call | tf_op jit(solution)/shard_map/pallas_call | solution.py:158
  38.5 1.9 %collective-permute-start.4 = (f32[2,4,4,128]{3,2,1,0:T(4,128)S(1)}, f32[2,4,4,128]{3,2,1,0:T(4,128)S(1)}, u32[]{:S(2)}, u32[]{:S(2)}) collective-permute-start(f32[2,4,4,128]{3,2,1,0:T(4,128)S(1)} %get-tuple-element.15), channel_id=1, source_target_pairs={{0,1},{1,2},{2,3},{3,4},{4,5},{5,6},{6,7},{7,8},{8,9},{9,10},{10,1... | collective-permute-start | bytes 49160 | tf_op jit(solution)/shard_map/ppermute | solution.py:65
  40.4 3.9 %collective-permute-start.5 = (f32[2,4,4,128]{3,2,1,0:T(4,128)S(1)}, f32[2,4,4,128]{3,2,1,0:T(4,128)S(1)}, u32[]{:S(2)}, u32[]{:S(2)}) collective-permute-start(f32[2,4,4,128]{3,2,1,0:T(4,128)S(1)} %get-tuple-element.16), channel_id=1, source_target_pairs={{1,0},{2,1},{3,2},{4,3},{5,4},{6,5},{7,6},{8,7},{9,8},{10,9},{11,1... | collective-permute-start | bytes 49160 | tf_op jit(solution)/shard_map/ppermute | solution.py:66
  44.3 0.0 collective-permute-done.4
  44.3 5.0 %collective-permute-done.5 = f32[2,4,4,128]{3,2,1,0:T(4,128)S(1)} collective-permute-done((f32[2,4,4,128]{3,2,1,0:T(4,128)S(1)}, f32[2,4,4,128]{3,2,1,0:T(4,128)S(1)}, u32[]{:S(2)}, u32[]{:S(2)}) %collective-permute-start.5) | collective-permute-done | bytes 16416 | tf_op jit(solution)/shard_map/ppermute | solution.py:66
  49.4 3.9 %collective-permute-start.7 = (f32[2,4,16,128]{3,2,1,0:T(8,128)S(1)}, f32[2,4,16,128]{3,2,1,0:T(8,128)S(1)}, u32[]{:S(2)}, u32[]{:S(2)}) collective-permute-start(f32[2,4,16,128]{3,2,1,0:T(8,128)S(1)} %pad_maximum_fusion.6), channel_id=1, source_target_pairs={{64,0},{128,64},{192,128},{256,192},{320,256},{384,320},{448,384},... | collective-permute-start | bytes 196616 | tf_op jit(solution)/shard_map/ppermute | solution.py:66
  53.2 1.9 %collective-permute-start.6 = (f32[2,4,16,128]{3,2,1,0:T(8,128)S(1)}, f32[2,4,16,128]{3,2,1,0:T(8,128)S(1)}, u32[]{:S(2)}, u32[]{:S(2)}) collective-permute-start(f32[2,4,16,128]{3,2,1,0:T(8,128)S(1)} %pad_maximum_fusion.6), channel_id=1, source_target_pairs={{0,64},{64,128},{128,192},{192,256},{256,320},{320,384},{384,448},... | collective-permute-start | bytes 196616 | tf_op jit(solution)/shard_map/ppermute | solution.py:65
  55.2 0.0 collective-permute-done.7
  55.2 4.9 %collective-permute-done.6 = f32[2,4,16,128]{3,2,1,0:T(8,128)S(1)} collective-permute-done((f32[2,4,16,128]{3,2,1,0:T(8,128)S(1)}, f32[2,4,16,128]{3,2,1,0:T(8,128)S(1)}, u32[]{:S(2)}, u32[]{:S(2)}) %collective-permute-start.6) | collective-permute-done | bytes 65568 | tf_op jit(solution)/shard_map/ppermute | solution.py:65
  60.1 1.2 %shard_map.59 = f32[4,8,128]{2,1,0:T(8,128)} custom-call(f32[2,12,16,128]{3,2,1,0:T(8,128)S(1)} %pad_maximum_fusion.5.region), custom_call_target="tpu_custom_call" | custom-call | tf_op jit(solution)/shard_map/pallas_call | solution.py:158
  (3 shorter events, 0.0 us)
Async XLA Ops:
  1.7 9.6 %collective-permute-start = (f32[3,16,8,128]{3,2,1,0:T(8,128)S(1)}, f32[3,16,8,128]{3,2,1,0:T(8,128)S(1)}, u32[]{:S(2)}, u32[]{:S(2)}) collective-permute-start(f32[3,16,8,128]{3,2,1,0:T(8,128)S(1)} %get-tuple-element.13), channel_id=1, source_target_pairs={{0,1},{1,2},{2,3},{3,4},{4,5},{5,6},{6,7},{7,8},{8,9},{9,10},{10,1... | collective-permute-start | bytes 589832 | tf_op jit(solution)/shard_map/ppermute | solution.py:65
  7.1 27.2 %copy-start = (f32[16,32,128]{2,1,0:T(8,128)S(1)}, f32[16,32,128]{2,1,0:T(8,128)}, u32[]{:S(2)}) copy-start(f32[16,32,128]{2,1,0:T(8,128)} %param.4) | copy-start | bytes 786436
  7.1 27.2 %copy-start.1 = (f32[16,32,128]{2,1,0:T(8,128)S(1)}, f32[16,32,128]{2,1,0:T(8,128)}, u32[]{:S(2)}) copy-start(f32[16,32,128]{2,1,0:T(8,128)} %param.3) | copy-start | bytes 786436
  7.1 27.2 %copy-start.2 = (f32[16,32,128]{2,1,0:T(8,128)S(1)}, f32[16,32,128]{2,1,0:T(8,128)}, u32[]{:S(2)}) copy-start(f32[16,32,128]{2,1,0:T(8,128)} %param.5) | copy-start | bytes 786436
  7.1 11.7 %collective-permute-start.1 = (f32[3,16,8,128]{3,2,1,0:T(8,128)S(1)}, f32[3,16,8,128]{3,2,1,0:T(8,128)S(1)}, u32[]{:S(2)}, u32[]{:S(2)}) collective-permute-start(f32[3,16,8,128]{3,2,1,0:T(8,128)S(1)} %get-tuple-element.14), channel_id=1, source_target_pairs={{1,0},{2,1},{3,2},{4,3},{5,4},{6,5},{7,6},{8,7},{9,8},{10,9},{11,1... | collective-permute-start | bytes 589832 | tf_op jit(solution)/shard_map/ppermute | solution.py:66
  20.1 12.4 %collective-permute-start.2 = (f32[3,8,48,128]{3,2,1,0:T(8,128)S(1)}, f32[3,8,48,128]{3,2,1,0:T(8,128)S(1)}, u32[]{:S(2)}, u32[]{:S(2)}) collective-permute-start(f32[3,8,48,128]{3,2,1,0:T(8,128)S(1)} %get-tuple-element.11), channel_id=1, source_target_pairs={{0,64},{64,128},{128,192},{192,256},{256,320},{320,384},{384,448},... | collective-permute-start | bytes 1769480 | tf_op jit(solution)/shard_map/ppermute | solution.py:65
  22.0 12.2 %collective-permute-start.3 = (f32[3,8,48,128]{3,2,1,0:T(8,128)S(1)}, f32[3,8,48,128]{3,2,1,0:T(8,128)S(1)}, u32[]{:S(2)}, u32[]{:S(2)}) collective-permute-start(f32[3,8,48,128]{3,2,1,0:T(8,128)S(1)} %get-tuple-element.12), channel_id=1, source_target_pairs={{64,0},{128,64},{192,128},{256,192},{320,256},{384,320},{448,384},... | collective-permute-start | bytes 1769480 | tf_op jit(solution)/shard_map/ppermute | solution.py:66
  38.5 5.9 %collective-permute-start.4 = (f32[2,4,4,128]{3,2,1,0:T(4,128)S(1)}, f32[2,4,4,128]{3,2,1,0:T(4,128)S(1)}, u32[]{:S(2)}, u32[]{:S(2)}) collective-permute-start(f32[2,4,4,128]{3,2,1,0:T(4,128)S(1)} %get-tuple-element.15), channel_id=1, source_target_pairs={{0,1},{1,2},{2,3},{3,4},{4,5},{5,6},{6,7},{7,8},{8,9},{9,10},{10,1... | collective-permute-start | bytes 49160 | tf_op jit(solution)/shard_map/ppermute | solution.py:65
  40.4 9.0 %collective-permute-start.5 = (f32[2,4,4,128]{3,2,1,0:T(4,128)S(1)}, f32[2,4,4,128]{3,2,1,0:T(4,128)S(1)}, u32[]{:S(2)}, u32[]{:S(2)}) collective-permute-start(f32[2,4,4,128]{3,2,1,0:T(4,128)S(1)} %get-tuple-element.16), channel_id=1, source_target_pairs={{1,0},{2,1},{3,2},{4,3},{5,4},{6,5},{7,6},{8,7},{9,8},{10,9},{11,1... | collective-permute-start | bytes 49160 | tf_op jit(solution)/shard_map/ppermute | solution.py:66
  49.4 5.8 %collective-permute-start.7 = (f32[2,4,16,128]{3,2,1,0:T(8,128)S(1)}, f32[2,4,16,128]{3,2,1,0:T(8,128)S(1)}, u32[]{:S(2)}, u32[]{:S(2)}) collective-permute-start(f32[2,4,16,128]{3,2,1,0:T(8,128)S(1)} %pad_maximum_fusion.6), channel_id=1, source_target_pairs={{64,0},{128,64},{192,128},{256,192},{320,256},{384,320},{448,384},... | collective-permute-start | bytes 196616 | tf_op jit(solution)/shard_map/ppermute | solution.py:66
  53.2 6.8 %collective-permute-start.6 = (f32[2,4,16,128]{3,2,1,0:T(8,128)S(1)}, f32[2,4,16,128]{3,2,1,0:T(8,128)S(1)}, u32[]{:S(2)}, u32[]{:S(2)}) collective-permute-start(f32[2,4,16,128]{3,2,1,0:T(8,128)S(1)} %pad_maximum_fusion.6), channel_id=1, source_target_pairs={{0,64},{64,128},{128,192},{192,256},{256,320},{320,384},{384,448},... | collective-permute-start | bytes 196616 | tf_op jit(solution)/shard_map/ppermute | solution.py:65

commit v5 on v4

--- a/solution.py
+++ b/solution.py
@@ -57,15 +57,31 @@
     return 0.25 * jnp.sum(field.reshape(sx // 2, 2, sy // 2, 2, sz), axis=(1, 3))
 
 
-def exchange(x, h):
-    for axis, dim in (("gy", x.ndim - 2), ("gx", x.ndim - 3)):
-        count, length = lax.axis_size(axis), x.shape[dim]
-        up = [(i, i + 1) for i in range(count - 1)]
-        down = [(i + 1, i) for i in range(count - 1)]
-        before = lax.ppermute(lax.slice_in_dim(x, length - h, length, axis=dim), axis, up)
-        after = lax.ppermute(lax.slice_in_dim(x, 0, h, axis=dim), axis, down)
-        x = jnp.concatenate([before, x, after], axis=dim)
-    return x
+def exchange(tiles, h):
+    lo_y, hi_y, lo_x, hi_x = exchange_pieces(tiles, h)
+    mid = jnp.concatenate([lo_y, jnp.stack(tiles), hi_y], axis=2)
+    return jnp.concatenate([lo_x, mid, hi_x], axis=1)
+
+
+def shift_in(edge, axis, step):
+    count = lax.axis_size(axis)
+    pairs = [(i, i + step) for i in range(count) if 0 <= i + step < count]
+    return lax.ppermute(edge, axis, pairs)
+
+
+def exchange_pieces(tiles, h):
+    ny = tiles[0].shape[1]
+    nx = tiles[0].shape[0]
+    lo_y = shift_in(jnp.stack([t[:, ny - h:] for t in tiles]), "gy", 1)
+    hi_y = shift_in(jnp.stack([t[:, :h] for t in tiles]), "gy", -1)
+
+    def rows(lo, hi):
+        body = jnp.stack([t[lo:hi] for t in tiles])
+        return jnp.concatenate([lo_y[:, lo:hi], body, hi_y[:, lo:hi]], axis=2)
+
+    lo_x = shift_in(rows(nx - h, nx), "gx", 1)
+    hi_x = shift_in(rows(0, h), "gx", -1)
+    return lo_y, hi_y, lo_x, hi_x
 
 
 def inner(a, h):
@@ -112,9 +128,17 @@
     return 0.25 * ((at(0, 0) + at(1, 0)) + (at(0, 1) + at(1, 1)))
 
 
-def fine_kernel(region, p_out, mid_out, rhs2_out, perm2_out, k0_scr, r0_scr, k1_scr, r1_scr):
+def fine_kernel(perm_in, p_in, s_in, lo_y, hi_y, lo_x, hi_x,
+                p_out, mid_out, rhs2_out, perm2_out, region, k0_scr, r0_scr, k1_scr, r1_scr):
     h0 = FINE_HALO
     h1 = h0 // 2
+    nx, ny = perm_in.shape[0], perm_in.shape[1]
+    for k, tile in enumerate((perm_in, p_in, s_in)):
+        region[k, pl.ds(h0, nx), pl.ds(0, h0), :] = lo_y[k]
+        region[k, pl.ds(h0, nx), pl.ds(h0, ny), :] = tile[...]
+        region[k, pl.ds(h0, nx), pl.ds(h0 + ny, h0), :] = hi_y[k]
+        region[k, pl.ds(0, h0), :, :] = lo_x[k]
+        region[k, pl.ds(h0 + nx, h0), :, :] = hi_x[k]
     perm0 = region[0]
     pressure = region[1]
     src = region[2]
@@ -168,17 +192,19 @@
 def body(pressure_init, source, permeability):
     h0, h2 = FINE_HALO, COARSE_HALO
     nx, ny, nz = pressure_init.shape
-    region = exchange(jnp.stack([permeability, pressure_init, source]), h0)
+    tiles = [permeability, pressure_init, source]
+    pieces = exchange_pieces(tiles, h0)
     px, py = nx + 2 * h0, ny + 2 * h0
     mid = (nx // 2, ny // 2, nz)
     coarse = (nx // 4, ny // 4, nz)
     pressure_out, correction_mid, rhs_coarse, perm_coarse = vmem_call(
         fine_kernel,
         [(nx, ny, nz), mid, coarse, coarse],
-        [(px, py, nz), (px, py, nz), (px // 2, py // 2, nz), (px // 2, py // 2, nz)],
-        region,
+        [(3, px, py, nz), (px, py, nz), (px, py, nz), (px // 2, py // 2, nz), (px // 2, py // 2, nz)],
+        *tiles,
+        *pieces,
     )
-    region2 = exchange(jnp.stack([perm_coarse, rhs_coarse]), h2)
+    region2 = exchange([perm_coarse, rhs_coarse], h2)
     c2x, c2y = coarse[0] + 2 * h2, coarse[1] + 2 * h2
     (correction_coarse,) = vmem_call(coarse_kernel, [coarse], [(c2x, c2y, nz)], region2)
     return (pressure_out, correction_mid, correction_coarse)

time: 61.6 us -> 62.9 us (1.021)
  the two profiles are of different devices: /device:TPU:486 before, /device:TPU:288 now
where the time goes in v5:
time: 62.9 us; the launch traced here: 62.5 us
  starting transfers between devices  31.3 us (50%)
  waiting for transfers between devices  23 us (37%)
  Pallas kernels  5.17 us (8%)
  local copies, waits for them, and re-layouts  2 us (3%)
  between operations  0.84 us (1%)
    ppermute x8, starting transfers between devices, shift_in(): return lax.ppermute(edge, axis, pairs)  31.3 us
    ppermute x8, waiting for transfers between devices, shift_in(): return lax.ppermute(edge, axis, pairs)  23 us
    pallas_call x2, Pallas kernels, vmem_call(): pl.pallas_call(kernel, out_shape=[jax.ShapeDtypeStruct(s, jnp.float32) fo...  5.17 us
    another operation x2, local copies, waits for them, and re-layouts, exchange_pieces(): hi_y = shift_in(jnp.stack([t[:, :h] for t in tiles]), 'gy', -1)  1.82 us
  transfers between devices with their start and end apart: 8, of which 6 were waited for; matrix products, arithmetic and copies ran while one was open for 0% of the time, Pallas kernels for 0%

profile of v5, /device:TPU:288, one launch (start us, length us, event | category | flops | bytes accessed | tf_op | source)
XLA Modules:
  0.0 62.5 jit_solution(8884631731252113118)
XLA Ops:
  0.6 0.0 copy-start.1
  0.6 0.9 %slice_bitcast_fusion.8 = (f32[1,16,8,128]{3,2,1,0:T(8,128)S(1)}, f32[1,16,8,128]{3,2,1,0:T(8,128)S(1)}) fusion(f32[16,32,128]{2,1,0:T(8,128)} %perm_in.1), kind=kLoop, calls=%fused_computation.14 | loop fusion | bytes 262144 | tf_op jit(solution)/shard_map/stack | solution.py:76
  1.6 0.1 copy-done.1
  1.6 0.9 %slice_bitcast_fusion.6 = (f32[1,16,8,128]{3,2,1,0:T(8,128)S(1)}, f32[1,16,8,128]{3,2,1,0:T(8,128)S(1)}, f32[1,16,8,128]{3,2,1,0:T(8,128)S(1)}, f32[1,16,8,128]{3,2,1,0:T(8,128)S(1)}) fusion(f32[16,32,128]{2,1,0:T(8,128)} %s_in.1, f32[16,32,128]{2,1,0:T(8,128)S(1)} %copy-done.1), kind=kLoop, calls=%fused_computation.12 | loop fusion | bytes 524288 | tf_op jit(solution)/shard_map/stack | solution.py:76
  2.6 0.0 copy-start.2
  2.6 3.5 %collective-permute-start = (f32[3,16,8,128]{3,2,1,0:T(8,128)S(1)}, f32[3,16,8,128]{3,2,1,0:T(8,128)S(1)}, u32[]{:S(2)}, u32[]{:S(2)}) collective-permute-start(f32[3,16,8,128]{3,2,1,0:T(8,128)S(1)} %pad_maximum_fusion.2), channel_id=1, source_target_pairs={{0,1},{1,2},{2,3},{3,4},{4,5},{5,6},{6,7},{7,8},{8,9},{9,10},{10,1... | collective-permute-start | bytes 589832 | tf_op jit(solution)/shard_map/ppermute | solution.py:69
  6.1 0.0 copy-start
  6.1 5.9 %collective-permute-start.1 = (f32[3,16,8,128]{3,2,1,0:T(8,128)S(1)}, f32[3,16,8,128]{3,2,1,0:T(8,128)S(1)}, u32[]{:S(2)}, u32[]{:S(2)}) collective-permute-start(f32[3,16,8,128]{3,2,1,0:T(8,128)S(1)} %pad_maximum_fusion.3), channel_id=1, source_target_pairs={{1,0},{2,1},{3,2},{4,3},{5,4},{6,5},{7,6},{8,7},{9,8},{10,9},{11,1... | collective-permute-start | bytes 589832 | tf_op jit(solution)/shard_map/ppermute | solution.py:69
  12.1 0.0 copy-done.2
  12.1 0.0 copy-done
  12.1 2.4 %collective-permute-done.lo_y = f32[3,16,8,128]{3,2,1,0:T(8,128)S(1)} collective-permute-done((f32[3,16,8,128]{3,2,1,0:T(8,128)S(1)}, f32[3,16,8,128]{3,2,1,0:T(8,128)S(1)}, u32[]{:S(2)}, u32[]{:S(2)}) %collective-permute-start) | collective-permute-done | bytes 196640 | tf_op jit(solution)/shard_map/ppermute | solution.py:69
  14.6 1.3 %collective-permute-done.1.hi_y = f32[3,16,8,128]{3,2,1,0:T(8,128)S(1)} collective-permute-done((f32[3,16,8,128]{3,2,1,0:T(8,128)S(1)}, f32[3,16,8,128]{3,2,1,0:T(8,128)S(1)}, u32[]{:S(2)}, u32[]{:S(2)}) %collective-permute-start.1) | collective-permute-done | bytes 196640 | tf_op jit(solution)/shard_map/ppermute | solution.py:69
  16.0 1.9 %collective-permute-start.2 = (f32[3,8,48,128]{3,2,1,0:T(8,128)S(1)}, f32[3,8,48,128]{3,2,1,0:T(8,128)S(1)}, u32[]{:S(2)}, u32[]{:S(2)}) collective-permute-start(f32[3,8,48,128]{3,2,1,0:T(8,128)S(1)} %pad_maximum_fusion), channel_id=1, source_target_pairs={{0,64},{64,128},{128,192},{192,256},{256,320},{320,384},{384,448},... | collective-permute-start | bytes 1769480 | tf_op jit(solution)/shard_map/ppermute | solution.py:69
  18.0 4.9 %collective-permute-start.3 = (f32[3,8,48,128]{3,2,1,0:T(8,128)S(1)}, f32[3,8,48,128]{3,2,1,0:T(8,128)S(1)}, u32[]{:S(2)}, u32[]{:S(2)}) collective-permute-start(f32[3,8,48,128]{3,2,1,0:T(8,128)S(1)} %pad_maximum_fusion.1), channel_id=1, source_target_pairs={{64,0},{128,64},{192,128},{256,192},{320,256},{384,320},{448,384},... | collective-permute-start | bytes 1769480 | tf_op jit(solution)/shard_map/ppermute | solution.py:69
  22.8 5.6 %collective-permute-done.2.lo_x = f32[3,8,48,128]{3,2,1,0:T(8,128)S(1)} collective-permute-done((f32[3,8,48,128]{3,2,1,0:T(8,128)S(1)}, f32[3,8,48,128]{3,2,1,0:T(8,128)S(1)}, u32[]{:S(2)}, u32[]{:S(2)}) %collective-permute-start.2) | collective-permute-done | bytes 589856 | tf_op jit(solution)/shard_map/ppermute | solution.py:69
  28.4 1.8 %collective-permute-done.3.hi_x = f32[3,8,48,128]{3,2,1,0:T(8,128)S(1)} collective-permute-done((f32[3,8,48,128]{3,2,1,0:T(8,128)S(1)}, f32[3,8,48,128]{3,2,1,0:T(8,128)S(1)}, u32[]{:S(2)}, u32[]{:S(2)}) %collective-permute-start.3) | collective-permute-done | bytes 589856 | tf_op jit(solution)/shard_map/ppermute | solution.py:69
  30.2 4.0 %shard_map.58 = (f32[16,32,128]{2,1,0:T(8,128)}, f32[8,16,128]{2,1,0:T(8,128)}, f32[4,8,128]{2,1,0:T(8,128)S(1)}, f32[4,8,128]{2,1,0:T(8,128)S(1)}) custom-call(f32[16,32,128]{2,1,0:T(8,128)S(1)} %copy-done, f32[16,32,128]{2,1,0:T(8,128)S(1)} %copy-done.1, f32[16,32,128]{2,1,0:T(8,128)S(1)} %copy-done.2, f32[3,16,8,128]{3,2,1,0:T(8,128)S(1)} %collective-permute-done.lo_y, ...), custom_call_target="tpu_custom_call" | custom-call | tf_op jit(solution)/shard_map/pallas_call | solution.py:182
  34.2 7.7 %collective-permute-start.5 = (f32[2,4,4,128]{3,2,1,0:T(4,128)S(1)}, f32[2,4,4,128]{3,2,1,0:T(4,128)S(1)}, u32[]{:S(2)}, u32[]{:S(2)}) collective-permute-start(f32[2,4,4,128]{3,2,1,0:T(4,128)S(1)} %pad_maximum_fusion.7), channel_id=1, source_target_pairs={{1,0},{2,1},{3,2},{4,3},{5,4},{6,5},{7,6},{8,7},{9,8},{10,9},{11,1... | collective-permute-start | bytes 49160 | tf_op jit(solution)/shard_map/ppermute | solution.py:69
  41.9 1.9 %collective-permute-start.4 = (f32[2,4,4,128]{3,2,1,0:T(4,128)S(1)}, f32[2,4,4,128]{3,2,1,0:T(4,128)S(1)}, u32[]{:S(2)}, u32[]{:S(2)}) collective-permute-start(f32[2,4,4,128]{3,2,1,0:T(4,128)S(1)} %pad_maximum_fusion.6), channel_id=1, source_target_pairs={{0,1},{1,2},{2,3},{3,4},{4,5},{5,6},{6,7},{7,8},{8,9},{9,10},{10,1... | collective-permute-start | bytes 49160 | tf_op jit(solution)/shard_map/ppermute | solution.py:69
  43.8 0.0 collective-permute-done.5
  43.9 7.0 %collective-permute-done.4 = f32[2,4,4,128]{3,2,1,0:T(4,128)S(1)} collective-permute-done((f32[2,4,4,128]{3,2,1,0:T(4,128)S(1)}, f32[2,4,4,128]{3,2,1,0:T(4,128)S(1)}, u32[]{:S(2)}, u32[]{:S(2)}) %collective-permute-start.4) | collective-permute-done | bytes 16416 | tf_op jit(solution)/shard_map/ppermute | solution.py:69
  50.9 3.6 %collective-permute-start.7 = (f32[2,4,16,128]{3,2,1,0:T(8,128)S(1)}, f32[2,4,16,128]{3,2,1,0:T(8,128)S(1)}, u32[]{:S(2)}, u32[]{:S(2)}) collective-permute-start(f32[2,4,16,128]{3,2,1,0:T(8,128)S(1)} %pad_maximum_fusion.5), channel_id=1, source_target_pairs={{64,0},{128,64},{192,128},{256,192},{320,256},{384,320},{448,384},... | collective-permute-start | bytes 196616 | tf_op jit(solution)/shard_map/ppermute | solution.py:69
  54.5 1.9 %collective-permute-start.6 = (f32[2,4,16,128]{3,2,1,0:T(8,128)S(1)}, f32[2,4,16,128]{3,2,1,0:T(8,128)S(1)}, u32[]{:S(2)}, u32[]{:S(2)}) collective-permute-start(f32[2,4,16,128]{3,2,1,0:T(8,128)S(1)} %pad_maximum_fusion.5), channel_id=1, source_target_pairs={{0,64},{64,128},{128,192},{192,256},{256,320},{320,384},{384,448},... | collective-permute-start | bytes 196616 | tf_op jit(solution)/shard_map/ppermute | solution.py:69
  56.4 0.0 collective-permute-done.7
  56.4 4.9 %collective-permute-done.6 = f32[2,4,16,128]{3,2,1,0:T(8,128)S(1)} collective-permute-done((f32[2,4,16,128]{3,2,1,0:T(8,128)S(1)}, f32[2,4,16,128]{3,2,1,0:T(8,128)S(1)}, u32[]{:S(2)}, u32[]{:S(2)}) %collective-permute-start.6) | collective-permute-done | bytes 65568 | tf_op jit(solution)/shard_map/ppermute | solution.py:69
  61.3 1.2 %shard_map.59 = f32[4,8,128]{2,1,0:T(8,128)} custom-call(f32[2,12,16,128]{3,2,1,0:T(8,128)S(1)} %pad_maximum_fusion.4.region), custom_call_target="tpu_custom_call" | custom-call | tf_op jit(solution)/shard_map/pallas_call | solution.py:182
  (14 shorter events, 0.3 us)
Async XLA Ops:
  0.6 1.0 %copy-start.1 = (f32[16,32,128]{2,1,0:T(8,128)S(1)}, f32[16,32,128]{2,1,0:T(8,128)}, u32[]{:S(2)}) copy-start(f32[16,32,128]{2,1,0:T(8,128)} %p_in.1) | copy-start | bytes 786436
  2.6 9.5 %copy-start.2 = (f32[16,32,128]{2,1,0:T(8,128)S(1)}, f32[16,32,128]{2,1,0:T(8,128)}, u32[]{:S(2)}) copy-start(f32[16,32,128]{2,1,0:T(8,128)} %s_in.1) | copy-start | bytes 786436
  2.6 12.0 %collective-permute-start = (f32[3,16,8,128]{3,2,1,0:T(8,128)S(1)}, f32[3,16,8,128]{3,2,1,0:T(8,128)S(1)}, u32[]{:S(2)}, u32[]{:S(2)}) collective-permute-start(f32[3,16,8,128]{3,2,1,0:T(8,128)S(1)} %pad_maximum_fusion.2), channel_id=1, source_target_pairs={{0,1},{1,2},{2,3},{3,4},{4,5},{5,6},{6,7},{7,8},{8,9},{9,10},{10,1... | collective-permute-start | bytes 589832 | tf_op jit(solution)/shard_map/ppermute | solution.py:69
  6.1 6.0 %copy-start = (f32[16,32,128]{2,1,0:T(8,128)S(1)}, f32[16,32,128]{2,1,0:T(8,128)}, u32[]{:S(2)}) copy-start(f32[16,32,128]{2,1,0:T(8,128)} %perm_in.1) | copy-start | bytes 786436
  6.1 9.8 %collective-permute-start.1 = (f32[3,16,8,128]{3,2,1,0:T(8,128)S(1)}, f32[3,16,8,128]{3,2,1,0:T(8,128)S(1)}, u32[]{:S(2)}, u32[]{:S(2)}) collective-permute-start(f32[3,16,8,128]{3,2,1,0:T(8,128)S(1)} %pad_maximum_fusion.3), channel_id=1, source_target_pairs={{1,0},{2,1},{3,2},{4,3},{5,4},{6,5},{7,6},{8,7},{9,8},{10,9},{11,1... | collective-permute-start | bytes 589832 | tf_op jit(solution)/shard_map/ppermute | solution.py:69
  16.0 12.4 %collective-permute-start.2 = (f32[3,8,48,128]{3,2,1,0:T(8,128)S(1)}, f32[3,8,48,128]{3,2,1,0:T(8,128)S(1)}, u32[]{:S(2)}, u32[]{:S(2)}) collective-permute-start(f32[3,8,48,128]{3,2,1,0:T(8,128)S(1)} %pad_maximum_fusion), channel_id=1, source_target_pairs={{0,64},{64,128},{128,192},{192,256},{256,320},{320,384},{384,448},... | collective-permute-start | bytes 1769480 | tf_op jit(solution)/shard_map/ppermute | solution.py:69
  18.0 12.2 %collective-permute-start.3 = (f32[3,8,48,128]{3,2,1,0:T(8,128)S(1)}, f32[3,8,48,128]{3,2,1,0:T(8,128)S(1)}, u32[]{:S(2)}, u32[]{:S(2)}) collective-permute-start(f32[3,8,48,128]{3,2,1,0:T(8,128)S(1)} %pad_maximum_fusion.1), channel_id=1, source_target_pairs={{64,0},{128,64},{192,128},{256,192},{320,256},{384,320},{448,384},... | collective-permute-start | bytes 1769480 | tf_op jit(solution)/shard_map/ppermute | solution.py:69
  34.2 9.7 %collective-permute-start.5 = (f32[2,4,4,128]{3,2,1,0:T(4,128)S(1)}, f32[2,4,4,128]{3,2,1,0:T(4,128)S(1)}, u32[]{:S(2)}, u32[]{:S(2)}) collective-permute-start(f32[2,4,4,128]{3,2,1,0:T(4,128)S(1)} %pad_maximum_fusion.7), channel_id=1, source_target_pairs={{1,0},{2,1},{3,2},{4,3},{5,4},{6,5},{7,6},{8,7},{9,8},{10,9},{11,1... | collective-permute-start | bytes 49160 | tf_op jit(solution)/shard_map/ppermute | solution.py:69
  41.9 9.0 %collective-permute-start.4 = (f32[2,4,4,128]{3,2,1,0:T(4,128)S(1)}, f32[2,4,4,128]{3,2,1,0:T(4,128)S(1)}, u32[]{:S(2)}, u32[]{:S(2)}) collective-permute-start(f32[2,4,4,128]{3,2,1,0:T(4,128)S(1)} %pad_maximum_fusion.6), channel_id=1, source_target_pairs={{0,1},{1,2},{2,3},{3,4},{4,5},{5,6},{6,7},{7,8},{8,9},{9,10},{10,1... | collective-permute-start | bytes 49160 | tf_op jit(solution)/shard_map/ppermute | solution.py:69
  50.9 5.5 %collective-permute-start.7 = (f32[2,4,16,128]{3,2,1,0:T(8,128)S(1)}, f32[2,4,16,128]{3,2,1,0:T(8,128)S(1)}, u32[]{:S(2)}, u32[]{:S(2)}) collective-permute-start(f32[2,4,16,128]{3,2,1,0:T(8,128)S(1)} %pad_maximum_fusion.5), channel_id=1, source_target_pairs={{64,0},{128,64},{192,128},{256,192},{320,256},{384,320},{448,384},... | collective-permute-start | bytes 196616 | tf_op jit(solution)/shard_map/ppermute | solution.py:69
  54.5 6.8 %collective-permute-start.6 = (f32[2,4,16,128]{3,2,1,0:T(8,128)S(1)}, f32[2,4,16,128]{3,2,1,0:T(8,128)S(1)}, u32[]{:S(2)}, u32[]{:S(2)}) collective-permute-start(f32[2,4,16,128]{3,2,1,0:T(8,128)S(1)} %pad_maximum_fusion.5), channel_id=1, source_target_pairs={{0,64},{64,128},{128,192},{192,256},{256,320},{320,384},{384,448},... | collective-permute-start | bytes 196616 | tf_op jit(solution)/shard_map/ppermute | solution.py:69

commit v6 on v5

--- a/solution.py
+++ b/solution.py
@@ -12,6 +12,7 @@
 OMEGA = 0.8
 
 FINE_HALO = 8
+FINE_Y_HALO = 20
 COARSE_HALO = 4
 
 
@@ -57,10 +58,11 @@
     return 0.25 * jnp.sum(field.reshape(sx // 2, 2, sy // 2, 2, sz), axis=(1, 3))
 
 
-def exchange(tiles, h):
-    lo_y, hi_y, lo_x, hi_x = exchange_pieces(tiles, h)
-    mid = jnp.concatenate([lo_y, jnp.stack(tiles), hi_y], axis=2)
-    return jnp.concatenate([lo_x, mid, hi_x], axis=1)
+def exchange_x(tiles, h):
+    nx = tiles[0].shape[0]
+    lo_x = shift_in(jnp.stack([t[nx - h:] for t in tiles]), "gx", 1)
+    hi_x = shift_in(jnp.stack([t[:h] for t in tiles]), "gx", -1)
+    return jnp.concatenate([lo_x, jnp.stack(tiles), hi_x], axis=1)
 
 
 def shift_in(edge, axis, step):
@@ -69,11 +71,12 @@
     return lax.ppermute(edge, axis, pairs)
 
 
-def exchange_pieces(tiles, h):
+def exchange_pieces(tiles, h, hy=None):
+    hy = h if hy is None else hy
     ny = tiles[0].shape[1]
     nx = tiles[0].shape[0]
-    lo_y = shift_in(jnp.stack([t[:, ny - h:] for t in tiles]), "gy", 1)
-    hi_y = shift_in(jnp.stack([t[:, :h] for t in tiles]), "gy", -1)
+    lo_y = shift_in(jnp.stack([t[:, ny - hy:] for t in tiles]), "gy", 1)
+    hi_y = shift_in(jnp.stack([t[:, :hy] for t in tiles]), "gy", -1)
 
     def rows(lo, hi):
         body = jnp.stack([t[lo:hi] for t in tiles])
@@ -122,21 +125,21 @@
     return out
 
 
-def k_restrict(ref, lo, nx, ny):
+def k_restrict(ref, lox, loy, nx, ny):
     def at(dx, dy):
-        return ref[pl.ds(lo + dx, nx, stride=2), pl.ds(lo + dy, ny, stride=2), :]
+        return ref[pl.ds(lox + dx, nx, stride=2), pl.ds(loy + dy, ny, stride=2), :]
     return 0.25 * ((at(0, 0) + at(1, 0)) + (at(0, 1) + at(1, 1)))
 
 
 def fine_kernel(perm_in, p_in, s_in, lo_y, hi_y, lo_x, hi_x,
                 p_out, mid_out, rhs2_out, perm2_out, region, k0_scr, r0_scr, k1_scr, r1_scr):
-    h0 = FINE_HALO
-    h1 = h0 // 2
+    h0, hy, h2 = FINE_HALO, FINE_Y_HALO, COARSE_HALO
+    h1, h1y = h0 // 2, hy // 2
     nx, ny = perm_in.shape[0], perm_in.shape[1]
     for k, tile in enumerate((perm_in, p_in, s_in)):
-        region[k, pl.ds(h0, nx), pl.ds(0, h0), :] = lo_y[k]
-        region[k, pl.ds(h0, nx), pl.ds(h0, ny), :] = tile[...]
-        region[k, pl.ds(h0, nx), pl.ds(h0 + ny, h0), :] = hi_y[k]
+        region[k, pl.ds(h0, nx), pl.ds(0, hy), :] = lo_y[k]
+        region[k, pl.ds(h0, nx), pl.ds(hy, ny), :] = tile[...]
+        region[k, pl.ds(h0, nx), pl.ds(hy + ny, hy), :] = hi_y[k]
         region[k, pl.ds(0, h0), :, :] = lo_x[k]
         region[k, pl.ds(h0 + nx, h0), :, :] = hi_x[k]
     perm0 = region[0]
@@ -146,12 +149,13 @@
     for step in range(SWEEPS):
         pressure = pressure + OMEGA * (src - k_apply(pressure, parts0)) / parts0[1]
     resid0 = src - k_apply(pressure, parts0)
-    p_out[...] = inner(pressure, h0)
+    r0_scr[...] = pressure
+    p_out[...] = r0_scr[pl.ds(h0, nx), pl.ds(hy, ny), :]
     k0_scr[...] = perm0
     r0_scr[...] = resid0
     cx, cy = r0_scr.shape[0] // 2, r0_scr.shape[1] // 2
-    rhs_mid = k_restrict(r0_scr, 0, cx, cy)
-    perm_mid = k_restrict(k0_scr, 0, cx, cy)
+    rhs_mid = k_restrict(r0_scr, 0, 0, cx, cy)
+    perm_mid = k_restrict(k0_scr, 0, 0, cx, cy)
     parts1 = k_coefficients(perm_mid, 0.25)
     value = OMEGA * rhs_mid / parts1[1]
     for step in range(SWEEPS - 1):
@@ -160,10 +164,11 @@
     k1_scr[...] = perm_mid
     mx, my = mid_out.shape[0], mid_out.shape[1]
     r1_scr[...] = value
-    mid_out[...] = r1_scr[pl.ds(h1, mx), pl.ds(h1, my), :]
+    mid_out[...] = r1_scr[pl.ds(h1, mx), pl.ds(h1y, my), :]
     r1_scr[...] = resid1
-    rhs2_out[...] = k_restrict(r1_scr, h1, mx // 2, my // 2)
-    perm2_out[...] = k_restrict(k1_scr, h1, mx // 2, my // 2)
+    qx, qy = rhs2_out.shape[0], rhs2_out.shape[1]
+    rhs2_out[...] = k_restrict(r1_scr, h1, h1y - 2 * h2, qx, qy)
+    perm2_out[...] = k_restrict(k1_scr, h1, h1y - 2 * h2, qx, qy)
 
 
 def coarse_kernel(region, out, scr):
@@ -192,19 +197,21 @@
 def body(pressure_init, source, permeability):
     h0, h2 = FINE_HALO, COARSE_HALO
     nx, ny, nz = pressure_init.shape
+    hy = FINE_Y_HALO
     tiles = [permeability, pressure_init, source]
-    pieces = exchange_pieces(tiles, h0)
-    px, py = nx + 2 * h0, ny + 2 * h0
+    pieces = exchange_pieces(tiles, h0, hy)
+    px, py = nx + 2 * h0, ny + 2 * hy
     mid = (nx // 2, ny // 2, nz)
     coarse = (nx // 4, ny // 4, nz)
+    coarse_y = (nx // 4, ny // 4 + 2 * h2, nz)
     pressure_out, correction_mid, rhs_coarse, perm_coarse = vmem_call(
         fine_kernel,
-        [(nx, ny, nz), mid, coarse, coarse],
+        [(nx, ny, nz), mid, coarse_y, coarse_y],
         [(3, px, py, nz), (px, py, nz), (px, py, nz), (px // 2, py // 2, nz), (px // 2, py // 2, nz)],
         *tiles,
         *pieces,
     )
-    region2 = exchange([perm_coarse, rhs_coarse], h2)
+    region2 = exchange_x([perm_coarse, rhs_coarse], h2)
     c2x, c2y = coarse[0] + 2 * h2, coarse[1] + 2 * h2
     (correction_coarse,) = vmem_call(coarse_kernel, [coarse], [(c2x, c2y, nz)], region2)
     return (pressure_out, correction_mid, correction_coarse)

time: 62.9 us -> 64 us (1.017)
  the two profiles are of different devices: /device:TPU:288 before, /device:TPU:800 now
where the time goes in v6:
time: 64 us; the launch traced here: 63.7 us
  waiting for transfers between devices  31.1 us (49%)
  starting transfers between devices  21.6 us (34%)
  Pallas kernels  7.18 us (11%)
  local copies, waits for them, and re-layouts  2.77 us (4%)
  between operations  0.83 us (1%)
    ppermute x6, waiting for transfers between devices, shift_in(): return lax.ppermute(edge, axis, pairs)  31.1 us
    ppermute x6, starting transfers between devices, shift_in(): return lax.ppermute(edge, axis, pairs)  21.6 us
    pallas_call x2, Pallas kernels, vmem_call(): pl.pallas_call(kernel, out_shape=[jax.ShapeDtypeStruct(s, jnp.float32) fo...  7.18 us
  transfers between devices with their start and end apart: 6, of which 5 were waited for; matrix products, arithmetic and copies ran while one was open for 1% of the time, Pallas kernels for 0%

profile of v6, /device:TPU:800, one launch (start us, length us, event | category | flops | bytes accessed | tf_op | source)
XLA Modules:
  0.0 63.7 jit_solution(9006675163003707786)
XLA Ops:
  0.6 0.0 copy-start.2
  0.6 1.1 %fusion.3 = (f32[16,20,128]{2,1,0:T(8,128)S(1)}, f32[16,20,128]{2,1,0:T(8,128)S(1)}) fusion(f32[16,32,128]{2,1,0:T(8,128)} %p_in.1), kind=kLoop, calls=%fused_computation.21 | loop fusion | bytes 655360 | tf_op jit(solution)/shard_map/slice | solution.py:79
  1.7 0.0 copy-done.2
  1.8 0.0 copy-start
  1.8 0.9 %copy-done = f32[16,32,128]{2,1,0:T(8,128)S(1)} copy-done((f32[16,32,128]{2,1,0:T(8,128)S(1)}, f32[16,32,128]{2,1,0:T(8,128)}, u32[]{:S(2)}) %copy-start) | copy-done | bytes 262168
  2.8 0.1 copy_bitcast_fusion
  2.9 5.9 %collective-permute-start.1 = (f32[3,16,20,128]{3,1,2,0:T(8,128)S(1)}, f32[3,16,20,128]{3,1,2,0:T(8,128)S(1)}, u32[]{:S(2)}, u32[]{:S(2)}) collective-permute-start(f32[3,16,20,128]{3,1,2,0:T(8,128)S(1)} %pad_maximum_fusion.3), channel_id=1, source_target_pairs={{1,0},{2,1},{3,2},{4,3},{5,4},{6,5},{7,6},{8,7},{9,8},{10,9},{11,1... | collective-permute-start | bytes 1474568 | tf_op jit(solution)/shard_map/ppermute | solution.py:71
  8.8 0.1 copy_bitcast_fusion.3
  8.9 0.0 copy-start.1
  9.0 2.1 %collective-permute-start = (f32[3,16,20,128]{3,1,2,0:T(8,128)S(1)}, f32[3,16,20,128]{3,1,2,0:T(8,128)S(1)}, u32[]{:S(2)}, u32[]{:S(2)}) collective-permute-start(f32[3,16,20,128]{3,1,2,0:T(8,128)S(1)} %pad_maximum_fusion.2), channel_id=1, source_target_pairs={{0,1},{1,2},{2,3},{3,4},{4,5},{5,6},{6,7},{7,8},{8,9},{9,10},{10,1... | collective-permute-start | bytes 1474568 | tf_op jit(solution)/shard_map/ppermute | solution.py:71
  11.0 0.0 copy-done.1
  11.1 8.1 %collective-permute-done.1 = f32[3,16,20,128]{3,1,2,0:T(8,128)S(1)} collective-permute-done((f32[3,16,20,128]{3,1,2,0:T(8,128)S(1)}, f32[3,16,20,128]{3,1,2,0:T(8,128)S(1)}, u32[]{:S(2)}, u32[]{:S(2)}) %collective-permute-start.1) | collective-permute-done | bytes 491552 | tf_op jit(solution)/shard_map/ppermute | solution.py:71
  19.2 0.2 copy.17.hi_y
  19.5 7.5 %collective-permute-done = f32[3,16,20,128]{3,1,2,0:T(8,128)S(1)} collective-permute-done((f32[3,16,20,128]{3,1,2,0:T(8,128)S(1)}, f32[3,16,20,128]{3,1,2,0:T(8,128)S(1)}, u32[]{:S(2)}, u32[]{:S(2)}) %collective-permute-start) | collective-permute-done | bytes 491552 | tf_op jit(solution)/shard_map/ppermute | solution.py:71
  27.0 0.2 copy.16.lo_y
  27.2 0.1 pad_maximum_fusion
  27.3 1.9 %collective-permute-start.2 = (f32[3,8,72,128]{3,2,1,0:T(8,128)S(1)}, f32[3,8,72,128]{3,2,1,0:T(8,128)S(1)}, u32[]{:S(2)}, u32[]{:S(2)}) collective-permute-start(f32[3,8,72,128]{3,2,1,0:T(8,128)S(1)} %pad_maximum_fusion), channel_id=1, source_target_pairs={{0,64},{64,128},{128,192},{192,256},{256,320},{320,384},{384,448},... | collective-permute-start | bytes 2654216 | tf_op jit(solution)/shard_map/ppermute | solution.py:71
  29.2 0.1 pad_maximum_fusion.1
  29.3 4.9 %collective-permute-start.3 = (f32[3,8,72,128]{3,2,1,0:T(8,128)S(1)}, f32[3,8,72,128]{3,2,1,0:T(8,128)S(1)}, u32[]{:S(2)}, u32[]{:S(2)}) collective-permute-start(f32[3,8,72,128]{3,2,1,0:T(8,128)S(1)} %pad_maximum_fusion.1), channel_id=1, source_target_pairs={{64,0},{128,64},{192,128},{256,192},{320,256},{384,320},{448,384},... | collective-permute-start | bytes 2654216 | tf_op jit(solution)/shard_map/ppermute | solution.py:71
  34.2 8.7 %collective-permute-done.2.lo_x = f32[3,8,72,128]{3,2,1,0:T(8,128)S(1)} collective-permute-done((f32[3,8,72,128]{3,2,1,0:T(8,128)S(1)}, f32[3,8,72,128]{3,2,1,0:T(8,128)S(1)}, u32[]{:S(2)}, u32[]{:S(2)}) %collective-permute-start.2) | collective-permute-done | bytes 884768 | tf_op jit(solution)/shard_map/ppermute | solution.py:71
  42.9 1.8 %collective-permute-done.3.hi_x = f32[3,8,72,128]{3,2,1,0:T(8,128)S(1)} collective-permute-done((f32[3,8,72,128]{3,2,1,0:T(8,128)S(1)}, f32[3,8,72,128]{3,2,1,0:T(8,128)S(1)}, u32[]{:S(2)}, u32[]{:S(2)}) %collective-permute-start.3) | collective-permute-done | bytes 884768 | tf_op jit(solution)/shard_map/ppermute | solution.py:71
  44.7 6.0 %shard_map.58 = (f32[16,32,128]{2,1,0:T(8,128)}, f32[8,16,128]{2,1,0:T(8,128)}, f32[4,16,128]{2,1,0:T(8,128)S(1)}, f32[4,16,128]{2,1,0:T(8,128)S(1)}) custom-call(f32[16,32,128]{2,1,0:T(8,128)S(1)} %copy-done, f32[16,32,128]{2,1,0:T(8,128)S(1)} %copy-done.1, f32[16,32,128]{2,1,0:T(8,128)S(1)} %copy-done.2, f32[3,16,20,128]{3,2,1,0:T(8,128)S(1)} %copy.16.lo_y, ...), custom_call_target="tpu_custom_call" | custom-call | tf_op jit(solution)/shard_map/pallas_call | solution.py:187
  50.7 5.0 %collective-permute-start.5 = (f32[2,4,16,128]{3,2,1,0:T(8,128)S(1)}, f32[2,4,16,128]{3,2,1,0:T(8,128)S(1)}, u32[]{:S(2)}, u32[]{:S(2)}) collective-permute-start(f32[2,4,16,128]{3,2,1,0:T(8,128)S(1)} %pad_maximum_fusion.5), channel_id=1, source_target_pairs={{64,0},{128,64},{192,128},{256,192},{320,256},{384,320},{448,384},... | collective-permute-start | bytes 196616 | tf_op jit(solution)/shard_map/ppermute | solution.py:71
  55.7 1.9 %collective-permute-start.4 = (f32[2,4,16,128]{3,2,1,0:T(8,128)S(1)}, f32[2,4,16,128]{3,2,1,0:T(8,128)S(1)}, u32[]{:S(2)}, u32[]{:S(2)}) collective-permute-start(f32[2,4,16,128]{3,2,1,0:T(8,128)S(1)} %pad_maximum_fusion.5), channel_id=1, source_target_pairs={{0,64},{64,128},{128,192},{192,256},{256,320},{320,384},{384,448},... | collective-permute-start | bytes 196616 | tf_op jit(solution)/shard_map/ppermute | solution.py:71
  57.6 0.0 collective-permute-done.5
  57.6 4.9 %collective-permute-done.4 = f32[2,4,16,128]{3,2,1,0:T(8,128)S(1)} collective-permute-done((f32[2,4,16,128]{3,2,1,0:T(8,128)S(1)}, f32[2,4,16,128]{3,2,1,0:T(8,128)S(1)}, u32[]{:S(2)}, u32[]{:S(2)}) %collective-permute-start.4) | collective-permute-done | bytes 65568 | tf_op jit(solution)/shard_map/ppermute | solution.py:71
  62.5 1.2 %shard_map.59 = f32[4,8,128]{2,1,0:T(8,128)} custom-call(f32[2,12,16,128]{3,2,1,0:T(8,128)S(1)} %pad_maximum_fusion.4.region), custom_call_target="tpu_custom_call" | custom-call | tf_op jit(solution)/shard_map/pallas_call | solution.py:187
  (12 shorter events, 0.3 us)
Async XLA Ops:
  0.6 1.1 %copy-start.2 = (f32[16,32,128]{2,1,0:T(8,128)S(1)}, f32[16,32,128]{2,1,0:T(8,128)}, u32[]{:S(2)}) copy-start(f32[16,32,128]{2,1,0:T(8,128)} %s_in.1) | copy-start | bytes 786436
  1.8 0.9 %copy-start = (f32[16,32,128]{2,1,0:T(8,128)S(1)}, f32[16,32,128]{2,1,0:T(8,128)}, u32[]{:S(2)}) copy-start(f32[16,32,128]{2,1,0:T(8,128)} %perm_in.1) | copy-start | bytes 786436
  2.9 16.3 %collective-permute-start.1 = (f32[3,16,20,128]{3,1,2,0:T(8,128)S(1)}, f32[3,16,20,128]{3,1,2,0:T(8,128)S(1)}, u32[]{:S(2)}, u32[]{:S(2)}) collective-permute-start(f32[3,16,20,128]{3,1,2,0:T(8,128)S(1)} %pad_maximum_fusion.3), channel_id=1, source_target_pairs={{1,0},{2,1},{3,2},{4,3},{5,4},{6,5},{7,6},{8,7},{9,8},{10,9},{11,1... | collective-permute-start | bytes 1474568 | tf_op jit(solution)/shard_map/ppermute | solution.py:71
  8.9 2.1 %copy-start.1 = (f32[16,32,128]{2,1,0:T(8,128)S(1)}, f32[16,32,128]{2,1,0:T(8,128)}, u32[]{:S(2)}) copy-start(f32[16,32,128]{2,1,0:T(8,128)} %p_in.1) | copy-start | bytes 786436
  9.0 18.0 %collective-permute-start = (f32[3,16,20,128]{3,1,2,0:T(8,128)S(1)}, f32[3,16,20,128]{3,1,2,0:T(8,128)S(1)}, u32[]{:S(2)}, u32[]{:S(2)}) collective-permute-start(f32[3,16,20,128]{3,1,2,0:T(8,128)S(1)} %pad_maximum_fusion.2), channel_id=1, source_target_pairs={{0,1},{1,2},{2,3},{3,4},{4,5},{5,6},{6,7},{7,8},{8,9},{9,10},{10,1... | collective-permute-start | bytes 1474568 | tf_op jit(solution)/shard_map/ppermute | solution.py:71
  27.3 15.6 %collective-permute-start.2 = (f32[3,8,72,128]{3,2,1,0:T(8,128)S(1)}, f32[3,8,72,128]{3,2,1,0:T(8,128)S(1)}, u32[]{:S(2)}, u32[]{:S(2)}) collective-permute-start(f32[3,8,72,128]{3,2,1,0:T(8,128)S(1)} %pad_maximum_fusion), channel_id=1, source_target_pairs={{0,64},{64,128},{128,192},{192,256},{256,320},{320,384},{384,448},... | collective-permute-start | bytes 2654216 | tf_op jit(solution)/shard_map/ppermute | solution.py:71
  29.3 15.4 %collective-permute-start.3 = (f32[3,8,72,128]{3,2,1,0:T(8,128)S(1)}, f32[3,8,72,128]{3,2,1,0:T(8,128)S(1)}, u32[]{:S(2)}, u32[]{:S(2)}) collective-permute-start(f32[3,8,72,128]{3,2,1,0:T(8,128)S(1)} %pad_maximum_fusion.1), channel_id=1, source_target_pairs={{64,0},{128,64},{192,128},{256,192},{320,256},{384,320},{448,384},... | collective-permute-start | bytes 2654216 | tf_op jit(solution)/shard_map/ppermute | solution.py:71
  50.7 7.0 %collective-permute-start.5 = (f32[2,4,16,128]{3,2,1,0:T(8,128)S(1)}, f32[2,4,16,128]{3,2,1,0:T(8,128)S(1)}, u32[]{:S(2)}, u32[]{:S(2)}) collective-permute-start(f32[2,4,16,128]{3,2,1,0:T(8,128)S(1)} %pad_maximum_fusion.5), channel_id=1, source_target_pairs={{64,0},{128,64},{192,128},{256,192},{320,256},{384,320},{448,384},... | collective-permute-start | bytes 196616 | tf_op jit(solution)/shard_map/ppermute | solution.py:71
  55.7 6.8 %collective-permute-start.4 = (f32[2,4,16,128]{3,2,1,0:T(8,128)S(1)}, f32[2,4,16,128]{3,2,1,0:T(8,128)S(1)}, u32[]{:S(2)}, u32[]{:S(2)}) collective-permute-start(f32[2,4,16,128]{3,2,1,0:T(8,128)S(1)} %pad_maximum_fusion.5), channel_id=1, source_target_pairs={{0,64},{64,128},{128,192},{192,256},{256,320},{320,384},{384,448},... | collective-permute-start | bytes 196616 | tf_op jit(solution)/shard_map/ppermute | solution.py:71

commit v7 on v4

--- a/solution.py
+++ b/solution.py
@@ -11,7 +11,8 @@
 STORE = 0.1
 OMEGA = 0.8
 
-FINE_HALO = 8
+FINE_HALO = 7
+FINE_Y_HALO = 8
 COARSE_HALO = 4
 
 
@@ -57,8 +58,9 @@
     return 0.25 * jnp.sum(field.reshape(sx // 2, 2, sy // 2, 2, sz), axis=(1, 3))
 
 
-def exchange(x, h):
-    for axis, dim in (("gy", x.ndim - 2), ("gx", x.ndim - 3)):
+def exchange(x, h, hy=None):
+    hy = h if hy is None else hy
+    for axis, dim, h in (("gx", x.ndim - 3, h), ("gy", x.ndim - 2, hy)):
         count, length = lax.axis_size(axis), x.shape[dim]
         up = [(i, i + 1) for i in range(count - 1)]
         down = [(i + 1, i) for i in range(count - 1)]
@@ -68,8 +70,9 @@
     return x
 
 
-def inner(a, h):
-    return a[h:a.shape[0] - h, h:a.shape[1] - h]
+def inner(a, h, hy=None):
+    hy = h if hy is None else hy
+    return a[h:a.shape[0] - h, hy:a.shape[1] - hy]
 
 
 def k_shift(a, axis, step):
@@ -106,15 +109,16 @@
     return out
 
 
-def k_restrict(ref, lo, nx, ny):
+def k_restrict(ref, lox, loy, nx, ny):
     def at(dx, dy):
-        return ref[pl.ds(lo + dx, nx, stride=2), pl.ds(lo + dy, ny, stride=2), :]
+        return ref[pl.ds(lox + dx, nx, stride=2), pl.ds(loy + dy, ny, stride=2), :]
     return 0.25 * ((at(0, 0) + at(1, 0)) + (at(0, 1) + at(1, 1)))
 
 
 def fine_kernel(region, p_out, mid_out, rhs2_out, perm2_out, k0_scr, r0_scr, k1_scr, r1_scr):
-    h0 = FINE_HALO
-    h1 = h0 // 2
+    h0, hy = FINE_HALO, FINE_Y_HALO
+    h1, h1y = h0 // 2, hy // 2
+    ox = h0 % 2
     perm0 = region[0]
     pressure = region[1]
     src = region[2]
@@ -122,12 +126,12 @@
     for step in range(SWEEPS):
         pressure = pressure + OMEGA * (src - k_apply(pressure, parts0)) / parts0[1]
     resid0 = src - k_apply(pressure, parts0)
-    p_out[...] = inner(pressure, h0)
+    p_out[...] = inner(pressure, h0, hy)
     k0_scr[...] = perm0
     r0_scr[...] = resid0
-    cx, cy = r0_scr.shape[0] // 2, r0_scr.shape[1] // 2
-    rhs_mid = k_restrict(r0_scr, 0, cx, cy)
-    perm_mid = k_restrict(k0_scr, 0, cx, cy)
+    cx, cy = k1_scr.shape[0], k1_scr.shape[1]
+    rhs_mid = k_restrict(r0_scr, ox, 0, cx, cy)
+    perm_mid = k_restrict(k0_scr, ox, 0, cx, cy)
     parts1 = k_coefficients(perm_mid, 0.25)
     value = OMEGA * rhs_mid / parts1[1]
     for step in range(SWEEPS - 1):
@@ -136,10 +140,10 @@
     k1_scr[...] = perm_mid
     mx, my = mid_out.shape[0], mid_out.shape[1]
     r1_scr[...] = value
-    mid_out[...] = r1_scr[pl.ds(h1, mx), pl.ds(h1, my), :]
+    mid_out[...] = r1_scr[pl.ds(h1, mx), pl.ds(h1y, my), :]
     r1_scr[...] = resid1
-    rhs2_out[...] = k_restrict(r1_scr, h1, mx // 2, my // 2)
-    perm2_out[...] = k_restrict(k1_scr, h1, mx // 2, my // 2)
+    rhs2_out[...] = k_restrict(r1_scr, h1, h1y, mx // 2, my // 2)
+    perm2_out[...] = k_restrict(k1_scr, h1, h1y, mx // 2, my // 2)
 
 
 def coarse_kernel(region, out, scr):
@@ -168,14 +172,16 @@
 def body(pressure_init, source, permeability):
     h0, h2 = FINE_HALO, COARSE_HALO
     nx, ny, nz = pressure_init.shape
-    region = exchange(jnp.stack([permeability, pressure_init, source]), h0)
-    px, py = nx + 2 * h0, ny + 2 * h0
+    hy = FINE_Y_HALO
+    region = exchange(jnp.stack([permeability, pressure_init, source]), h0, hy)
+    px, py = nx + 2 * h0, ny + 2 * hy
+    qx = (px - h0 % 2) // 2
     mid = (nx // 2, ny // 2, nz)
     coarse = (nx // 4, ny // 4, nz)
     pressure_out, correction_mid, rhs_coarse, perm_coarse = vmem_call(
         fine_kernel,
         [(nx, ny, nz), mid, coarse, coarse],
-        [(px, py, nz), (px, py, nz), (px // 2, py // 2, nz), (px // 2, py // 2, nz)],
+        [(px, py, nz), (px, py, nz), (qx, py // 2, nz), (qx, py // 2, nz)],
         region,
     )
     region2 = exchange(jnp.stack([perm_coarse, rhs_coarse]), h2)

time: 61.6 us -> 60.5 us (0.982)
  starting transfers between devices: 25.9 us -> 24.3 us
    ppermute x4, starting transfers between devices: 14.7 us -> 12.8 us  [exchange(): after = lax.ppermute(lax.slice_in_dim(x, 0, h, axis=dim), axis, down)]
    slice x1 -> x2, other arithmetic: 1.03 us -> 2.35 us  [exchange(): lax.slice_in_dim(x, length - h, length, axis=dim)]
    concatenate x4 -> x3, other arithmetic: 1.41 us -> 0.21 us  [exchange(): x = jnp.concatenate([before, x, after], axis=dim)]
  transfers between devices with their start and end apart: 8 -> 8, of which waited for: 6 -> 7; matrix products, arithmetic and copies ran while one was open for 0% -> 0% of each run, Pallas kernels for 0% -> 0%
where the time goes in v7:
time: 60.5 us; the launch traced here: 60.1 us
  waiting for transfers between devices  27.5 us (45%)
  starting transfers between devices  24.3 us (40%)
  Pallas kernels  4.94 us (8%)
  other arithmetic  2.56 us (4%)
  between operations  0.77 us (1%)
    ppermute x4, waiting for transfers between devices, exchange(): after = lax.ppermute(lax.slice_in_dim(x, 0, h, axis=dim), axis, down)  14.4 us
    ppermute x4, waiting for transfers between devices, exchange(): lax.ppermute(lax.slice_in_dim(x, length - h, length, axis=dim), axis, up)  13.1 us
    ppermute x4, starting transfers between devices, exchange(): after = lax.ppermute(lax.slice_in_dim(x, 0, h, axis=dim), axis, down)  12.8 us
    ppermute x4, starting transfers between devices, exchange(): lax.ppermute(lax.slice_in_dim(x, length - h, length, axis=dim), axis, up)  11.5 us
    pallas_call x2, Pallas kernels, vmem_call(): pl.pallas_call(kernel, out_shape=[jax.ShapeDtypeStruct(s, jnp.float32) fo...  4.94 us
    slice x2, other arithmetic, exchange(): lax.slice_in_dim(x, length - h, length, axis=dim)  2.35 us
  transfers between devices with their start and end apart: 8, of which 7 were waited for; matrix products, arithmetic and copies ran while one was open for 0% of the time, Pallas kernels for 0%

profile of v7, /device:TPU:486, one launch (start us, length us, event | category | flops | bytes accessed | tf_op | source)
XLA Modules:
  0.0 60.1 jit_solution(10409595533891345777)
XLA Ops:
  0.6 0.0 copy-start.2
  0.6 0.0 copy-start
  0.7 0.0 copy-start.1
  0.7 1.3 %pad_maximum_fusion.8 = (f32[3,7,32,128]{3,2,1,0:T(8,128)S(1)}, f32[3,7,32,128]{3,2,1,0:T(8,128)S(1)}) fusion(f32[1,16,32,128]{3,2,1,0:T(8,128)} %bitcast.11, f32[1,16,32,128]{3,2,1,0:T(8,128)} %bitcast.14, f32[1,16,32,128]{3,2,1,0:T(8,128)} %bitcast.17), kind=kLoop, calls=%fused_computation.8 | loop fusion | flops 344064 | bytes 1474560 | tf_op jit(solution)/shard_map/slice | solution.py:67
  2.0 1.9 %collective-permute-start = (f32[3,7,32,128]{3,2,1,0:T(8,128)S(1)}, f32[3,7,32,128]{3,2,1,0:T(8,128)S(1)}, u32[]{:S(2)}, u32[]{:S(2)}) collective-permute-start(f32[3,7,32,128]{3,2,1,0:T(8,128)S(1)} %get-tuple-element.13), channel_id=1, source_target_pairs={{0,64},{64,128},{128,192},{192,256},{256,320},{320,384},{384,448},... | collective-permute-start | bytes 1032200 | tf_op jit(solution)/shard_map/ppermute | solution.py:67
  3.9 4.9 %collective-permute-start.1 = (f32[3,7,32,128]{3,2,1,0:T(8,128)S(1)}, f32[3,7,32,128]{3,2,1,0:T(8,128)S(1)}, u32[]{:S(2)}, u32[]{:S(2)}) collective-permute-start(f32[3,7,32,128]{3,2,1,0:T(8,128)S(1)} %get-tuple-element.14), channel_id=1, source_target_pairs={{64,0},{128,64},{192,128},{256,192},{320,256},{384,320},{448,384},... | collective-permute-start | bytes 1032200 | tf_op jit(solution)/shard_map/ppermute | solution.py:68
  8.8 3.0 %collective-permute-done = f32[3,7,32,128]{3,2,1,0:T(8,128)S(1)} collective-permute-done((f32[3,7,32,128]{3,2,1,0:T(8,128)S(1)}, f32[3,7,32,128]{3,2,1,0:T(8,128)S(1)}, u32[]{:S(2)}, u32[]{:S(2)}) %collective-permute-start) | collective-permute-done | bytes 344096 | tf_op jit(solution)/shard_map/ppermute | solution.py:67
  11.7 1.8 %collective-permute-done.1 = f32[3,7,32,128]{3,2,1,0:T(8,128)S(1)} collective-permute-done((f32[3,7,32,128]{3,2,1,0:T(8,128)S(1)}, f32[3,7,32,128]{3,2,1,0:T(8,128)S(1)}, u32[]{:S(2)}, u32[]{:S(2)}) %collective-permute-start.1) | collective-permute-done | bytes 344096 | tf_op jit(solution)/shard_map/ppermute | solution.py:68
  13.5 1.1 %pad_maximum_fusion.5 = (f32[3,30,8,128]{3,2,1,0:T(8,128)S(1)}, f32[3,30,8,128]{3,2,1,0:T(8,128)S(1)}) fusion(f32[3,7,32,128]{3,2,1,0:T(8,128)S(1)} %collective-permute-done.1, f32[3,7,32,128]{3,2,1,0:T(8,128)S(1)} %collective-permute-done, f32[1,16,32,128]{3,2,1,0:T(8,128)} %bitcast.12, f32[1,16,32,128]{3,2,1,0:T(8,128)} %bitcast.15, ...), kind=kLoop, calls=%fused_computation.5 | loop fusion | flops 737280 | bytes 2211840 | tf_op jit(solution)/shard_map/slice | solution.py:67
  14.6 5.4 %collective-permute-start.2 = (f32[3,30,8,128]{3,2,1,0:T(8,128)S(1)}, f32[3,30,8,128]{3,2,1,0:T(8,128)S(1)}, u32[]{:S(2)}, u32[]{:S(2)}) collective-permute-start(f32[3,30,8,128]{3,2,1,0:T(8,128)S(1)} %get-tuple-element.11), channel_id=1, source_target_pairs={{0,1},{1,2},{2,3},{3,4},{4,5},{5,6},{6,7},{7,8},{8,9},{9,10},{10,1... | collective-permute-start | bytes 1105928 | tf_op jit(solution)/shard_map/ppermute | solution.py:67
  20.0 1.9 %collective-permute-start.3 = (f32[3,30,8,128]{3,2,1,0:T(8,128)S(1)}, f32[3,30,8,128]{3,2,1,0:T(8,128)S(1)}, u32[]{:S(2)}, u32[]{:S(2)}) collective-permute-start(f32[3,30,8,128]{3,2,1,0:T(8,128)S(1)} %get-tuple-element.12), channel_id=1, source_target_pairs={{1,0},{2,1},{3,2},{4,3},{5,4},{6,5},{7,6},{8,7},{9,8},{10,9},{11,1... | collective-permute-start | bytes 1105928 | tf_op jit(solution)/shard_map/ppermute | solution.py:68
  21.9 5.8 %collective-permute-done.2 = f32[3,30,8,128]{3,2,1,0:T(8,128)S(1)} collective-permute-done((f32[3,30,8,128]{3,2,1,0:T(8,128)S(1)}, f32[3,30,8,128]{3,2,1,0:T(8,128)S(1)}, u32[]{:S(2)}, u32[]{:S(2)}) %collective-permute-start.2) | collective-permute-done | bytes 368672 | tf_op jit(solution)/shard_map/ppermute | solution.py:67
  27.7 7.4 %collective-permute-done.3 = f32[3,30,8,128]{3,2,1,0:T(8,128)S(1)} collective-permute-done((f32[3,30,8,128]{3,2,1,0:T(8,128)S(1)}, f32[3,30,8,128]{3,2,1,0:T(8,128)S(1)}, u32[]{:S(2)}, u32[]{:S(2)}) %collective-permute-start.3) | collective-permute-done | bytes 368672 | tf_op jit(solution)/shard_map/ppermute | solution.py:68
  35.1 0.0 copy-done.2
  35.1 0.0 copy-done
  35.1 0.0 copy-done.1
  35.2 0.2 pad_maximum_fusion.region
  35.3 3.7 %shard_map.58 = (f32[16,32,128]{2,1,0:T(8,128)}, f32[8,16,128]{2,1,0:T(8,128)}, f32[4,8,128]{2,1,0:T(8,128)S(1)}, f32[4,8,128]{2,1,0:T(8,128)S(1)}) custom-call(f32[3,30,48,128]{3,2,1,0:T(8,128)S(1)} %pad_maximum_fusion.region), custom_call_target="tpu_custom_call" | custom-call | tf_op jit(solution)/shard_map/pallas_call | solution.py:162
  39.1 2.1 %collective-permute-start.5 = (f32[2,4,8,128]{3,2,1,0:T(8,128)S(1)}, f32[2,4,8,128]{3,2,1,0:T(8,128)S(1)}, u32[]{:S(2)}, u32[]{:S(2)}) collective-permute-start(f32[2,4,8,128]{3,2,1,0:T(8,128)S(1)} %pad_maximum_fusion.11), channel_id=1, source_target_pairs={{64,0},{128,64},{192,128},{256,192},{320,256},{384,320},{448,384},... | collective-permute-start | bytes 98312 | tf_op jit(solution)/shard_map/ppermute | solution.py:68
  41.1 2.2 %collective-permute-start.4 = (f32[2,4,8,128]{3,2,1,0:T(8,128)S(1)}, f32[2,4,8,128]{3,2,1,0:T(8,128)S(1)}, u32[]{:S(2)}, u32[]{:S(2)}) collective-permute-start(f32[2,4,8,128]{3,2,1,0:T(8,128)S(1)} %pad_maximum_fusion.11), channel_id=1, source_target_pairs={{0,64},{64,128},{128,192},{192,256},{256,320},{320,384},{384,448},... | collective-permute-start | bytes 98312 | tf_op jit(solution)/shard_map/ppermute | solution.py:67
  43.4 0.0 collective-permute-done.5
  43.4 4.2 %collective-permute-done.4 = f32[2,4,8,128]{3,2,1,0:T(8,128)S(1)} collective-permute-done((f32[2,4,8,128]{3,2,1,0:T(8,128)S(1)}, f32[2,4,8,128]{3,2,1,0:T(8,128)S(1)}, u32[]{:S(2)}, u32[]{:S(2)}) %collective-permute-start.4) | collective-permute-done | bytes 32800 | tf_op jit(solution)/shard_map/ppermute | solution.py:67
  47.6 1.9 %collective-permute-start.6 = (f32[2,12,4,128]{3,2,1,0:T(4,128)S(1)}, f32[2,12,4,128]{3,2,1,0:T(4,128)S(1)}, u32[]{:S(2)}, u32[]{:S(2)}) collective-permute-start(f32[2,12,4,128]{3,2,1,0:T(4,128)S(1)} %get-tuple-element.15), channel_id=1, source_target_pairs={{0,1},{1,2},{2,3},{3,4},{4,5},{5,6},{6,7},{7,8},{8,9},{9,10},{10,1... | collective-permute-start | bytes 147464 | tf_op jit(solution)/shard_map/ppermute | solution.py:67
  49.5 3.9 %collective-permute-start.7 = (f32[2,12,4,128]{3,2,1,0:T(4,128)S(1)}, f32[2,12,4,128]{3,2,1,0:T(4,128)S(1)}, u32[]{:S(2)}, u32[]{:S(2)}) collective-permute-start(f32[2,12,4,128]{3,2,1,0:T(4,128)S(1)} %get-tuple-element.16), channel_id=1, source_target_pairs={{1,0},{2,1},{3,2},{4,3},{5,4},{6,5},{7,6},{8,7},{9,8},{10,9},{11,1... | collective-permute-start | bytes 147464 | tf_op jit(solution)/shard_map/ppermute | solution.py:68
  53.5 0.1 collective-permute-done.6
  53.6 5.2 %collective-permute-done.7 = f32[2,12,4,128]{3,2,1,0:T(4,128)S(1)} collective-permute-done((f32[2,12,4,128]{3,2,1,0:T(4,128)S(1)}, f32[2,12,4,128]{3,2,1,0:T(4,128)S(1)}, u32[]{:S(2)}, u32[]{:S(2)}) %collective-permute-start.7) | collective-permute-done | bytes 49184 | tf_op jit(solution)/shard_map/ppermute | solution.py:68
  58.9 1.2 %shard_map.59 = f32[4,8,128]{2,1,0:T(8,128)} custom-call(f32[2,12,16,128]{3,2,1,0:T(8,128)S(1)} %pad_maximum_fusion.9.region), custom_call_target="tpu_custom_call" | custom-call | tf_op jit(solution)/shard_map/pallas_call | solution.py:162
  (4 shorter events, 0.1 us)
Async XLA Ops:
  0.6 34.5 %copy-start.2 = (f32[16,32,128]{2,1,0:T(8,128)S(1)}, f32[16,32,128]{2,1,0:T(8,128)}, u32[]{:S(2)}) copy-start(f32[16,32,128]{2,1,0:T(8,128)} %param.5) | copy-start | bytes 786436
  0.6 34.5 %copy-start = (f32[16,32,128]{2,1,0:T(8,128)S(1)}, f32[16,32,128]{2,1,0:T(8,128)}, u32[]{:S(2)}) copy-start(f32[16,32,128]{2,1,0:T(8,128)} %param.4) | copy-start | bytes 786436
  0.7 34.5 %copy-start.1 = (f32[16,32,128]{2,1,0:T(8,128)S(1)}, f32[16,32,128]{2,1,0:T(8,128)}, u32[]{:S(2)}) copy-start(f32[16,32,128]{2,1,0:T(8,128)} %param.3) | copy-start | bytes 786436
  2.0 9.8 %collective-permute-start = (f32[3,7,32,128]{3,2,1,0:T(8,128)S(1)}, f32[3,7,32,128]{3,2,1,0:T(8,128)S(1)}, u32[]{:S(2)}, u32[]{:S(2)}) collective-permute-start(f32[3,7,32,128]{3,2,1,0:T(8,128)S(1)} %get-tuple-element.13), channel_id=1, source_target_pairs={{0,64},{64,128},{128,192},{192,256},{256,320},{320,384},{384,448},... | collective-permute-start | bytes 1032200 | tf_op jit(solution)/shard_map/ppermute | solution.py:67
  3.9 9.6 %collective-permute-start.1 = (f32[3,7,32,128]{3,2,1,0:T(8,128)S(1)}, f32[3,7,32,128]{3,2,1,0:T(8,128)S(1)}, u32[]{:S(2)}, u32[]{:S(2)}) collective-permute-start(f32[3,7,32,128]{3,2,1,0:T(8,128)S(1)} %get-tuple-element.14), channel_id=1, source_target_pairs={{64,0},{128,64},{192,128},{256,192},{320,256},{384,320},{448,384},... | collective-permute-start | bytes 1032200 | tf_op jit(solution)/shard_map/ppermute | solution.py:68
  14.6 13.1 %collective-permute-start.2 = (f32[3,30,8,128]{3,2,1,0:T(8,128)S(1)}, f32[3,30,8,128]{3,2,1,0:T(8,128)S(1)}, u32[]{:S(2)}, u32[]{:S(2)}) collective-permute-start(f32[3,30,8,128]{3,2,1,0:T(8,128)S(1)} %get-tuple-element.11), channel_id=1, source_target_pairs={{0,1},{1,2},{2,3},{3,4},{4,5},{5,6},{6,7},{7,8},{8,9},{9,10},{10,1... | collective-permute-start | bytes 1105928 | tf_op jit(solution)/shard_map/ppermute | solution.py:67
  20.0 15.2 %collective-permute-start.3 = (f32[3,30,8,128]{3,2,1,0:T(8,128)S(1)}, f32[3,30,8,128]{3,2,1,0:T(8,128)S(1)}, u32[]{:S(2)}, u32[]{:S(2)}) collective-permute-start(f32[3,30,8,128]{3,2,1,0:T(8,128)S(1)} %get-tuple-element.12), channel_id=1, source_target_pairs={{1,0},{2,1},{3,2},{4,3},{5,4},{6,5},{7,6},{8,7},{9,8},{10,9},{11,1... | collective-permute-start | bytes 1105928 | tf_op jit(solution)/shard_map/ppermute | solution.py:68
  39.1 4.3 %collective-permute-start.5 = (f32[2,4,8,128]{3,2,1,0:T(8,128)S(1)}, f32[2,4,8,128]{3,2,1,0:T(8,128)S(1)}, u32[]{:S(2)}, u32[]{:S(2)}) collective-permute-start(f32[2,4,8,128]{3,2,1,0:T(8,128)S(1)} %pad_maximum_fusion.11), channel_id=1, source_target_pairs={{64,0},{128,64},{192,128},{256,192},{320,256},{384,320},{448,384},... | collective-permute-start | bytes 98312 | tf_op jit(solution)/shard_map/ppermute | solution.py:68
  41.1 6.4 %collective-permute-start.4 = (f32[2,4,8,128]{3,2,1,0:T(8,128)S(1)}, f32[2,4,8,128]{3,2,1,0:T(8,128)S(1)}, u32[]{:S(2)}, u32[]{:S(2)}) collective-permute-start(f32[2,4,8,128]{3,2,1,0:T(8,128)S(1)} %pad_maximum_fusion.11), channel_id=1, source_target_pairs={{0,64},{64,128},{128,192},{192,256},{256,320},{320,384},{384,448},... | collective-permute-start | bytes 98312 | tf_op jit(solution)/shard_map/ppermute | solution.py:67
  47.6 6.0 %collective-permute-start.6 = (f32[2,12,4,128]{3,2,1,0:T(4,128)S(1)}, f32[2,12,4,128]{3,2,1,0:T(4,128)S(1)}, u32[]{:S(2)}, u32[]{:S(2)}) collective-permute-start(f32[2,12,4,128]{3,2,1,0:T(4,128)S(1)} %get-tuple-element.15), channel_id=1, source_target_pairs={{0,1},{1,2},{2,3},{3,4},{4,5},{5,6},{6,7},{7,8},{8,9},{9,10},{10,1... | collective-permute-start | bytes 147464 | tf_op jit(solution)/shard_map/ppermute | solution.py:67
  49.5 9.3 %collective-permute-start.7 = (f32[2,12,4,128]{3,2,1,0:T(4,128)S(1)}, f32[2,12,4,128]{3,2,1,0:T(4,128)S(1)}, u32[]{:S(2)}, u32[]{:S(2)}) collective-permute-start(f32[2,12,4,128]{3,2,1,0:T(4,128)S(1)} %get-tuple-element.16), channel_id=1, source_target_pairs={{1,0},{2,1},{3,2},{4,3},{5,4},{6,5},{7,6},{8,7},{9,8},{10,9},{11,1... | collective-permute-start | bytes 147464 | tf_op jit(solution)/shard_map/ppermute | solution.py:68

commit v8 on v7

--- a/solution.py
+++ b/solution.py
@@ -70,6 +70,26 @@
     return x
 
 
+def shift_in(edge, axis, step):
+    count = lax.axis_size(axis)
+    pairs = [(i, i + step) for i in range(count) if 0 <= i + step < count]
+    return lax.ppermute(edge, axis, pairs)
+
+
+def exchange_pieces(tiles, hx, hy):
+    nx, ny = tiles[0].shape[0], tiles[0].shape[1]
+    lo_x = shift_in(jnp.stack([t[nx - hx:] for t in tiles]), "gx", 1)
+    hi_x = shift_in(jnp.stack([t[:hx] for t in tiles]), "gx", -1)
+
+    def cols(lo, hi):
+        body = jnp.stack([t[:, lo:hi] for t in tiles])
+        return jnp.concatenate([lo_x[:, :, lo:hi], body, hi_x[:, :, lo:hi]], axis=1)
+
+    lo_y = shift_in(cols(ny - hy, ny), "gy", 1)
+    hi_y = shift_in(cols(0, hy), "gy", -1)
+    return lo_x, hi_x, lo_y, hi_y
+
+
 def inner(a, h, hy=None):
     hy = h if hy is None else hy
     return a[h:a.shape[0] - h, hy:a.shape[1] - hy]
@@ -115,10 +135,18 @@
     return 0.25 * ((at(0, 0) + at(1, 0)) + (at(0, 1) + at(1, 1)))
 
 
-def fine_kernel(region, p_out, mid_out, rhs2_out, perm2_out, k0_scr, r0_scr, k1_scr, r1_scr):
+def fine_kernel(perm_in, p_in, s_in, lo_x, hi_x, lo_y, hi_y,
+                p_out, mid_out, rhs2_out, perm2_out, region, k0_scr, r0_scr, k1_scr, r1_scr):
     h0, hy = FINE_HALO, FINE_Y_HALO
     h1, h1y = h0 // 2, hy // 2
     ox = h0 % 2
+    nx, ny = perm_in.shape[0], perm_in.shape[1]
+    for k, tile in enumerate((perm_in, p_in, s_in)):
+        region[k, pl.ds(0, h0), pl.ds(hy, ny), :] = lo_x[k]
+        region[k, pl.ds(h0, nx), pl.ds(hy, ny), :] = tile[...]
+        region[k, pl.ds(h0 + nx, h0), pl.ds(hy, ny), :] = hi_x[k]
+        region[k, :, pl.ds(0, hy), :] = lo_y[k]
+        region[k, :, pl.ds(hy + ny, hy), :] = hi_y[k]
     perm0 = region[0]
     pressure = region[1]
     src = region[2]
@@ -173,7 +201,8 @@
     h0, h2 = FINE_HALO, COARSE_HALO
     nx, ny, nz = pressure_init.shape
     hy = FINE_Y_HALO
-    region = exchange(jnp.stack([permeability, pressure_init, source]), h0, hy)
+    tiles = [permeability, pressure_init, source]
+    pieces = exchange_pieces(tiles, h0, hy)
     px, py = nx + 2 * h0, ny + 2 * hy
     qx = (px - h0 % 2) // 2
     mid = (nx // 2, ny // 2, nz)
@@ -181,8 +210,9 @@
     pressure_out, correction_mid, rhs_coarse, perm_coarse = vmem_call(
         fine_kernel,
         [(nx, ny, nz), mid, coarse, coarse],
-        [(px, py, nz), (px, py, nz), (qx, py // 2, nz), (qx, py // 2, nz)],
-        region,
+        [(3, px, py, nz), (px, py, nz), (px, py, nz), (qx, py // 2, nz), (qx, py // 2, nz)],
+        *tiles,
+        *pieces,
     )
     region2 = exchange(jnp.stack([perm_coarse, rhs_coarse]), h2)
     c2x, c2y = coarse[0] + 2 * h2, coarse[1] + 2 * h2

time: 60.5 us -> 60.3 us (level)
  other arithmetic: 2.56 us -> 0.16 us
  local copies, waits for them, and re-layouts: 0.04 us -> 2.12 us
    ppermute x0 -> x4, waiting for transfers between devices: none -> 17.9 us  [shift_in(): return lax.ppermute(edge, axis, pairs)]
    ppermute x0 -> x4, starting transfers between devices: none -> 14.2 us  [shift_in(): return lax.ppermute(edge, axis, pairs)]
    ppermute x4 -> x2, waiting for transfers between devices: 14.4 us -> 5.25 us  [exchange(): after = lax.ppermute(lax.slice_in_dim(x, 0, h, axis=dim), axis, down)]
    ppermute x4 -> x2, waiting for transfers between devices: 13.1 us -> 4.3 us  [exchange(): lax.ppermute(lax.slice_in_dim(x, length - h, length, axis=dim), axis, up)]
    ppermute x4 -> x2, starting transfers between devices: 11.5 us -> 4.17 us  [exchange(): lax.ppermute(lax.slice_in_dim(x, length - h, length, axis=dim), axis, up)]
    ppermute x4 -> x2, starting transfers between devices: 12.8 us -> 5.99 us  [exchange(): after = lax.ppermute(lax.slice_in_dim(x, 0, h, axis=dim), axis, down)]
    slice x2 -> x0, other arithmetic: 2.35 us -> none  [exchange(): lax.slice_in_dim(x, length - h, length, axis=dim)]
    another operation x0 -> x4, local copies, waits for them, and re-layouts: none -> 2.03 us  [the longest x2 2 us: exchange_pieces(): hi_x = shift_in(jnp.stack([t[:hx] for t in tiles]), 'gx', -1)]
where the time goes in v8:
time: 60.3 us; the launch traced here: 59.9 us
  waiting for transfers between devices  27.5 us (46%)
  starting transfers between devices  24.4 us (40%)
  Pallas kernels  4.98 us (8%)
  local copies, waits for them, and re-layouts  2.12 us (4%)
  between operations  0.82 us (1%)
    ppermute x4, waiting for transfers between devices, shift_in(): return lax.ppermute(edge, axis, pairs)  17.9 us
    ppermute x4, starting transfers between devices, shift_in(): return lax.ppermute(edge, axis, pairs)  14.2 us
    ppermute x2, starting transfers between devices, exchange(): after = lax.ppermute(lax.slice_in_dim(x, 0, h, axis=dim), axis, down)  5.99 us
    ppermute x2, waiting for transfers between devices, exchange(): after = lax.ppermute(lax.slice_in_dim(x, 0, h, axis=dim), axis, down)  5.25 us
    pallas_call x2, Pallas kernels, vmem_call(): pl.pallas_call(kernel, out_shape=[jax.ShapeDtypeStruct(s, jnp.float32) fo...  4.98 us
    ppermute x2, waiting for transfers between devices, exchange(): lax.ppermute(lax.slice_in_dim(x, length - h, length, axis=dim), axis, up)  4.3 us
    ppermute x2, starting transfers between devices, exchange(): lax.ppermute(lax.slice_in_dim(x, length - h, length, axis=dim), axis, up)  4.17 us
    another operation x2, local copies, waits for them, and re-layouts, exchange_pieces(): hi_x = shift_in(jnp.stack([t[:hx] for t in tiles]), 'gx', -1)  2 us
  transfers between devices with their start and end apart: 8, of which 7 were waited for; matrix products, arithmetic and copies ran while one was open for 0% of the time, Pallas kernels for 0%

profile of v8, /device:TPU:486, one launch (start us, length us, event | category | flops | bytes accessed | tf_op | source)
XLA Modules:
  0.0 59.9 jit_solution(2755296982680702908)
XLA Ops:
  0.6 0.0 copy-start.1
  0.6 1.0 %slice_bitcast_fusion.2 = (f32[1,7,32,128]{3,2,1,0:T(8,128)S(1)}, f32[1,7,32,128]{3,2,1,0:T(8,128)S(1)}) fusion(f32[16,32,128]{2,1,0:T(8,128)} %perm_in.1), kind=kLoop, calls=%fused_computation.7 | loop fusion | bytes 458752 | tf_op jit(solution)/shard_map/stack | solution.py:82
  1.7 0.0 copy-done.1
  1.7 1.0 %slice_bitcast_fusion = (f32[1,7,32,128]{3,2,1,0:T(8,128)S(1)}, f32[1,7,32,128]{3,2,1,0:T(8,128)S(1)}, f32[1,7,32,128]{3,2,1,0:T(8,128)S(1)}, f32[1,7,32,128]{3,2,1,0:T(8,128)S(1)}) fusion(f32[16,32,128]{2,1,0:T(8,128)} %s_in.1, f32[16,32,128]{2,1,0:T(8,128)S(1)} %copy-done.1), kind=kLoop, calls=%fused_computation.5 | loop fusion | bytes 917504 | tf_op jit(solution)/shard_map/stack | solution.py:82
  2.7 1.9 %collective-permute-start = (f32[3,7,32,128]{3,2,1,0:T(8,128)S(1)}, f32[3,7,32,128]{3,2,1,0:T(8,128)S(1)}, u32[]{:S(2)}, u32[]{:S(2)}) collective-permute-start(f32[3,7,32,128]{3,2,1,0:T(8,128)S(1)} %pad_maximum_fusion.2), channel_id=1, source_target_pairs={{0,64},{64,128},{128,192},{192,256},{256,320},{320,384},{384,448},... | collective-permute-start | bytes 1032200 | tf_op jit(solution)/shard_map/ppermute | solution.py:76
  4.6 0.0 copy-start.2
  4.7 0.0 copy-start
  4.7 5.0 %collective-permute-start.1 = (f32[3,7,32,128]{3,2,1,0:T(8,128)S(1)}, f32[3,7,32,128]{3,2,1,0:T(8,128)S(1)}, u32[]{:S(2)}, u32[]{:S(2)}) collective-permute-start(f32[3,7,32,128]{3,2,1,0:T(8,128)S(1)} %pad_maximum_fusion.3), channel_id=1, source_target_pairs={{64,0},{128,64},{192,128},{256,192},{320,256},{384,320},{448,384},... | collective-permute-start | bytes 1032200 | tf_op jit(solution)/shard_map/ppermute | solution.py:76
  9.7 0.0 copy-done.2
  9.7 0.0 copy-done
  9.8 2.7 %collective-permute-done.lo_x = f32[3,7,32,128]{3,2,1,0:T(8,128)S(1)} collective-permute-done((f32[3,7,32,128]{3,2,1,0:T(8,128)S(1)}, f32[3,7,32,128]{3,2,1,0:T(8,128)S(1)}, u32[]{:S(2)}, u32[]{:S(2)}) %collective-permute-start) | collective-permute-done | bytes 344096 | tf_op jit(solution)/shard_map/ppermute | solution.py:76
  12.5 1.9 %collective-permute-done.1.hi_x = f32[3,7,32,128]{3,2,1,0:T(8,128)S(1)} collective-permute-done((f32[3,7,32,128]{3,2,1,0:T(8,128)S(1)}, f32[3,7,32,128]{3,2,1,0:T(8,128)S(1)}, u32[]{:S(2)}, u32[]{:S(2)}) %collective-permute-start.1) | collective-permute-done | bytes 344096 | tf_op jit(solution)/shard_map/ppermute | solution.py:76
  14.5 5.4 %collective-permute-start.2 = (f32[3,30,8,128]{3,2,1,0:T(8,128)S(1)}, f32[3,30,8,128]{3,2,1,0:T(8,128)S(1)}, u32[]{:S(2)}, u32[]{:S(2)}) collective-permute-start(f32[3,30,8,128]{3,2,1,0:T(8,128)S(1)} %pad_maximum_fusion), channel_id=1, source_target_pairs={{0,1},{1,2},{2,3},{3,4},{4,5},{5,6},{6,7},{7,8},{8,9},{9,10},{10,1... | collective-permute-start | bytes 1105928 | tf_op jit(solution)/shard_map/ppermute | solution.py:76
  19.9 1.9 %collective-permute-start.3 = (f32[3,30,8,128]{3,2,1,0:T(8,128)S(1)}, f32[3,30,8,128]{3,2,1,0:T(8,128)S(1)}, u32[]{:S(2)}, u32[]{:S(2)}) collective-permute-start(f32[3,30,8,128]{3,2,1,0:T(8,128)S(1)} %pad_maximum_fusion.1), channel_id=1, source_target_pairs={{1,0},{2,1},{3,2},{4,3},{5,4},{6,5},{7,6},{8,7},{9,8},{10,9},{11,1... | collective-permute-start | bytes 1105928 | tf_op jit(solution)/shard_map/ppermute | solution.py:76
  21.9 5.8 %collective-permute-done.2.lo_y = f32[3,30,8,128]{3,2,1,0:T(8,128)S(1)} collective-permute-done((f32[3,30,8,128]{3,2,1,0:T(8,128)S(1)}, f32[3,30,8,128]{3,2,1,0:T(8,128)S(1)}, u32[]{:S(2)}, u32[]{:S(2)}) %collective-permute-start.2) | collective-permute-done | bytes 368672 | tf_op jit(solution)/shard_map/ppermute | solution.py:76
  27.6 7.5 %collective-permute-done.3.hi_y = f32[3,30,8,128]{3,2,1,0:T(8,128)S(1)} collective-permute-done((f32[3,30,8,128]{3,2,1,0:T(8,128)S(1)}, f32[3,30,8,128]{3,2,1,0:T(8,128)S(1)}, u32[]{:S(2)}, u32[]{:S(2)}) %collective-permute-start.3) | collective-permute-done | bytes 368672 | tf_op jit(solution)/shard_map/ppermute | solution.py:76
  35.1 3.8 %shard_map.58 = (f32[16,32,128]{2,1,0:T(8,128)}, f32[8,16,128]{2,1,0:T(8,128)}, f32[4,8,128]{2,1,0:T(8,128)S(1)}, f32[4,8,128]{2,1,0:T(8,128)S(1)}) custom-call(f32[16,32,128]{2,1,0:T(8,128)S(1)} %copy-done, f32[16,32,128]{2,1,0:T(8,128)S(1)} %copy-done.1, f32[16,32,128]{2,1,0:T(8,128)S(1)} %copy-done.2, f32[3,7,32,128]{3,2,1,0:T(8,128)S(1)} %collective-permute-done.lo_x, ...), custom_call_target="tpu_custom_call" | custom-call | tf_op jit(solution)/shard_map/pallas_call | solution.py:190
  38.9 2.1 %collective-permute-start.5 = (f32[2,4,8,128]{3,2,1,0:T(8,128)S(1)}, f32[2,4,8,128]{3,2,1,0:T(8,128)S(1)}, u32[]{:S(2)}, u32[]{:S(2)}) collective-permute-start(f32[2,4,8,128]{3,2,1,0:T(8,128)S(1)} %pad_maximum_fusion.6), channel_id=1, source_target_pairs={{64,0},{128,64},{192,128},{256,192},{320,256},{384,320},{448,384},... | collective-permute-start | bytes 98312 | tf_op jit(solution)/shard_map/ppermute | solution.py:68
  41.0 2.2 %collective-permute-start.4 = (f32[2,4,8,128]{3,2,1,0:T(8,128)S(1)}, f32[2,4,8,128]{3,2,1,0:T(8,128)S(1)}, u32[]{:S(2)}, u32[]{:S(2)}) collective-permute-start(f32[2,4,8,128]{3,2,1,0:T(8,128)S(1)} %pad_maximum_fusion.6), channel_id=1, source_target_pairs={{0,64},{64,128},{128,192},{192,256},{256,320},{320,384},{384,448},... | collective-permute-start | bytes 98312 | tf_op jit(solution)/shard_map/ppermute | solution.py:67
  43.2 0.0 collective-permute-done.5
  43.2 4.2 %collective-permute-done.4 = f32[2,4,8,128]{3,2,1,0:T(8,128)S(1)} collective-permute-done((f32[2,4,8,128]{3,2,1,0:T(8,128)S(1)}, f32[2,4,8,128]{3,2,1,0:T(8,128)S(1)}, u32[]{:S(2)}, u32[]{:S(2)}) %collective-permute-start.4) | collective-permute-done | bytes 32800 | tf_op jit(solution)/shard_map/ppermute | solution.py:67
  47.4 1.9 %collective-permute-start.6 = (f32[2,12,4,128]{3,2,1,0:T(4,128)S(1)}, f32[2,12,4,128]{3,2,1,0:T(4,128)S(1)}, u32[]{:S(2)}, u32[]{:S(2)}) collective-permute-start(f32[2,12,4,128]{3,2,1,0:T(4,128)S(1)} %get-tuple-element.27), channel_id=1, source_target_pairs={{0,1},{1,2},{2,3},{3,4},{4,5},{5,6},{6,7},{7,8},{8,9},{9,10},{10,1... | collective-permute-start | bytes 147464 | tf_op jit(solution)/shard_map/ppermute | solution.py:67
  49.4 3.9 %collective-permute-start.7 = (f32[2,12,4,128]{3,2,1,0:T(4,128)S(1)}, f32[2,12,4,128]{3,2,1,0:T(4,128)S(1)}, u32[]{:S(2)}, u32[]{:S(2)}) collective-permute-start(f32[2,12,4,128]{3,2,1,0:T(4,128)S(1)} %get-tuple-element.28), channel_id=1, source_target_pairs={{1,0},{2,1},{3,2},{4,3},{5,4},{6,5},{7,6},{8,7},{9,8},{10,9},{11,1... | collective-permute-start | bytes 147464 | tf_op jit(solution)/shard_map/ppermute | solution.py:68
  53.3 0.1 collective-permute-done.6
  53.4 5.2 %collective-permute-done.7 = f32[2,12,4,128]{3,2,1,0:T(4,128)S(1)} collective-permute-done((f32[2,12,4,128]{3,2,1,0:T(4,128)S(1)}, f32[2,12,4,128]{3,2,1,0:T(4,128)S(1)}, u32[]{:S(2)}, u32[]{:S(2)}) %collective-permute-start.7) | collective-permute-done | bytes 49184 | tf_op jit(solution)/shard_map/ppermute | solution.py:68
  58.7 1.2 %shard_map.59 = f32[4,8,128]{2,1,0:T(8,128)} custom-call(f32[2,12,16,128]{3,2,1,0:T(8,128)S(1)} %pad_maximum_fusion.4.region), custom_call_target="tpu_custom_call" | custom-call | tf_op jit(solution)/shard_map/pallas_call | solution.py:190
  (12 shorter events, 0.2 us)
Async XLA Ops:
  0.6 1.1 %copy-start.1 = (f32[16,32,128]{2,1,0:T(8,128)S(1)}, f32[16,32,128]{2,1,0:T(8,128)}, u32[]{:S(2)}) copy-start(f32[16,32,128]{2,1,0:T(8,128)} %p_in.1) | copy-start | bytes 786436
  2.7 9.8 %collective-permute-start = (f32[3,7,32,128]{3,2,1,0:T(8,128)S(1)}, f32[3,7,32,128]{3,2,1,0:T(8,128)S(1)}, u32[]{:S(2)}, u32[]{:S(2)}) collective-permute-start(f32[3,7,32,128]{3,2,1,0:T(8,128)S(1)} %pad_maximum_fusion.2), channel_id=1, source_target_pairs={{0,64},{64,128},{128,192},{192,256},{256,320},{320,384},{384,448},... | collective-permute-start | bytes 1032200 | tf_op jit(solution)/shard_map/ppermute | solution.py:76
  4.6 5.1 %copy-start.2 = (f32[16,32,128]{2,1,0:T(8,128)S(1)}, f32[16,32,128]{2,1,0:T(8,128)}, u32[]{:S(2)}) copy-start(f32[16,32,128]{2,1,0:T(8,128)} %s_in.1) | copy-start | bytes 786436
  4.7 5.0 %copy-start = (f32[16,32,128]{2,1,0:T(8,128)S(1)}, f32[16,32,128]{2,1,0:T(8,128)}, u32[]{:S(2)}) copy-start(f32[16,32,128]{2,1,0:T(8,128)} %perm_in.1) | copy-start | bytes 786436
  4.7 9.7 %collective-permute-start.1 = (f32[3,7,32,128]{3,2,1,0:T(8,128)S(1)}, f32[3,7,32,128]{3,2,1,0:T(8,128)S(1)}, u32[]{:S(2)}, u32[]{:S(2)}) collective-permute-start(f32[3,7,32,128]{3,2,1,0:T(8,128)S(1)} %pad_maximum_fusion.3), channel_id=1, source_target_pairs={{64,0},{128,64},{192,128},{256,192},{320,256},{384,320},{448,384},... | collective-permute-start | bytes 1032200 | tf_op jit(solution)/shard_map/ppermute | solution.py:76
  14.5 13.1 %collective-permute-start.2 = (f32[3,30,8,128]{3,2,1,0:T(8,128)S(1)}, f32[3,30,8,128]{3,2,1,0:T(8,128)S(1)}, u32[]{:S(2)}, u32[]{:S(2)}) collective-permute-start(f32[3,30,8,128]{3,2,1,0:T(8,128)S(1)} %pad_maximum_fusion), channel_id=1, source_target_pairs={{0,1},{1,2},{2,3},{3,4},{4,5},{5,6},{6,7},{7,8},{8,9},{9,10},{10,1... | collective-permute-start | bytes 1105928 | tf_op jit(solution)/shard_map/ppermute | solution.py:76
  19.9 15.2 %collective-permute-start.3 = (f32[3,30,8,128]{3,2,1,0:T(8,128)S(1)}, f32[3,30,8,128]{3,2,1,0:T(8,128)S(1)}, u32[]{:S(2)}, u32[]{:S(2)}) collective-permute-start(f32[3,30,8,128]{3,2,1,0:T(8,128)S(1)} %pad_maximum_fusion.1), channel_id=1, source_target_pairs={{1,0},{2,1},{3,2},{4,3},{5,4},{6,5},{7,6},{8,7},{9,8},{10,9},{11,1... | collective-permute-start | bytes 1105928 | tf_op jit(solution)/shard_map/ppermute | solution.py:76
  38.9 4.3 %collective-permute-start.5 = (f32[2,4,8,128]{3,2,1,0:T(8,128)S(1)}, f32[2,4,8,128]{3,2,1,0:T(8,128)S(1)}, u32[]{:S(2)}, u32[]{:S(2)}) collective-permute-start(f32[2,4,8,128]{3,2,1,0:T(8,128)S(1)} %pad_maximum_fusion.6), channel_id=1, source_target_pairs={{64,0},{128,64},{192,128},{256,192},{320,256},{384,320},{448,384},... | collective-permute-start | bytes 98312 | tf_op jit(solution)/shard_map/ppermute | solution.py:68
  41.0 6.4 %collective-permute-start.4 = (f32[2,4,8,128]{3,2,1,0:T(8,128)S(1)}, f32[2,4,8,128]{3,2,1,0:T(8,128)S(1)}, u32[]{:S(2)}, u32[]{:S(2)}) collective-permute-start(f32[2,4,8,128]{3,2,1,0:T(8,128)S(1)} %pad_maximum_fusion.6), channel_id=1, source_target_pairs={{0,64},{64,128},{128,192},{192,256},{256,320},{320,384},{384,448},... | collective-permute-start | bytes 98312 | tf_op jit(solution)/shard_map/ppermute | solution.py:67
  47.4 6.0 %collective-permute-start.6 = (f32[2,12,4,128]{3,2,1,0:T(4,128)S(1)}, f32[2,12,4,128]{3,2,1,0:T(4,128)S(1)}, u32[]{:S(2)}, u32[]{:S(2)}) collective-permute-start(f32[2,12,4,128]{3,2,1,0:T(4,128)S(1)} %get-tuple-element.27), channel_id=1, source_target_pairs={{0,1},{1,2},{2,3},{3,4},{4,5},{5,6},{6,7},{7,8},{8,9},{9,10},{10,1... | collective-permute-start | bytes 147464 | tf_op jit(solution)/shard_map/ppermute | solution.py:67
  49.4 9.3 %collective-permute-start.7 = (f32[2,12,4,128]{3,2,1,0:T(4,128)S(1)}, f32[2,12,4,128]{3,2,1,0:T(4,128)S(1)}, u32[]{:S(2)}, u32[]{:S(2)}) collective-permute-start(f32[2,12,4,128]{3,2,1,0:T(4,128)S(1)} %get-tuple-element.28), channel_id=1, source_target_pairs={{1,0},{2,1},{3,2},{4,3},{5,4},{6,5},{7,6},{8,7},{9,8},{10,9},{11,1... | collective-permute-start | bytes 147464 | tf_op jit(solution)/shard_map/ppermute | solution.py:68

commit v9 on v8

--- a/solution.py
+++ b/solution.py
@@ -151,8 +151,9 @@
     pressure = region[1]
     src = region[2]
     parts0 = k_coefficients(perm0, 1.0)
+    scale0 = OMEGA / parts0[1]
     for step in range(SWEEPS):
-        pressure = pressure + OMEGA * (src - k_apply(pressure, parts0)) / parts0[1]
+        pressure = pressure + (src - k_apply(pressure, parts0)) * scale0
     resid0 = src - k_apply(pressure, parts0)
     p_out[...] = inner(pressure, h0, hy)
     k0_scr[...] = perm0
@@ -161,9 +162,10 @@
     rhs_mid = k_restrict(r0_scr, ox, 0, cx, cy)
     perm_mid = k_restrict(k0_scr, ox, 0, cx, cy)
     parts1 = k_coefficients(perm_mid, 0.25)
-    value = OMEGA * rhs_mid / parts1[1]
+    scale1 = OMEGA / parts1[1]
+    value = rhs_mid * scale1
     for step in range(SWEEPS - 1):
-        value = value + OMEGA * (rhs_mid - k_apply(value, parts1)) / parts1[1]
+        value = value + (rhs_mid - k_apply(value, parts1)) * scale1
     resid1 = rhs_mid - k_apply(value, parts1)
     k1_scr[...] = perm_mid
     mx, my = mid_out.shape[0], mid_out.shape[1]
@@ -179,9 +181,10 @@
     perm2 = region[0]
     rhs2 = region[1]
     parts2 = k_coefficients(perm2, 0.0625)
-    value = OMEGA * rhs2 / parts2[1]
+    scale2 = OMEGA / parts2[1]
+    value = rhs2 * scale2
     for step in range(COARSE - 1):
-        value = value + OMEGA * (rhs2 - k_apply(value, parts2)) / parts2[1]
+        value = value + (rhs2 - k_apply(value, parts2)) * scale2
     scr[...] = value
     out[...] = scr[pl.ds(h2, out.shape[0]), pl.ds(h2, out.shape[1]), :]
 

time: 60.3 us -> 60.3 us (level)
  no operation moved by 1% of the time
where the time goes in v9:
time: 60.3 us; the launch traced here: 59.9 us
  waiting for transfers between devices  27.5 us (46%)
  starting transfers between devices  24.4 us (40%)
  Pallas kernels  4.99 us (8%)
  local copies, waits for them, and re-layouts  2.12 us (4%)
  between operations  0.82 us (1%)
    ppermute x4, waiting for transfers between devices, shift_in(): return lax.ppermute(edge, axis, pairs)  17.9 us
    ppermute x4, starting transfers between devices, shift_in(): return lax.ppermute(edge, axis, pairs)  14.2 us
    ppermute x2, starting transfers between devices, exchange(): after = lax.ppermute(lax.slice_in_dim(x, 0, h, axis=dim), axis, down)  5.99 us
    ppermute x2, waiting for transfers between devices, exchange(): after = lax.ppermute(lax.slice_in_dim(x, 0, h, axis=dim), axis, down)  5.25 us
    pallas_call x2, Pallas kernels, vmem_call(): pl.pallas_call(kernel, out_shape=[jax.ShapeDtypeStruct(s, jnp.float32) fo...  4.99 us
    ppermute x2, waiting for transfers between devices, exchange(): lax.ppermute(lax.slice_in_dim(x, length - h, length, axis=dim), axis, up)  4.3 us
    ppermute x2, starting transfers between devices, exchange(): lax.ppermute(lax.slice_in_dim(x, length - h, length, axis=dim), axis, up)  4.17 us
    another operation x2, local copies, waits for them, and re-layouts, exchange_pieces(): hi_x = shift_in(jnp.stack([t[:hx] for t in tiles]), 'gx', -1)  2 us
  transfers between devices with their start and end apart: 8, of which 7 were waited for; matrix products, arithmetic and copies ran while one was open for 0% of the time, Pallas kernels for 0%

profile of v9, /device:TPU:486, one launch (start us, length us, event | category | flops | bytes accessed | tf_op | source)
XLA Modules:
  0.0 59.9 jit_solution(9900548264408346343)
XLA Ops:
  0.6 0.0 copy-start.1
  0.6 1.0 %slice_bitcast_fusion.2 = (f32[1,7,32,128]{3,2,1,0:T(8,128)S(1)}, f32[1,7,32,128]{3,2,1,0:T(8,128)S(1)}) fusion(f32[16,32,128]{2,1,0:T(8,128)} %perm_in.1), kind=kLoop, calls=%fused_computation.7 | loop fusion | bytes 458752 | tf_op jit(solution)/shard_map/stack | solution.py:82
  1.7 0.0 copy-done.1
  1.7 1.0 %slice_bitcast_fusion = (f32[1,7,32,128]{3,2,1,0:T(8,128)S(1)}, f32[1,7,32,128]{3,2,1,0:T(8,128)S(1)}, f32[1,7,32,128]{3,2,1,0:T(8,128)S(1)}, f32[1,7,32,128]{3,2,1,0:T(8,128)S(1)}) fusion(f32[16,32,128]{2,1,0:T(8,128)} %s_in.1, f32[16,32,128]{2,1,0:T(8,128)S(1)} %copy-done.1), kind=kLoop, calls=%fused_computation.5 | loop fusion | bytes 917504 | tf_op jit(solution)/shard_map/stack | solution.py:82
  2.7 1.9 %collective-permute-start = (f32[3,7,32,128]{3,2,1,0:T(8,128)S(1)}, f32[3,7,32,128]{3,2,1,0:T(8,128)S(1)}, u32[]{:S(2)}, u32[]{:S(2)}) collective-permute-start(f32[3,7,32,128]{3,2,1,0:T(8,128)S(1)} %pad_maximum_fusion.2), channel_id=1, source_target_pairs={{0,64},{64,128},{128,192},{192,256},{256,320},{320,384},{384,448},... | collective-permute-start | bytes 1032200 | tf_op jit(solution)/shard_map/ppermute | solution.py:76
  4.6 0.0 copy-start.2
  4.7 0.0 copy-start
  4.7 5.0 %collective-permute-start.1 = (f32[3,7,32,128]{3,2,1,0:T(8,128)S(1)}, f32[3,7,32,128]{3,2,1,0:T(8,128)S(1)}, u32[]{:S(2)}, u32[]{:S(2)}) collective-permute-start(f32[3,7,32,128]{3,2,1,0:T(8,128)S(1)} %pad_maximum_fusion.3), channel_id=1, source_target_pairs={{64,0},{128,64},{192,128},{256,192},{320,256},{384,320},{448,384},... | collective-permute-start | bytes 1032200 | tf_op jit(solution)/shard_map/ppermute | solution.py:76
  9.7 0.0 copy-done.2
  9.7 0.0 copy-done
  9.8 2.7 %collective-permute-done.lo_x = f32[3,7,32,128]{3,2,1,0:T(8,128)S(1)} collective-permute-done((f32[3,7,32,128]{3,2,1,0:T(8,128)S(1)}, f32[3,7,32,128]{3,2,1,0:T(8,128)S(1)}, u32[]{:S(2)}, u32[]{:S(2)}) %collective-permute-start) | collective-permute-done | bytes 344096 | tf_op jit(solution)/shard_map/ppermute | solution.py:76
  12.5 1.9 %collective-permute-done.1.hi_x = f32[3,7,32,128]{3,2,1,0:T(8,128)S(1)} collective-permute-done((f32[3,7,32,128]{3,2,1,0:T(8,128)S(1)}, f32[3,7,32,128]{3,2,1,0:T(8,128)S(1)}, u32[]{:S(2)}, u32[]{:S(2)}) %collective-permute-start.1) | collective-permute-done | bytes 344096 | tf_op jit(solution)/shard_map/ppermute | solution.py:76
  14.5 5.4 %collective-permute-start.2 = (f32[3,30,8,128]{3,2,1,0:T(8,128)S(1)}, f32[3,30,8,128]{3,2,1,0:T(8,128)S(1)}, u32[]{:S(2)}, u32[]{:S(2)}) collective-permute-start(f32[3,30,8,128]{3,2,1,0:T(8,128)S(1)} %pad_maximum_fusion), channel_id=1, source_target_pairs={{0,1},{1,2},{2,3},{3,4},{4,5},{5,6},{6,7},{7,8},{8,9},{9,10},{10,1... | collective-permute-start | bytes 1105928 | tf_op jit(solution)/shard_map/ppermute | solution.py:76
  19.9 1.9 %collective-permute-start.3 = (f32[3,30,8,128]{3,2,1,0:T(8,128)S(1)}, f32[3,30,8,128]{3,2,1,0:T(8,128)S(1)}, u32[]{:S(2)}, u32[]{:S(2)}) collective-permute-start(f32[3,30,8,128]{3,2,1,0:T(8,128)S(1)} %pad_maximum_fusion.1), channel_id=1, source_target_pairs={{1,0},{2,1},{3,2},{4,3},{5,4},{6,5},{7,6},{8,7},{9,8},{10,9},{11,1... | collective-permute-start | bytes 1105928 | tf_op jit(solution)/shard_map/ppermute | solution.py:76
  21.9 5.8 %collective-permute-done.2.lo_y = f32[3,30,8,128]{3,2,1,0:T(8,128)S(1)} collective-permute-done((f32[3,30,8,128]{3,2,1,0:T(8,128)S(1)}, f32[3,30,8,128]{3,2,1,0:T(8,128)S(1)}, u32[]{:S(2)}, u32[]{:S(2)}) %collective-permute-start.2) | collective-permute-done | bytes 368672 | tf_op jit(solution)/shard_map/ppermute | solution.py:76
  27.6 7.5 %collective-permute-done.3.hi_y = f32[3,30,8,128]{3,2,1,0:T(8,128)S(1)} collective-permute-done((f32[3,30,8,128]{3,2,1,0:T(8,128)S(1)}, f32[3,30,8,128]{3,2,1,0:T(8,128)S(1)}, u32[]{:S(2)}, u32[]{:S(2)}) %collective-permute-start.3) | collective-permute-done | bytes 368672 | tf_op jit(solution)/shard_map/ppermute | solution.py:76
  35.1 3.8 %shard_map.58 = (f32[16,32,128]{2,1,0:T(8,128)}, f32[8,16,128]{2,1,0:T(8,128)}, f32[4,8,128]{2,1,0:T(8,128)S(1)}, f32[4,8,128]{2,1,0:T(8,128)S(1)}) custom-call(f32[16,32,128]{2,1,0:T(8,128)S(1)} %copy-done, f32[16,32,128]{2,1,0:T(8,128)S(1)} %copy-done.1, f32[16,32,128]{2,1,0:T(8,128)S(1)} %copy-done.2, f32[3,7,32,128]{3,2,1,0:T(8,128)S(1)} %collective-permute-done.lo_x, ...), custom_call_target="tpu_custom_call" | custom-call | tf_op jit(solution)/shard_map/pallas_call | solution.py:193
  38.9 2.1 %collective-permute-start.5 = (f32[2,4,8,128]{3,2,1,0:T(8,128)S(1)}, f32[2,4,8,128]{3,2,1,0:T(8,128)S(1)}, u32[]{:S(2)}, u32[]{:S(2)}) collective-permute-start(f32[2,4,8,128]{3,2,1,0:T(8,128)S(1)} %pad_maximum_fusion.6), channel_id=1, source_target_pairs={{64,0},{128,64},{192,128},{256,192},{320,256},{384,320},{448,384},... | collective-permute-start | bytes 98312 | tf_op jit(solution)/shard_map/ppermute | solution.py:68
  41.0 2.2 %collective-permute-start.4 = (f32[2,4,8,128]{3,2,1,0:T(8,128)S(1)}, f32[2,4,8,128]{3,2,1,0:T(8,128)S(1)}, u32[]{:S(2)}, u32[]{:S(2)}) collective-permute-start(f32[2,4,8,128]{3,2,1,0:T(8,128)S(1)} %pad_maximum_fusion.6), channel_id=1, source_target_pairs={{0,64},{64,128},{128,192},{192,256},{256,320},{320,384},{384,448},... | collective-permute-start | bytes 98312 | tf_op jit(solution)/shard_map/ppermute | solution.py:67
  43.2 0.0 collective-permute-done.5
  43.2 4.2 %collective-permute-done.4 = f32[2,4,8,128]{3,2,1,0:T(8,128)S(1)} collective-permute-done((f32[2,4,8,128]{3,2,1,0:T(8,128)S(1)}, f32[2,4,8,128]{3,2,1,0:T(8,128)S(1)}, u32[]{:S(2)}, u32[]{:S(2)}) %collective-permute-start.4) | collective-permute-done | bytes 32800 | tf_op jit(solution)/shard_map/ppermute | solution.py:67
  47.4 1.9 %collective-permute-start.6 = (f32[2,12,4,128]{3,2,1,0:T(4,128)S(1)}, f32[2,12,4,128]{3,2,1,0:T(4,128)S(1)}, u32[]{:S(2)}, u32[]{:S(2)}) collective-permute-start(f32[2,12,4,128]{3,2,1,0:T(4,128)S(1)} %get-tuple-element.27), channel_id=1, source_target_pairs={{0,1},{1,2},{2,3},{3,4},{4,5},{5,6},{6,7},{7,8},{8,9},{9,10},{10,1... | collective-permute-start | bytes 147464 | tf_op jit(solution)/shard_map/ppermute | solution.py:67
  49.4 3.9 %collective-permute-start.7 = (f32[2,12,4,128]{3,2,1,0:T(4,128)S(1)}, f32[2,12,4,128]{3,2,1,0:T(4,128)S(1)}, u32[]{:S(2)}, u32[]{:S(2)}) collective-permute-start(f32[2,12,4,128]{3,2,1,0:T(4,128)S(1)} %get-tuple-element.28), channel_id=1, source_target_pairs={{1,0},{2,1},{3,2},{4,3},{5,4},{6,5},{7,6},{8,7},{9,8},{10,9},{11,1... | collective-permute-start | bytes 147464 | tf_op jit(solution)/shard_map/ppermute | solution.py:68
  53.3 0.1 collective-permute-done.6
  53.4 5.2 %collective-permute-done.7 = f32[2,12,4,128]{3,2,1,0:T(4,128)S(1)} collective-permute-done((f32[2,12,4,128]{3,2,1,0:T(4,128)S(1)}, f32[2,12,4,128]{3,2,1,0:T(4,128)S(1)}, u32[]{:S(2)}, u32[]{:S(2)}) %collective-permute-start.7) | collective-permute-done | bytes 49184 | tf_op jit(solution)/shard_map/ppermute | solution.py:68
  58.7 1.2 %shard_map.59 = f32[4,8,128]{2,1,0:T(8,128)} custom-call(f32[2,12,16,128]{3,2,1,0:T(8,128)S(1)} %pad_maximum_fusion.4.region), custom_call_target="tpu_custom_call" | custom-call | tf_op jit(solution)/shard_map/pallas_call | solution.py:193
  (12 shorter events, 0.2 us)
Async XLA Ops:
  0.6 1.1 %copy-start.1 = (f32[16,32,128]{2,1,0:T(8,128)S(1)}, f32[16,32,128]{2,1,0:T(8,128)}, u32[]{:S(2)}) copy-start(f32[16,32,128]{2,1,0:T(8,128)} %p_in.1) | copy-start | bytes 786436
  2.7 9.8 %collective-permute-start = (f32[3,7,32,128]{3,2,1,0:T(8,128)S(1)}, f32[3,7,32,128]{3,2,1,0:T(8,128)S(1)}, u32[]{:S(2)}, u32[]{:S(2)}) collective-permute-start(f32[3,7,32,128]{3,2,1,0:T(8,128)S(1)} %pad_maximum_fusion.2), channel_id=1, source_target_pairs={{0,64},{64,128},{128,192},{192,256},{256,320},{320,384},{384,448},... | collective-permute-start | bytes 1032200 | tf_op jit(solution)/shard_map/ppermute | solution.py:76
  4.6 5.1 %copy-start.2 = (f32[16,32,128]{2,1,0:T(8,128)S(1)}, f32[16,32,128]{2,1,0:T(8,128)}, u32[]{:S(2)}) copy-start(f32[16,32,128]{2,1,0:T(8,128)} %s_in.1) | copy-start | bytes 786436
  4.7 5.0 %copy-start = (f32[16,32,128]{2,1,0:T(8,128)S(1)}, f32[16,32,128]{2,1,0:T(8,128)}, u32[]{:S(2)}) copy-start(f32[16,32,128]{2,1,0:T(8,128)} %perm_in.1) | copy-start | bytes 786436
  4.7 9.7 %collective-permute-start.1 = (f32[3,7,32,128]{3,2,1,0:T(8,128)S(1)}, f32[3,7,32,128]{3,2,1,0:T(8,128)S(1)}, u32[]{:S(2)}, u32[]{:S(2)}) collective-permute-start(f32[3,7,32,128]{3,2,1,0:T(8,128)S(1)} %pad_maximum_fusion.3), channel_id=1, source_target_pairs={{64,0},{128,64},{192,128},{256,192},{320,256},{384,320},{448,384},... | collective-permute-start | bytes 1032200 | tf_op jit(solution)/shard_map/ppermute | solution.py:76
  14.5 13.1 %collective-permute-start.2 = (f32[3,30,8,128]{3,2,1,0:T(8,128)S(1)}, f32[3,30,8,128]{3,2,1,0:T(8,128)S(1)}, u32[]{:S(2)}, u32[]{:S(2)}) collective-permute-start(f32[3,30,8,128]{3,2,1,0:T(8,128)S(1)} %pad_maximum_fusion), channel_id=1, source_target_pairs={{0,1},{1,2},{2,3},{3,4},{4,5},{5,6},{6,7},{7,8},{8,9},{9,10},{10,1... | collective-permute-start | bytes 1105928 | tf_op jit(solution)/shard_map/ppermute | solution.py:76
  19.9 15.2 %collective-permute-start.3 = (f32[3,30,8,128]{3,2,1,0:T(8,128)S(1)}, f32[3,30,8,128]{3,2,1,0:T(8,128)S(1)}, u32[]{:S(2)}, u32[]{:S(2)}) collective-permute-start(f32[3,30,8,128]{3,2,1,0:T(8,128)S(1)} %pad_maximum_fusion.1), channel_id=1, source_target_pairs={{1,0},{2,1},{3,2},{4,3},{5,4},{6,5},{7,6},{8,7},{9,8},{10,9},{11,1... | collective-permute-start | bytes 1105928 | tf_op jit(solution)/shard_map/ppermute | solution.py:76
  38.9 4.3 %collective-permute-start.5 = (f32[2,4,8,128]{3,2,1,0:T(8,128)S(1)}, f32[2,4,8,128]{3,2,1,0:T(8,128)S(1)}, u32[]{:S(2)}, u32[]{:S(2)}) collective-permute-start(f32[2,4,8,128]{3,2,1,0:T(8,128)S(1)} %pad_maximum_fusion.6), channel_id=1, source_target_pairs={{64,0},{128,64},{192,128},{256,192},{320,256},{384,320},{448,384},... | collective-permute-start | bytes 98312 | tf_op jit(solution)/shard_map/ppermute | solution.py:68
  41.0 6.4 %collective-permute-start.4 = (f32[2,4,8,128]{3,2,1,0:T(8,128)S(1)}, f32[2,4,8,128]{3,2,1,0:T(8,128)S(1)}, u32[]{:S(2)}, u32[]{:S(2)}) collective-permute-start(f32[2,4,8,128]{3,2,1,0:T(8,128)S(1)} %pad_maximum_fusion.6), channel_id=1, source_target_pairs={{0,64},{64,128},{128,192},{192,256},{256,320},{320,384},{384,448},... | collective-permute-start | bytes 98312 | tf_op jit(solution)/shard_map/ppermute | solution.py:67
  47.4 6.0 %collective-permute-start.6 = (f32[2,12,4,128]{3,2,1,0:T(4,128)S(1)}, f32[2,12,4,128]{3,2,1,0:T(4,128)S(1)}, u32[]{:S(2)}, u32[]{:S(2)}) collective-permute-start(f32[2,12,4,128]{3,2,1,0:T(4,128)S(1)} %get-tuple-element.27), channel_id=1, source_target_pairs={{0,1},{1,2},{2,3},{3,4},{4,5},{5,6},{6,7},{7,8},{8,9},{9,10},{10,1... | collective-permute-start | bytes 147464 | tf_op jit(solution)/shard_map/ppermute | solution.py:67
  49.4 9.3 %collective-permute-start.7 = (f32[2,12,4,128]{3,2,1,0:T(4,128)S(1)}, f32[2,12,4,128]{3,2,1,0:T(4,128)S(1)}, u32[]{:S(2)}, u32[]{:S(2)}) collective-permute-start(f32[2,12,4,128]{3,2,1,0:T(4,128)S(1)} %get-tuple-element.28), channel_id=1, source_target_pairs={{1,0},{2,1},{3,2},{4,3},{5,4},{6,5},{7,6},{8,7},{9,8},{10,9},{11,1... | collective-permute-start | bytes 147464 | tf_op jit(solution)/shard_map/ppermute | solution.py:68
